TPU v7x, 512 devices: a whole 4x8x8 slice. The times are simulated.
512 devices in a mesh: row: 16 (over y, core), col: 32 (over z, x).
Axes of the slice: x: 4, y: 8, z: 8, core: 2. Of those that a mesh axis runs over, the one named last changes fastest.
Arguments:
- tokens: bfloat16 [1024, 8192], P('col', 'row'), may hold values from -6 to 6
- gate_weight: bfloat16 [8192, 16384], P('row', 'col'), may hold values from -0.09375 to 0.09375
- up_weight: bfloat16 [8192, 16384], P('row', 'col'), may hold values from -0.09375 to 0.09375
- down_weight: bfloat16 [16384, 8192], P('col', 'row'), may hold values from -0.0625 to 0.0625
- gate_mask: int32 [64, 128], P('row', 'col'), may hold values from 0 to 1, as said below
- up_mask: int32 [64, 128], P('row', 'col'), may hold values from 0 to 1, as said below
- down_mask: int32 [128, 64], P('col', 'row'), may hold values from 0 to 1, as said below
Outputs:
- mixed: bfloat16 [1024, 8192], P('col', 'row')
Inputs may be any that keep to these rules, and one draw needn't show every extreme that they name: `gate_mask`: each entry is 0 or 1; the share of ones differs from one block column of hidden units to another. `up_mask`: each entry is 0 or 1; the share of ones differs from one block column of hidden units to another. `down_mask`: each entry is 0 or 1; the share of ones differs from one block row of hidden units to another.
All inputs are finite; a program needn't handle non-finite values.
Results may differ from a plain program's by a relative error of at most 0.0049.
Values may be sent and summed in bfloat16 or wider, within the bound.
No kernel may reach another device: no remote copies, remote signals or barrier semaphores. Data moves between devices by JAX's collectives and lax.ppermute only.
A program may use at most 64 MiB of HBM per device.

v0:
```python
import jax
import jax.numpy as jnp
from jax import lax
from jax.sharding import PartitionSpec as P

BLK = 128


def widen(block_mask):
    rows_blocks, cols_blocks = block_mask.shape
    spread = jnp.broadcast_to(block_mask[:, None, :, None], (rows_blocks, BLK, cols_blocks, BLK))
    return spread.reshape(rows_blocks * BLK, cols_blocks * BLK).astype(jnp.bfloat16)


def swiglu(summed, hidden_cols):
    return (jax.nn.silu(summed[:, :hidden_cols]) * summed[:, hidden_cols:]).astype(jnp.bfloat16)


def on_device(tokens, gate_weight, up_weight, down_weight, gate_mask, up_mask, down_mask):
    hidden_cols = gate_weight.shape[1]
    both_weights = jnp.concatenate(
        [gate_weight * widen(gate_mask), up_weight * widen(up_mask)], axis=1
    )
    down_eff = down_weight * widen(down_mask)
    all_tokens = lax.all_gather(tokens, "col", axis=0, tiled=True)
    summed = lax.psum_scatter(
        jnp.dot(all_tokens, both_weights, preferred_element_type=jnp.float32),
        "row",
        scatter_dimension=0,
        tiled=True,
    )
    hidden_share = swiglu(summed, hidden_cols)
    hidden = lax.all_gather(hidden_share, "row", axis=0, tiled=True)
    out_rows = tokens.shape[0]
    partial_out = jnp.dot(hidden, down_eff, preferred_element_type=jnp.float32)
    whole_out = lax.psum(partial_out, "col")
    first_row = lax.axis_index("col") * out_rows
    mixed = lax.dynamic_slice_in_dim(whole_out, first_row, out_rows, 0)
    return mixed.astype(jnp.bfloat16)


def solution(mesh):
    placed = (
        P("col", "row"),
        P("row", "col"),
        P("row", "col"),
        P("col", "row"),
        P("row", "col"),
        P("row", "col"),
        P("col", "row"),
    )
    return jax.shard_map(
        on_device, mesh=mesh, in_specs=placed, out_specs=P("col", "row"), check_vma=False
    )
```

profile of v0, /device:TPU:8, one launch (start us, length us, event | category | flops | bytes accessed | tf_op | source)
XLA Modules:
  0.0 389.6 jit_solution(954516948314816408)
XLA Ops:
  6.5 0.0 all-gather.3.cloned.1.call-start
  6.5 0.7 all-gather.3.cloned.1.call-update
  7.3 0.0 reduce-scatter.4.cloned.1.call-start
  7.3 0.7 convert_element_type.29
  8.0 0.7 convert_element_type.27
  8.7 0.2 broadcast_in_dim.7
  8.9 0.2 broadcast_in_dim.6
  9.1 1.4 bitcast_multiply_fusion.2
  10.5 87.2 %all-gather.3.cloned.1.call-done = bf16[1024,512]{1,0:T(8,128)(2,1)} async-done(((bf16[32,512]{1,0:T(8,128)(2,1)}), bf16[1024,512]{1,0:T(8,128)(2,1)}) %all-gather.3.cloned.1.call-update) | async-done | bytes 1048592 | tf_op jit(solution)/shard_map/all_gather | solution.py:25
  97.7 4.5 %convolution_bitcast_fusion = f32[1024,1024]{0,1:T(8,128)} fusion(bf16[1024,512]{1,0:T(8,128)(2,1)} %all-gather.3.cloned.1.call-done, bf16[512,512]{1,0:T(8,128)(2,1)S(1)} %get-tuple-element.5, bf16[512,512]{1,0:T(8,128)(2,1)S(1)} %get-tuple-element.6), kind=kOutput, calls=%fused_computation | convolution fusion | flops 1075838976 | bytes 6291456 | tf_op jit(solution)/shard_map/dot_general | solution.py:27
  102.2 5.4 %copy.11 = f32[1024,1024]{1,0:T(8,128)} copy(f32[1024,1024]{0,1:T(8,128)} %convolution_bitcast_fusion) | data formatting | bytes 8388608
  107.5 0.0 copy-start.1
  107.5 0.0 copy-start
  107.5 0.0 reduce-scatter.4.cloned.1.call-update
  107.6 0.0 all-gather.5.cloned.1.call-start
  107.6 59.4 %reduce-scatter.4.cloned.1.call-done = f32[64,1024]{1,0:T(8,128)} async-done(((f32[1024,1024]{1,0:T(8,128)}), f32[64,1024]{1,0:T(8,128)}) %reduce-scatter.4.cloned.1.call-update) | async-done | bytes 262160 | tf_op jit(solution)/shard_map/reduce_scatter | solution.py:26
  167.1 1.6 fusion.5
  168.7 0.0 all-gather.5.cloned.1.call-update
  168.7 0.0 copy-done.1
  168.8 43.1 %all-gather.5.cloned.1.call-done = bf16[1024,512]{1,0:T(8,128)(2,1)} async-done(((bf16[64,512]{1,0:T(8,128)(2,1)}), bf16[1024,512]{1,0:T(8,128)(2,1)}) %all-gather.5.cloned.1.call-update) | async-done | bytes 1048592 | tf_op jit(solution)/shard_map/all_gather | solution.py:33
  211.9 0.2 broadcast_in_dim.8
  212.1 0.0 copy-done
  212.1 1.9 fusion.3
  214.1 168.3 %all-reduce.1 = bf16[1024,512]{1,0:T(8,128)(2,1)S(1)} all-reduce(f32[1024,512]{1,0:T(8,128)S(1)} %fusion.3), channel_id=1, replica_groups=mesh['row'=16,'col'=32] {'col'}, use_global_device_ids=true, to_apply=%region_1.2 | all-reduce | flops 524288 | bytes 3145728 | tf_op jit(solution)/shard_map/psum | solution.py:36
  382.4 0.6 dynamic-slice_convert_fusion
  (1 shorter events, 0.0 us)
Async XLA Ops:
  6.5 91.2 %all-gather.3.cloned.1.call-start = ((), (), s32[]{:S(2)}) async-start(), calls=%async_computation.1 | async-start | bytes 1081344 | tf_op jit(solution)/shard_map/all_gather | solution.py:25
  7.3 159.8 %reduce-scatter.4.cloned.1.call-start = ((), (), s32[]{:S(2)}) async-start(), calls=%async_computation.3 | async-start | bytes 4456448 | tf_op jit(solution)/shard_map/reduce_scatter | solution.py:26
  107.5 61.2 %copy-start.1 = (s32[4,4]{1,0:T(4,128)S(1)}, s32[4,4]{1,0:T(4,128)}, u32[]{:S(2)}) copy-start(s32[4,4]{1,0:T(4,128)} %param.13) | copy-start | bytes 196
  107.5 104.6 %copy-start = (bf16[512,512]{1,0:T(8,128)(2,1)S(1)}, bf16[512,512]{1,0:T(8,128)(2,1)}, u32[]{:S(2)}) copy-start(bf16[512,512]{1,0:T(8,128)(2,1)} %param.10) | copy-start | bytes 1572868
  107.6 104.3 %all-gather.5.cloned.1.call-start = ((), (), s32[]{:S(2)}) async-start(), calls=%async_computation.2 | async-start | bytes 1114112 | tf_op jit(solution)/shard_map/all_gather | solution.py:33
Sparse Core Ops, SparseCore 0:
  10.5 87.1 all-gather.2
  107.7 59.3 reduce-scatter.3
  169.2 42.6 all-gather.4
where the time goes:
time: 390 us
  waiting for transfers between devices  191 us (49%)
  blocking collectives  168 us (43%)
  between operations  13.2 us (3%)
  local copies, waits for them, and re-layouts  6.63 us (2%)
  matrix products  6.41 us (2%)
  other arithmetic  4.37 us (1%)
    psum x1, blocking collectives, on_device(): whole_out = lax.psum(partial_out, 'col')  168 us
    all_gather x1, waiting for transfers between devices, on_device(): all_tokens = lax.all_gather(tokens, 'col', axis=0, tiled=True)  87.2 us
    reduce_scatter x1, waiting for transfers between devices, on_device(): lax.psum_scatter(jnp.dot(all_tokens, both_weights, preferred_element_type...  59.4 us
    all_gather x1, waiting for transfers between devices, on_device(): hidden = lax.all_gather(hidden_share, 'row', axis=0, tiled=True)  43.1 us
  transfers between devices with their start and end apart: 3, of which 3 were waited for; matrix products, arithmetic and copies ran while one was open for 1% of the time, Pallas kernels for 0%

commit v1 on v0

v1 whole, which is shorter than its diff:
```python
import jax
import jax.numpy as jnp
from jax import lax
from jax.sharding import Mesh
from jax.sharding import PartitionSpec as P

BLK = 128

ROW = ("y", "c")
COL = ("z", "x")


def widen(block_mask):
    rows_blocks, cols_blocks = block_mask.shape
    spread = jnp.broadcast_to(block_mask[:, None, :, None], (rows_blocks, BLK, cols_blocks, BLK))
    return spread.reshape(rows_blocks * BLK, cols_blocks * BLK).astype(jnp.bfloat16)


def swiglu(summed, hidden_cols):
    return (jax.nn.silu(summed[:, :hidden_cols]) * summed[:, hidden_cols:]).astype(jnp.bfloat16)


def gather_rows(x, axes):
    for axis in reversed(axes):
        x = lax.all_gather(x, axis, axis=0, tiled=True)
    return x


def on_device(tokens, gate_weight, up_weight, down_weight, gate_mask, up_mask, down_mask):
    hidden_cols = gate_weight.shape[1]
    both_weights = jnp.concatenate(
        [gate_weight * widen(gate_mask), up_weight * widen(up_mask)], axis=1
    )
    down_eff = down_weight * widen(down_mask)
    all_tokens = gather_rows(tokens, COL)
    n_y, n_c = lax.axis_size("y"), lax.axis_size("c")
    rows, feats = all_tokens.shape
    share = rows // (n_y * n_c)
    by_core = all_tokens.reshape(n_y, n_c, share, feats).transpose(1, 0, 2, 3).reshape(rows, feats)
    partial = jnp.dot(by_core, both_weights, preferred_element_type=jnp.float32)
    partial = lax.psum_scatter(partial, "c", scatter_dimension=0, tiled=True)
    summed = lax.psum_scatter(partial, "y", scatter_dimension=0, tiled=True)
    hidden_share = swiglu(summed, hidden_cols)
    hidden = gather_rows(hidden_share, ROW)
    partial_out = jnp.dot(hidden, down_eff, preferred_element_type=jnp.float32)
    for axis in COL:
        partial_out = lax.psum_scatter(partial_out, axis, scatter_dimension=0, tiled=True)
    return partial_out.astype(jnp.bfloat16)


def solution(mesh):
    n_row, n_col = mesh.devices.shape
    n_c = 2
    n_x = 4
    sub = Mesh(
        mesh.devices.reshape(n_row // n_c, n_c, n_col // n_x, n_x), ROW + COL
    )
    placed = (
        P(COL, ROW),
        P(ROW, COL),
        P(ROW, COL),
        P(COL, ROW),
        P(ROW, COL),
        P(ROW, COL),
        P(COL, ROW),
    )
    return jax.shard_map(
        on_device, mesh=sub, in_specs=placed, out_specs=P(COL, ROW), check_vma=False
    )
```

time: 390 us -> 266 us (0.68)
  the two profiles are of different devices: /device:TPU:8 before, /device:TPU:1 now
where the time goes in v1:
time: 266 us; the launch traced here: 264 us
  waiting for transfers between devices  214 us (80%)
  blocking collectives  19.1 us (7%)
  between operations  13.5 us (5%)
  matrix products  6.55 us (2%)
  other arithmetic  5.21 us (2%)
  local copies, waits for them, and re-layouts  4.87 us (2%)
    all_gather x2, waiting for transfers between devices, gather_rows(): x = lax.all_gather(x, axis, axis=0, tiled=True)  74.6 us
    reduce_scatter x2, waiting for transfers between devices, on_device(): lax.psum_scatter(partial_out, axis, scatter_dimension=0, tiled=True)  74.5 us
    reduce_scatter x1, waiting for transfers between devices, on_device(): summed = lax.psum_scatter(partial, 'y', scatter_dimension=0, tiled=True)  41.3 us
    reduce_scatter x1, waiting for transfers between devices, on_device(): partial = lax.psum_scatter(partial, 'c', scatter_dimension=0, tiled=True)  23.9 us
    all_gather x2, blocking collectives, gather_rows(): x = lax.all_gather(x, axis, axis=0, tiled=True)  19.1 us
  transfers between devices with their start and end apart: 6, of which 6 were waited for; matrix products, arithmetic and copies ran while one was open for 1% of the time, Pallas kernels for 0%

profile of v1, /device:TPU:1, one launch (start us, length us, event | category | flops | bytes accessed | tf_op | source)
XLA Modules:
  0.0 263.9 jit_solution(16039085546751924385)
XLA Ops:
  6.5 0.0 all-gather.3.cloned.1.call-start
  6.5 12.5 %all_gather.12 = bf16[128,512]{1,0:T(8,128)(2,1)} all-gather(bf16[32,512]{1,0:T(8,128)(2,1)} %param.7), channel_id=1, replica_groups=mesh['y'=8,'c'=2,'z'=8,'x'=4] {'x'}, dimensions={0}, use_global_device_ids=true | all-gather | bytes 163840 | tf_op jit(solution)/shard_map/all_gather | solution.py:25
  19.0 0.0 all-gather.3.cloned.1.call-update
  19.0 0.0 reduce-scatter.7.cloned.1.call-start
  19.1 0.7 convert_element_type.29
  19.8 0.7 convert_element_type.27
  20.5 0.2 broadcast_in_dim.7
  20.7 0.2 broadcast_in_dim.6
  20.9 1.4 bitcast_multiply_fusion.2
  22.2 39.9 %all-gather.3.cloned.1.call-done = bf16[1024,512]{1,0:T(8,128)(2,1)} async-done(((bf16[128,512]{1,0:T(8,128)(2,1)}), bf16[1024,512]{1,0:T(8,128)(2,1)}) %all-gather.3.cloned.1.call-update) | async-done | bytes 1048592 | tf_op jit(solution)/shard_map/all_gather | solution.py:25
  62.1 1.3 copy.11
  63.4 3.3 %convolution_bitcast_fusion = f32[1024,1024]{0,1:T(8,128)} fusion(bf16[1024,512]{1,0:T(8,128)(2,1)S(1)} %bitcast.26, bf16[512,512]{1,0:T(8,128)(2,1)S(1)} %get-tuple-element.5, bf16[512,512]{1,0:T(8,128)(2,1)S(1)} %get-tuple-element.6), kind=kOutput, calls=%fused_computation | convolution fusion | flops 1075838976 | bytes 6291456 | tf_op jit(solution)/shard_map/dot_general | solution.py:40
  66.7 0.0 reduce-scatter.7.cloned.1.call-update
  66.7 0.0 reduce-scatter.13.cloned.1.call-start
  66.8 23.9 %reduce-scatter.7.cloned.1.call-done = f32[512,1024]{0,1:T(8,128)} async-done(((f32[1024,1024]{0,1:T(8,128)}), f32[512,1024]{0,1:T(8,128)}) %reduce-scatter.7.cloned.1.call-update) | async-done | bytes 2097168 | tf_op jit(solution)/shard_map/reduce_scatter | solution.py:41
  90.7 2.9 %copy.14 = f32[512,1024]{1,0:T(8,128)} copy(f32[512,1024]{0,1:T(8,128)} %reduce-scatter.7.cloned.1.call-done) | data formatting | bytes 4194304
  93.6 0.0 copy-start.1
  93.6 0.0 copy-start
  93.6 0.0 reduce-scatter.13.cloned.1.call-update
  93.6 0.0 all-gather.5.cloned.1.call-start
  93.7 41.3 %reduce-scatter.13.cloned.1.call-done = f32[64,1024]{1,0:T(8,128)} async-done(((f32[512,1024]{1,0:T(8,128)}), f32[64,1024]{1,0:T(8,128)}) %reduce-scatter.13.cloned.1.call-update) | async-done | bytes 262160 | tf_op jit(solution)/shard_map/reduce_scatter | solution.py:42
  134.9 1.0 fusion.5
  136.0 6.6 %all_gather.14 = bf16[128,512]{1,0:T(8,128)(2,1)} all-gather(bf16[64,512]{1,0:T(8,128)(2,1)S(1)} %fusion.5), channel_id=1, replica_groups=mesh['y'=8,'c'=2,'z'=8,'x'=4] {'c'}, dimensions={0}, use_global_device_ids=true | all-gather | bytes 196608 | tf_op jit(solution)/shard_map/all_gather | solution.py:25
  142.5 0.0 all-gather.5.cloned.1.call-update
  142.6 0.0 reduce-scatter.9.cloned.1.call-start
  142.6 0.0 copy-done.1
  142.6 34.8 %all-gather.5.cloned.1.call-done = bf16[1024,512]{1,0:T(8,128)(2,1)} async-done(((bf16[128,512]{1,0:T(8,128)(2,1)}), bf16[1024,512]{1,0:T(8,128)(2,1)}) %all-gather.5.cloned.1.call-update) | async-done | bytes 1048592 | tf_op jit(solution)/shard_map/all_gather | solution.py:25
  177.4 0.2 broadcast_in_dim.8
  177.6 0.0 copy-done
  177.6 3.3 %fusion.3 = f32[1024,512]{1,0:T(8,128)} fusion(bf16[1024,512]{1,0:T(8,128)(2,1)} %all-gather.5.cloned.1.call-done, bf16[512,512]{1,0:T(8,128)(2,1)S(1)} %copy-done, bf16[64,8,4,128]{3,2,1,0:T(4,128)(2,1)S(1)} %bitcast.24), kind=kOutput, calls=%fused_computation.5 | convolution fusion | flops 537133056 | bytes 4194304 | tf_op jit(solution)/shard_map/dot_general | solution.py:45
  180.9 0.0 reduce-scatter.9.cloned.1.call-update
  180.9 0.0 reduce-scatter.11.cloned.1.call-start
  181.0 45.7 %reduce-scatter.9.cloned.1.call-done = f32[128,512]{1,0:T(8,128)} async-done(((f32[1024,512]{1,0:T(8,128)}), f32[128,512]{1,0:T(8,128)}) %reduce-scatter.9.cloned.1.call-update) | async-done | bytes 262160 | tf_op jit(solution)/shard_map/reduce_scatter | solution.py:47
  226.7 0.0 reduce-scatter.11.cloned.1.call-update
  226.7 28.8 %reduce-scatter.11.cloned.1.call-done = f32[32,512]{1,0:T(8,128)} async-done(((f32[128,512]{1,0:T(8,128)}), f32[32,512]{1,0:T(8,128)}) %reduce-scatter.11.cloned.1.call-update) | async-done | bytes 65552 | tf_op jit(solution)/shard_map/reduce_scatter | solution.py:47
  255.6 1.5 convert_element_type.34
  (1 shorter events, 0.0 us)
Async XLA Ops:
  6.5 55.6 %all-gather.3.cloned.1.call-start = ((), (), s32[]{:S(2)}) async-start(), calls=%async_computation.4 | async-start | bytes 1179648 | tf_op jit(solution)/shard_map/all_gather | solution.py:25
  19.0 71.6 %reduce-scatter.7.cloned.1.call-start = ((), (), s32[]{:S(2)}) async-start(), calls=%async_computation.5 | async-start | bytes 6291456 | tf_op jit(solution)/shard_map/reduce_scatter | solution.py:41
  66.7 68.2 %reduce-scatter.13.cloned.1.call-start = ((), (), s32[]{:S(2)}) async-start(), calls=%async_computation.9 | async-start | bytes 2359296 | tf_op jit(solution)/shard_map/reduce_scatter | solution.py:42
  93.6 49.0 %copy-start.1 = (s32[4,4]{1,0:T(4,128)S(1)}, s32[4,4]{1,0:T(4,128)}, u32[]{:S(2)}) copy-start(s32[4,4]{1,0:T(4,128)} %param.13) | copy-start | bytes 196
  93.6 84.0 %copy-start = (bf16[512,512]{1,0:T(8,128)(2,1)S(1)}, bf16[512,512]{1,0:T(8,128)(2,1)}, u32[]{:S(2)}) copy-start(bf16[512,512]{1,0:T(8,128)(2,1)} %param.10) | copy-start | bytes 1572868
  93.6 83.8 %all-gather.5.cloned.1.call-start = ((), (), s32[]{:S(2)}) async-start(), calls=%async_computation.6 | async-start | bytes 1179648 | tf_op jit(solution)/shard_map/all_gather | solution.py:25
  142.6 84.1 %reduce-scatter.9.cloned.1.call-start = ((), (), s32[]{:S(2)}) async-start(), calls=%async_computation.7 | async-start | bytes 2359296 | tf_op jit(solution)/shard_map/reduce_scatter | solution.py:47
  180.9 74.6 %reduce-scatter.11.cloned.1.call-start = ((), (), s32[]{:S(2)}) async-start(), calls=%async_computation.8 | async-start | bytes 327680 | tf_op jit(solution)/shard_map/reduce_scatter | solution.py:47
Sparse Core Ops, SparseCore 0:
  19.2 42.9 all-gather.2
  66.8 23.7 reduce-scatter.6
  93.8 41.1 reduce-scatter.12
  142.7 34.6 all-gather.4
  181.1 45.5 reduce-scatter.8
  229.4 26.1 reduce-scatter.10

commit v2 on v1

--- a/solution.py
+++ b/solution.py
@@ -20,10 +20,16 @@
     return (jax.nn.silu(summed[:, :hidden_cols]) * summed[:, hidden_cols:]).astype(jnp.bfloat16)
 
 
-def gather_rows(x, axes):
-    for axis in reversed(axes):
-        x = lax.all_gather(x, axis, axis=0, tiled=True)
-    return x
+def gather_a2a(x, axis):
+    n = lax.axis_size(axis)
+    copies = jnp.broadcast_to(x[None], (n,) + x.shape).reshape((n * x.shape[0],) + x.shape[1:])
+    return lax.all_to_all(copies, axis, 0, 0, tiled=True)
+
+
+def scatter_sum_a2a(x, axis):
+    n = lax.axis_size(axis)
+    got = lax.all_to_all(x, axis, 0, 0, tiled=True)
+    return got.reshape((n, x.shape[0] // n) + x.shape[1:]).sum(axis=0)
 
 
 def on_device(tokens, gate_weight, up_weight, down_weight, gate_mask, up_mask, down_mask):
@@ -32,19 +38,19 @@
         [gate_weight * widen(gate_mask), up_weight * widen(up_mask)], axis=1
     )
     down_eff = down_weight * widen(down_mask)
-    all_tokens = gather_rows(tokens, COL)
+    all_tokens = gather_a2a(lax.all_gather(tokens, "x", axis=0, tiled=True), "z")
     n_y, n_c = lax.axis_size("y"), lax.axis_size("c")
     rows, feats = all_tokens.shape
     share = rows // (n_y * n_c)
     by_core = all_tokens.reshape(n_y, n_c, share, feats).transpose(1, 0, 2, 3).reshape(rows, feats)
     partial = jnp.dot(by_core, both_weights, preferred_element_type=jnp.float32)
-    partial = lax.psum_scatter(partial, "c", scatter_dimension=0, tiled=True)
-    summed = lax.psum_scatter(partial, "y", scatter_dimension=0, tiled=True)
+    summed = scatter_sum_a2a(scatter_sum_a2a(partial, "c"), "y")
     hidden_share = swiglu(summed, hidden_cols)
-    hidden = gather_rows(hidden_share, ROW)
+    half = gather_a2a(hidden_share, "y")
+    both = lax.all_gather(half, "c", axis=0, tiled=True)
+    hidden = both.reshape(n_c, n_y, share, -1).transpose(1, 0, 2, 3).reshape(rows, -1)
     partial_out = jnp.dot(hidden, down_eff, preferred_element_type=jnp.float32)
-    for axis in COL:
-        partial_out = lax.psum_scatter(partial_out, axis, scatter_dimension=0, tiled=True)
+    partial_out = scatter_sum_a2a(scatter_sum_a2a(partial_out, "z"), "x")
     return partial_out.astype(jnp.bfloat16)
 
 

time: 266 us -> 237 us (0.89)
  waiting for transfers between devices: 214 us -> 37 us
  blocking collectives: 19.1 us -> 164 us
  starting transfers between devices: 0.21 us -> 10.1 us
  matrix products: 6.55 us -> 1.96 us
    all_to_all x0 -> x5, blocking collectives: none -> 154 us  [the longest x4 135 us: scatter_sum_a2a(): got = lax.all_to_all(x, axis, 0, 0, tiled=True)]
    reduce_scatter x4 -> x0, waiting for transfers between devices: 140 us -> none  [the longest x2 74.5 us: on_device(): lax.psum_scatter(partial_out, axis, scatter_dimension=0, tiled=True)]
    all_gather x2 -> x1, waiting for transfers between devices: 74.6 us -> 11.7 us  [on_device(): both = lax.all_gather(half, 'c', axis=0, tiled=True)]
    all_to_all x0 -> x1, waiting for transfers between devices: none -> 25.2 us  [gather_a2a(): return lax.all_to_all(copies, axis, 0, 0, tiled=True)]
    all_to_all x0 -> x1, starting transfers between devices: none -> 10.1 us  [gather_a2a(): return lax.all_to_all(copies, axis, 0, 0, tiled=True)]
    all_gather x2 -> x1, blocking collectives: 19.1 us -> 10.6 us  [on_device(): lax.all_gather(tokens, 'x', axis=0, tiled=True)]
    reduce_sum x0 -> x4, other arithmetic: none -> 5.37 us  [scatter_sum_a2a(): return got.reshape((n, x.shape[0] // n) + x.shape[1:]).sum(axis=0)]
    unnamed x5 -> x12, local copies, waits for them, and re-layouts: 2.94 us -> 0.02 us
  transfers between devices with their start and end apart: 6 -> 2, of which waited for: 6 -> 2; matrix products, arithmetic and copies ran while one was open for 1% -> 0% of each run, Pallas kernels for 0% -> 0%
where the time goes in v2:
time: 237 us; the launch traced here: 236 us
  blocking collectives  164 us (69%)
  waiting for transfers between devices  37 us (16%)
  between operations  13.6 us (6%)
  starting transfers between devices  10.1 us (4%)
  other arithmetic  5.59 us (2%)
  local copies, waits for them, and re-layouts  3.13 us (1%)
    all_to_all x4, blocking collectives, scatter_sum_a2a(): got = lax.all_to_all(x, axis, 0, 0, tiled=True)  135 us
    all_to_all x1, waiting for transfers between devices, gather_a2a(): return lax.all_to_all(copies, axis, 0, 0, tiled=True)  25.2 us
    all_to_all x1, blocking collectives, gather_a2a(): return lax.all_to_all(copies, axis, 0, 0, tiled=True)  18.3 us
    all_gather x1, waiting for transfers between devices, on_device(): both = lax.all_gather(half, 'c', axis=0, tiled=True)  11.7 us
    all_gather x1, blocking collectives, on_device(): lax.all_gather(tokens, 'x', axis=0, tiled=True)  10.6 us
    all_to_all x1, starting transfers between devices, gather_a2a(): return lax.all_to_all(copies, axis, 0, 0, tiled=True)  10.1 us
    reduce_sum x4, other arithmetic, scatter_sum_a2a(): return got.reshape((n, x.shape[0] // n) + x.shape[1:]).sum(axis=0)  5.37 us
  transfers between devices with their start and end apart: 2, of which 2 were waited for; matrix products, arithmetic and copies ran while one was open for 0% of the time, Pallas kernels for 0%

profile of v2, /device:TPU:1, one launch (start us, length us, event | category | flops | bytes accessed | tf_op | source)
XLA Modules:
  0.0 235.7 jit_solution(4000642944982304375)
XLA Ops:
  6.5 0.0 copy-start.3
  6.5 0.0 copy-start.4
  6.5 10.6 %all_gather.6 = bf16[128,512]{1,0:T(8,128)(2,1)S(1)} all-gather(bf16[32,512]{1,0:T(8,128)(2,1)} %param.7), channel_id=1, replica_groups=mesh['y'=8,'c'=2,'z'=8,'x'=4] {'x'}, dimensions={0}, use_global_device_ids=true | all-gather | bytes 163840 | tf_op jit(solution)/shard_map/all_gather | solution.py:41
  17.1 0.0 copy-start
  17.1 0.0 copy-start.1
  17.1 1.1 broadcast_in_dim.12
  18.2 10.1 %all-to-all-start = ((bf16[8,128,512]{2,1,0:T(8,128)(2,1)}), bf16[8,128,512]{2,1,0:T(8,128)(2,1)S(1)}, u32[]{:S(2)}, u32[]{:S(2)}) async-start(bf16[8,128,512]{2,1,0:T(8,128)(2,1)} %broadcast_in_dim.12), calls=%async_computation | async-start | bytes 2097152 | tf_op jit(solution)/shard_map/all_to_all | solution.py:26
  28.3 0.0 all-gather.2.cloned.1.call-start
  28.3 0.0 copy-done.3
  28.3 0.0 copy-done.4
  28.4 0.2 broadcast_in_dim.10
  28.6 0.2 broadcast_in_dim.11
  28.8 0.0 copy-done
  28.8 0.0 copy-done.1
  28.8 0.2 bitcast_multiply_fusion.1
  29.0 25.2 %all-to-all-done = bf16[8,128,512]{2,1,0:T(8,128)(2,1)S(1)} async-done(((bf16[8,128,512]{2,1,0:T(8,128)(2,1)}), bf16[8,128,512]{2,1,0:T(8,128)(2,1)S(1)}, u32[]{:S(2)}, u32[]{:S(2)}) %all-to-all-start) | async-done | bytes 1048608 | tf_op jit(solution)/shard_map/all_to_all | solution.py:26
  54.2 0.1 copy.11
  54.3 1.2 fusion
  55.5 11.6 %all_to_all.48 = f32[2,512,1024]{2,1,0:T(8,128)} all-to-all(f32[2,512,1024]{2,1,0:T(8,128)S(1)} %bitcast.34), channel_id=1, replica_groups=mesh['y'=8,'c'=2,'z'=8,'x'=4] {'c'}, dimensions={0} | all-to-all | bytes 8388608 | tf_op jit(solution)/shard_map/all_to_all | solution.py:31
  67.1 2.8 %reduce_sum.36 = f32[512,1024]{1,0:T(8,128)S(1)} reduce(f32[2,512,1024]{2,1,0:T(8,128)} %all_to_all.48, f32[]{:T(128)} %constant.1.clone.1), dimensions={0}, to_apply=%region_0.0 | reduce | flops 524288 | bytes 6291460 | tf_op jit(solution)/shard_map/reduce_sum | solution.py:32
  69.9 57.2 %all_to_all.49 = f32[8,64,1024]{2,1,0:T(8,128)} all-to-all(f32[8,64,1024]{2,1,0:T(8,128)S(1)} %bitcast.35), channel_id=1, replica_groups=mesh['y'=8,'c'=2,'z'=8,'x'=4] {'y'}, dimensions={0} | all-to-all | bytes 4194304 | tf_op jit(solution)/shard_map/all_to_all | solution.py:31
  127.1 0.0 copy-start.5
  127.1 1.7 reduce_sum.37
  128.9 0.0 copy-start.2
  128.9 18.3 %all_to_all.50 = bf16[8,64,512]{2,1,0:T(8,128)(2,1)} all-to-all(bf16[8,64,512]{2,1,0:T(8,128)(2,1)S(1)} %broadcast_in_dim.13), channel_id=1, replica_groups=mesh['y'=8,'c'=2,'z'=8,'x'=4] {'y'}, dimensions={0} | all-to-all | bytes 1048576 | tf_op jit(solution)/shard_map/all_to_all | solution.py:26
  147.3 0.0 all-gather.2.cloned.1.call-update
  147.3 0.0 copy-done.5
  147.3 11.7 %all-gather.2.cloned.1.call-done = bf16[1024,512]{1,0:T(8,128)(2,1)} async-done(((bf16[512,512]{1,0:T(8,128)(2,1)}), bf16[1024,512]{1,0:T(8,128)(2,1)}) %all-gather.2.cloned.1.call-update) | async-done | bytes 1048592 | tf_op jit(solution)/shard_map/all_gather | solution.py:50
  159.0 1.3 copy.12
  160.3 0.2 broadcast_in_dim.14
  160.5 0.0 copy-done.2
  160.6 0.7 fusion.5
  161.3 57.4 %all_to_all.51 = f32[8,128,512]{2,1,0:T(8,128)S(1)} all-to-all(f32[8,128,512]{2,1,0:T(8,128)S(1)} %fusion.5), channel_id=1, replica_groups=mesh['y'=8,'c'=2,'z'=8,'x'=4] {'z'}, dimensions={0} | all-to-all | bytes 4194304 | tf_op jit(solution)/shard_map/all_to_all | solution.py:31
  218.7 0.2 reduce_sum.38
  218.9 9.3 %all_to_all.52 = f32[4,32,512]{2,1,0:T(8,128)S(1)} all-to-all(f32[4,32,512]{2,1,0:T(8,128)S(1)} %bitcast.43), channel_id=1, replica_groups=mesh['y'=8,'c'=2,'z'=8,'x'=4] {'x'}, dimensions={0} | all-to-all | bytes 524288 | tf_op jit(solution)/shard_map/all_to_all | solution.py:31
  228.2 0.6 reduce_sum.39
  (5 shorter events, 0.1 us)
Async XLA Ops:
  6.5 21.8 %copy-start.3 = (s32[4,4]{1,0:T(4,128)S(1)}, s32[4,4]{1,0:T(4,128)}, u32[]{:S(2)}) copy-start(s32[4,4]{1,0:T(4,128)} %param.11) | copy-start | bytes 196
  6.5 21.8 %copy-start.4 = (s32[4,4]{1,0:T(4,128)S(1)}, s32[4,4]{1,0:T(4,128)}, u32[]{:S(2)}) copy-start(s32[4,4]{1,0:T(4,128)} %param.12) | copy-start | bytes 196
  17.1 11.6 %copy-start = (bf16[512,512]{1,0:T(8,128)(2,1)S(1)}, bf16[512,512]{1,0:T(8,128)(2,1)}, u32[]{:S(2)}) copy-start(bf16[512,512]{1,0:T(8,128)(2,1)} %param.9) | copy-start | bytes 1572868
  17.1 11.7 %copy-start.1 = (bf16[512,512]{1,0:T(8,128)(2,1)S(1)}, bf16[512,512]{1,0:T(8,128)(2,1)}, u32[]{:S(2)}) copy-start(bf16[512,512]{1,0:T(8,128)(2,1)} %param.8) | copy-start | bytes 1572868
  18.2 36.0 %all-to-all-start = ((bf16[8,128,512]{2,1,0:T(8,128)(2,1)}), bf16[8,128,512]{2,1,0:T(8,128)(2,1)S(1)}, u32[]{:S(2)}, u32[]{:S(2)}) async-start(bf16[8,128,512]{2,1,0:T(8,128)(2,1)} %broadcast_in_dim.12), calls=%async_computation | async-start | bytes 2097152 | tf_op jit(solution)/shard_map/all_to_all | solution.py:26
  28.3 130.7 %all-gather.2.cloned.1.call-start = ((), (), s32[]{:S(2)}) async-start(), calls=%async_computation.6 | async-start | bytes 1572864 | tf_op jit(solution)/shard_map/all_gather | solution.py:50
  127.1 20.2 %copy-start.5 = (s32[4,4]{1,0:T(4,128)S(1)}, s32[4,4]{1,0:T(4,128)}, u32[]{:S(2)}) copy-start(s32[4,4]{1,0:T(4,128)} %param.13) | copy-start | bytes 196
  128.9 31.6 %copy-start.2 = (bf16[512,512]{1,0:T(8,128)(2,1)S(1)}, bf16[512,512]{1,0:T(8,128)(2,1)}, u32[]{:S(2)}) copy-start(bf16[512,512]{1,0:T(8,128)(2,1)} %param.10) | copy-start | bytes 1572868
Sparse Core Ops, SparseCore 0:
  147.4 11.5 all-gather.1

commit v3 on v2

--- a/solution.py
+++ b/solution.py
@@ -1,3 +1,5 @@
+import math
+
 import jax
 import jax.numpy as jnp
 from jax import lax
@@ -20,14 +22,19 @@
     return (jax.nn.silu(summed[:, :hidden_cols]) * summed[:, hidden_cols:]).astype(jnp.bfloat16)
 
 
+def group_size(axis):
+    axes = axis if isinstance(axis, tuple) else (axis,)
+    return math.prod(lax.axis_size(a) for a in axes)
+
+
 def gather_a2a(x, axis):
-    n = lax.axis_size(axis)
+    n = group_size(axis)
     copies = jnp.broadcast_to(x[None], (n,) + x.shape).reshape((n * x.shape[0],) + x.shape[1:])
     return lax.all_to_all(copies, axis, 0, 0, tiled=True)
 
 
 def scatter_sum_a2a(x, axis):
-    n = lax.axis_size(axis)
+    n = group_size(axis)
     got = lax.all_to_all(x, axis, 0, 0, tiled=True)
     return got.reshape((n, x.shape[0] // n) + x.shape[1:]).sum(axis=0)
 
@@ -38,19 +45,19 @@
         [gate_weight * widen(gate_mask), up_weight * widen(up_mask)], axis=1
     )
     down_eff = down_weight * widen(down_mask)
-    all_tokens = gather_a2a(lax.all_gather(tokens, "x", axis=0, tiled=True), "z")
+    all_tokens = gather_a2a(tokens, COL)
     n_y, n_c = lax.axis_size("y"), lax.axis_size("c")
     rows, feats = all_tokens.shape
     share = rows // (n_y * n_c)
     by_core = all_tokens.reshape(n_y, n_c, share, feats).transpose(1, 0, 2, 3).reshape(rows, feats)
     partial = jnp.dot(by_core, both_weights, preferred_element_type=jnp.float32)
-    summed = scatter_sum_a2a(scatter_sum_a2a(partial, "c"), "y")
+    summed = lax.psum_scatter(scatter_sum_a2a(partial, "c"), "y", scatter_dimension=0, tiled=True)
     hidden_share = swiglu(summed, hidden_cols)
     half = gather_a2a(hidden_share, "y")
-    both = lax.all_gather(half, "c", axis=0, tiled=True)
+    both = gather_a2a(half, "c")
     hidden = both.reshape(n_c, n_y, share, -1).transpose(1, 0, 2, 3).reshape(rows, -1)
     partial_out = jnp.dot(hidden, down_eff, preferred_element_type=jnp.float32)
-    partial_out = scatter_sum_a2a(scatter_sum_a2a(partial_out, "z"), "x")
+    partial_out = scatter_sum_a2a(lax.psum_scatter(partial_out, "z", scatter_dimension=0, tiled=True), "x")
     return partial_out.astype(jnp.bfloat16)
 
 

time: 237 us -> 195 us (0.82)
  the two profiles are of different devices: /device:TPU:1 before, /device:TPU:8 now
where the time goes in v3:
time: 195 us
  waiting for transfers between devices  125 us (64%)
  blocking collectives  24.1 us (12%)
  starting transfers between devices  18.6 us (10%)
  between operations  13.5 us (7%)
  other arithmetic  5.92 us (3%)
  local copies, waits for them, and re-layouts  3.63 us (2%)
  matrix products  3.31 us (2%)
    reduce_scatter x1, waiting for transfers between devices, on_device(): lax.psum_scatter(partial_out, 'z', scatter_dimension=0, tiled=True)  44.4 us
    reduce_scatter x1, waiting for transfers between devices, on_device(): lax.psum_scatter(scatter_sum_a2a(partial, 'c'), 'y', scatter_dimension=0,...  41.8 us
    all_to_all x2, waiting for transfers between devices, gather_a2a(): return lax.all_to_all(copies, axis, 0, 0, tiled=True)  39.2 us
    all_to_all x2, blocking collectives, scatter_sum_a2a(): got = lax.all_to_all(x, axis, 0, 0, tiled=True)  19.4 us
    all_to_all x2, starting transfers between devices, gather_a2a(): return lax.all_to_all(copies, axis, 0, 0, tiled=True)  18.6 us
    reduce_sum x2, other arithmetic, scatter_sum_a2a(): return got.reshape((n, x.shape[0] // n) + x.shape[1:]).sum(axis=0)  4.74 us
    all_to_all x1, blocking collectives, gather_a2a(): return lax.all_to_all(copies, axis, 0, 0, tiled=True)  4.71 us
  transfers between devices with their start and end apart: 4, of which 4 were waited for; matrix products, arithmetic and copies ran while one was open for 0% of the time, Pallas kernels for 0%

profile of v3, /device:TPU:8, one launch (start us, length us, event | category | flops | bytes accessed | tf_op | source)
XLA Modules:
  0.0 194.6 jit_solution(11767634492538882377)
XLA Ops:
  6.5 0.0 copy-start.3
  6.5 0.0 copy-start.4
  6.5 0.0 copy-start.1
  6.5 0.0 copy-start
  6.5 1.9 broadcast_in_dim.16
  8.5 13.2 %all-to-all-start = ((bf16[32,32,512]{2,1,0:T(8,128)(2,1)}), bf16[32,32,512]{2,1,0:T(8,128)(2,1)S(1)}, u32[]{:S(2)}, u32[]{:S(2)}) async-start(bf16[32,32,512]{2,1,0:T(8,128)(2,1)} %broadcast_in_dim.16), calls=%async_computation | async-start | bytes 2097152 | tf_op jit(solution)/shard_map/all_to_all | solution.py:33
  21.7 0.0 reduce-scatter.3.cloned.1.call-start
  21.7 0.0 copy-done.3
  21.7 0.0 copy-done.4
  21.7 0.2 broadcast_in_dim.14
  22.0 0.2 broadcast_in_dim.15
  22.2 0.0 copy-done.1
  22.2 0.0 copy-done
  22.2 0.2 bitcast_multiply_fusion.2
  22.3 27.4 %all-to-all-done = bf16[32,32,512]{2,1,0:T(8,128)(2,1)S(1)} async-done(((bf16[32,32,512]{2,1,0:T(8,128)(2,1)}), bf16[32,32,512]{2,1,0:T(8,128)(2,1)S(1)}, u32[]{:S(2)}, u32[]{:S(2)}) %all-to-all-start) | async-done | bytes 1048608 | tf_op jit(solution)/shard_map/all_to_all | solution.py:33
  49.7 0.1 copy.8
  49.8 1.2 fusion
  51.0 8.2 %all_to_all.36 = f32[2,512,1024]{2,1,0:T(8,128)} all-to-all(f32[2,512,1024]{2,1,0:T(8,128)S(1)} %bitcast.28), channel_id=1, replica_groups=mesh['y'=8,'c'=2,'z'=8,'x'=4] {'c'}, dimensions={0} | all-to-all | bytes 8388608 | tf_op jit(solution)/shard_map/all_to_all | solution.py:38
  59.2 4.1 %reduce_sum.18 = f32[512,1024]{1,0:T(8,128)} reduce(f32[2,512,1024]{2,1,0:T(8,128)} %all_to_all.36, f32[]{:T(128)} %constant.1.clone.1), dimensions={0}, to_apply=%region_0.0 | reduce | flops 524288 | bytes 6291460 | tf_op jit(solution)/shard_map/reduce_sum | solution.py:39
  63.3 0.0 copy-start.5
  63.3 0.0 reduce-scatter.3.cloned.1.call-update
  63.3 41.8 %reduce-scatter.3.cloned.1.call-done = f32[64,1024]{1,0:T(8,128)} async-done(((f32[512,1024]{1,0:T(8,128)}), f32[64,1024]{1,0:T(8,128)}) %reduce-scatter.3.cloned.1.call-update) | async-done | bytes 262160 | tf_op jit(solution)/shard_map/reduce_scatter | solution.py:54
  105.2 1.0 fusion.6
  106.2 0.8 broadcast_in_dim.17
  107.0 5.4 %all-to-all-start.2 = ((bf16[8,64,512]{2,1,0:T(8,128)(2,1)}), bf16[8,64,512]{2,1,0:T(8,128)(2,1)S(1)}, u32[]{:S(2)}, u32[]{:S(2)}) async-start(bf16[8,64,512]{2,1,0:T(8,128)(2,1)} %broadcast_in_dim.17), calls=%async_computation.3 | async-start | bytes 1048576 | tf_op jit(solution)/shard_map/all_to_all | solution.py:33
  112.4 0.0 reduce-scatter.5.cloned.1.call-start
  112.4 0.0 copy-done.5
  112.4 11.8 %all-to-all-done.2 = bf16[8,64,512]{2,1,0:T(8,128)(2,1)S(1)} async-done(((bf16[8,64,512]{2,1,0:T(8,128)(2,1)}), bf16[8,64,512]{2,1,0:T(8,128)(2,1)S(1)}, u32[]{:S(2)}, u32[]{:S(2)}) %all-to-all-start.2) | async-done | bytes 524320 | tf_op jit(solution)/shard_map/all_to_all | solution.py:33
  124.3 0.1 broadcast_in_dim.19
  124.3 0.0 copy-start.2
  124.4 4.7 %all_to_all.37 = bf16[2,512,512]{2,1,0:T(8,128)(2,1)S(1)} all-to-all(bf16[2,512,512]{2,1,0:T(8,128)(2,1)S(1)} %broadcast_in_dim.19), channel_id=1, replica_groups=mesh['y'=8,'c'=2,'z'=8,'x'=4] {'c'}, dimensions={0} | all-to-all | bytes 2097152 | tf_op jit(solution)/shard_map/all_to_all | solution.py:33
  129.1 0.1 copy.9
  129.2 0.2 broadcast_in_dim.20
  129.4 0.0 copy-done.2
  129.4 2.1 %fusion.4 = f32[1024,512]{1,0:T(8,128)} fusion(bf16[1024,512]{1,0:T(8,128)(2,1)S(1)} %bitcast.32, bf16[512,512]{1,0:T(8,128)(2,1)S(1)} %copy-done.2, bf16[64,8,4,128]{3,2,1,0:T(4,128)(2,1)S(1)} %bitcast.36), kind=kOutput, calls=%fused_computation.5 | convolution fusion | flops 537133056 | bytes 4194304 | tf_op jit(solution)/shard_map/dot_general | solution.py:59
  131.4 0.0 reduce-scatter.5.cloned.1.call-update
  131.5 44.4 %reduce-scatter.5.cloned.1.call-done = f32[128,512]{1,0:T(8,128)} async-done(((f32[1024,512]{1,0:T(8,128)}), f32[128,512]{1,0:T(8,128)}) %reduce-scatter.5.cloned.1.call-update) | async-done | bytes 262160 | tf_op jit(solution)/shard_map/reduce_scatter | solution.py:60
  175.9 11.3 %all_to_all.38 = f32[4,32,512]{2,1,0:T(8,128)S(1)} all-to-all(f32[4,32,512]{2,1,0:T(8,128)} %bitcast.37), channel_id=1, replica_groups=mesh['y'=8,'c'=2,'z'=8,'x'=4] {'x'}, dimensions={0} | all-to-all | bytes 524288 | tf_op jit(solution)/shard_map/all_to_all | solution.py:38
  187.1 0.6 reduce_sum.19
  (3 shorter events, 0.0 us)
Async XLA Ops:
  6.5 15.2 %copy-start.3 = (s32[4,4]{1,0:T(4,128)S(1)}, s32[4,4]{1,0:T(4,128)}, u32[]{:S(2)}) copy-start(s32[4,4]{1,0:T(4,128)} %param.11) | copy-start | bytes 196
  6.5 15.2 %copy-start.4 = (s32[4,4]{1,0:T(4,128)S(1)}, s32[4,4]{1,0:T(4,128)}, u32[]{:S(2)}) copy-start(s32[4,4]{1,0:T(4,128)} %param.12) | copy-start | bytes 196
  6.5 15.6 %copy-start.1 = (bf16[512,512]{1,0:T(8,128)(2,1)S(1)}, bf16[512,512]{1,0:T(8,128)(2,1)}, u32[]{:S(2)}) copy-start(bf16[512,512]{1,0:T(8,128)(2,1)} %param.8) | copy-start | bytes 1572868
  6.5 15.6 %copy-start = (bf16[512,512]{1,0:T(8,128)(2,1)S(1)}, bf16[512,512]{1,0:T(8,128)(2,1)}, u32[]{:S(2)}) copy-start(bf16[512,512]{1,0:T(8,128)(2,1)} %param.9) | copy-start | bytes 1572868
  8.5 41.2 %all-to-all-start = ((bf16[32,32,512]{2,1,0:T(8,128)(2,1)}), bf16[32,32,512]{2,1,0:T(8,128)(2,1)S(1)}, u32[]{:S(2)}, u32[]{:S(2)}) async-start(bf16[32,32,512]{2,1,0:T(8,128)(2,1)} %broadcast_in_dim.16), calls=%async_computation | async-start | bytes 2097152 | tf_op jit(solution)/shard_map/all_to_all | solution.py:33
  21.7 83.5 %reduce-scatter.3.cloned.1.call-start = ((), (), s32[]{:S(2)}) async-start(), calls=%async_computation.7 | async-start | bytes 2359296 | tf_op jit(solution)/shard_map/reduce_scatter | solution.py:54
  63.3 49.1 %copy-start.5 = (s32[4,4]{1,0:T(4,128)S(1)}, s32[4,4]{1,0:T(4,128)}, u32[]{:S(2)}) copy-start(s32[4,4]{1,0:T(4,128)} %param.13) | copy-start | bytes 196
  107.0 17.3 %all-to-all-start.2 = ((bf16[8,64,512]{2,1,0:T(8,128)(2,1)}), bf16[8,64,512]{2,1,0:T(8,128)(2,1)S(1)}, u32[]{:S(2)}, u32[]{:S(2)}) async-start(bf16[8,64,512]{2,1,0:T(8,128)(2,1)} %broadcast_in_dim.17), calls=%async_computation.3 | async-start | bytes 1048576 | tf_op jit(solution)/shard_map/all_to_all | solution.py:33
  112.4 63.4 %reduce-scatter.5.cloned.1.call-start = ((), (), s32[]{:S(2)}) async-start(), calls=%async_computation.8 | async-start | bytes 2359296 | tf_op jit(solution)/shard_map/reduce_scatter | solution.py:60
  124.3 5.0 %copy-start.2 = (bf16[512,512]{1,0:T(8,128)(2,1)S(1)}, bf16[512,512]{1,0:T(8,128)(2,1)}, u32[]{:S(2)}) copy-start(bf16[512,512]{1,0:T(8,128)(2,1)} %param.10) | copy-start | bytes 1572868
Sparse Core Ops, SparseCore 0:
  63.4 41.6 reduce-scatter.2
  131.6 44.2 reduce-scatter.4

commit v4 on v3

--- a/solution.py
+++ b/solution.py
@@ -33,10 +33,10 @@
     return lax.all_to_all(copies, axis, 0, 0, tiled=True)
 
 
-def scatter_sum_a2a(x, axis):
+def scatter_sum_a2a(x, axis, sent=jnp.float32):
     n = group_size(axis)
-    got = lax.all_to_all(x, axis, 0, 0, tiled=True)
-    return got.reshape((n, x.shape[0] // n) + x.shape[1:]).sum(axis=0)
+    got = lax.all_to_all(x.astype(sent), axis, 0, 0, tiled=True)
+    return got.reshape((n, x.shape[0] // n) + x.shape[1:]).astype(jnp.float32).sum(axis=0)
 
 
 def on_device(tokens, gate_weight, up_weight, down_weight, gate_mask, up_mask, down_mask):
@@ -51,13 +51,13 @@
     share = rows // (n_y * n_c)
     by_core = all_tokens.reshape(n_y, n_c, share, feats).transpose(1, 0, 2, 3).reshape(rows, feats)
     partial = jnp.dot(by_core, both_weights, preferred_element_type=jnp.float32)
-    summed = lax.psum_scatter(scatter_sum_a2a(partial, "c"), "y", scatter_dimension=0, tiled=True)
+    summed = scatter_sum_a2a(scatter_sum_a2a(partial, "c"), "y", sent=jnp.bfloat16)
     hidden_share = swiglu(summed, hidden_cols)
     half = gather_a2a(hidden_share, "y")
     both = gather_a2a(half, "c")
     hidden = both.reshape(n_c, n_y, share, -1).transpose(1, 0, 2, 3).reshape(rows, -1)
     partial_out = jnp.dot(hidden, down_eff, preferred_element_type=jnp.float32)
-    partial_out = scatter_sum_a2a(lax.psum_scatter(partial_out, "z", scatter_dimension=0, tiled=True), "x")
+    partial_out = scatter_sum_a2a(scatter_sum_a2a(partial_out, "z", sent=jnp.bfloat16), "x")
     return partial_out.astype(jnp.bfloat16)
 
 

time: 195 us -> 162 us (0.83)
  the two profiles are of different devices: /device:TPU:8 before, /device:TPU:1 now
where the time goes in v4:
time: 162 us
  blocking collectives  93.3 us (58%)
  waiting for transfers between devices  41.5 us (26%)
  starting transfers between devices  17.2 us (11%)
  other arithmetic  3.91 us (2%)
  local copies, waits for them, and re-layouts  3.65 us (2%)
  matrix products  1.96 us (1%)
    all_to_all x4, blocking collectives, scatter_sum_a2a(): got = lax.all_to_all(x.astype(sent), axis, 0, 0, tiled=True)  86.6 us
    all_to_all x2, waiting for transfers between devices, gather_a2a(): return lax.all_to_all(copies, axis, 0, 0, tiled=True)  41.5 us
    all_to_all x2, starting transfers between devices, gather_a2a(): return lax.all_to_all(copies, axis, 0, 0, tiled=True)  17.2 us
    all_to_all x1, blocking collectives, gather_a2a(): return lax.all_to_all(copies, axis, 0, 0, tiled=True)  6.77 us
    reduce_sum x4, other arithmetic, scatter_sum_a2a(): got.reshape((n, x.shape[0] // n) + x.shape[1:]).astype(jnp.float32)  3.69 us
  transfers between devices with their start and end apart: 2, of which 2 were waited for; matrix products, arithmetic and copies ran while one was open for 0% of the time, Pallas kernels for 0%

profile of v4, /device:TPU:1, one launch (start us, length us, event | category | flops | bytes accessed | tf_op | source)
XLA Modules:
  0.0 161.7 jit_solution(11395514944804389176)
XLA Ops:
  0.0 0.0 copy-start.2
  0.0 0.0 copy-start.3
  0.0 0.0 copy-start.1
  0.0 0.0 copy-start
  0.0 2.0 %broadcast_in_dim.16 = bf16[32,32,512]{2,1,0:T(8,128)(2,1)} broadcast(bf16[32,512]{1,0:T(8,128)(2,1)} %param.7), dimensions={1,2} | broadcast | bytes 1081344 | tf_op jit(solution)/shard_map/broadcast_in_dim | solution.py:32
  2.0 13.7 %all-to-all-start = ((bf16[32,32,512]{2,1,0:T(8,128)(2,1)}), bf16[32,32,512]{2,1,0:T(8,128)(2,1)S(1)}, u32[]{:S(2)}, u32[]{:S(2)}) async-start(bf16[32,32,512]{2,1,0:T(8,128)(2,1)} %broadcast_in_dim.16), calls=%async_computation | async-start | bytes 2097152 | tf_op jit(solution)/shard_map/all_to_all | solution.py:33
  15.7 0.0 copy-done.2
  15.7 0.0 copy-done.3
  15.7 0.2 broadcast_in_dim.14
  15.9 0.2 broadcast_in_dim.15
  16.2 0.0 copy-done.1
  16.2 0.0 copy-done
  16.2 0.2 bitcast_multiply_fusion.2
  16.3 25.6 %all-to-all-done = bf16[32,32,512]{2,1,0:T(8,128)(2,1)S(1)} async-done(((bf16[32,32,512]{2,1,0:T(8,128)(2,1)}), bf16[32,32,512]{2,1,0:T(8,128)(2,1)S(1)}, u32[]{:S(2)}, u32[]{:S(2)}) %all-to-all-start) | async-done | bytes 1048608 | tf_op jit(solution)/shard_map/all_to_all | solution.py:33
  41.9 0.1 copy.10
  42.0 1.2 fusion
  43.2 10.6 %all_to_all.51 = f32[2,512,1024]{2,1,0:T(8,128)} all-to-all(f32[2,512,1024]{2,1,0:T(8,128)S(1)} %bitcast.30), channel_id=1, replica_groups=mesh['y'=8,'c'=2,'z'=8,'x'=4] {'c'}, dimensions={0} | all-to-all | bytes 8388608 | tf_op jit(solution)/shard_map/all_to_all | solution.py:38
  53.8 2.7 %reduce_sum.36 = bf16[512,1024]{1,0:T(8,128)(2,1)S(1)} reduce(f32[2,512,1024]{2,1,0:T(8,128)} %all_to_all.51, f32[]{:T(128)} %constant.1.clone.1), dimensions={0}, to_apply=%region_0.0 | reduce | flops 524288 | bytes 5242884 | tf_op jit(solution)/shard_map/reduce_sum | solution.py:39
  56.6 34.6 %all_to_all.52 = bf16[8,64,1024]{2,1,0:T(8,128)(2,1)S(1)} all-to-all(bf16[8,64,1024]{2,1,0:T(8,128)(2,1)S(1)} %bitcast.34), channel_id=1, replica_groups=mesh['y'=8,'c'=2,'z'=8,'x'=4] {'y'}, dimensions={0} | all-to-all | bytes 2097152 | tf_op jit(solution)/shard_map/all_to_all | solution.py:38
  91.1 0.0 copy-start.4
  91.1 0.2 convert_reduce_fusion.1
  91.4 0.8 broadcast_in_dim.17
  92.2 3.5 %all-to-all-start.3 = ((bf16[8,64,512]{2,1,0:T(8,128)(2,1)}), bf16[8,64,512]{2,1,0:T(8,128)(2,1)S(1)}, u32[]{:S(2)}, u32[]{:S(2)}) async-start(bf16[8,64,512]{2,1,0:T(8,128)(2,1)} %broadcast_in_dim.17), calls=%async_computation.3 | async-start | bytes 1048576 | tf_op jit(solution)/shard_map/all_to_all | solution.py:33
  95.7 0.0 copy-done.4
  95.7 15.9 %all-to-all-done.3 = bf16[8,64,512]{2,1,0:T(8,128)(2,1)S(1)} async-done(((bf16[8,64,512]{2,1,0:T(8,128)(2,1)}), bf16[8,64,512]{2,1,0:T(8,128)(2,1)S(1)}, u32[]{:S(2)}, u32[]{:S(2)}) %all-to-all-start.3) | async-done | bytes 524320 | tf_op jit(solution)/shard_map/all_to_all | solution.py:33
  111.6 0.1 broadcast_in_dim.19
  111.7 0.0 copy-start.5
  111.7 6.8 %all_to_all.53 = bf16[2,512,512]{2,1,0:T(8,128)(2,1)S(1)} all-to-all(bf16[2,512,512]{2,1,0:T(8,128)(2,1)S(1)} %broadcast_in_dim.19), channel_id=1, replica_groups=mesh['y'=8,'c'=2,'z'=8,'x'=4] {'c'}, dimensions={0} | all-to-all | bytes 2097152 | tf_op jit(solution)/shard_map/all_to_all | solution.py:33
  118.5 0.1 copy.11
  118.6 0.2 broadcast_in_dim.20
  118.8 0.0 copy-done.5
  118.8 0.7 convolution_convert_fusion
  119.5 31.6 %all_to_all.54 = bf16[8,128,512]{2,1,0:T(8,128)(2,1)S(1)} all-to-all(bf16[8,128,512]{2,1,0:T(8,128)(2,1)S(1)} %bitcast.40), channel_id=1, replica_groups=mesh['y'=8,'c'=2,'z'=8,'x'=4] {'z'}, dimensions={0} | all-to-all | bytes 2097152 | tf_op jit(solution)/shard_map/all_to_all | solution.py:38
  151.1 0.1 convert_reduce_fusion
  151.3 9.8 %all_to_all.55 = f32[4,32,512]{2,1,0:T(8,128)S(1)} all-to-all(f32[4,32,512]{2,1,0:T(8,128)S(1)} %bitcast.38), channel_id=1, replica_groups=mesh['y'=8,'c'=2,'z'=8,'x'=4] {'x'}, dimensions={0} | all-to-all | bytes 524288 | tf_op jit(solution)/shard_map/all_to_all | solution.py:38
  161.1 0.6 reduce_sum.39
  (4 shorter events, 0.1 us)
Async XLA Ops:
  0.0 15.7 %copy-start.2 = (s32[4,4]{1,0:T(4,128)S(1)}, s32[4,4]{1,0:T(4,128)}, u32[]{:S(2)}) copy-start(s32[4,4]{1,0:T(4,128)} %param.11) | copy-start | bytes 196
  0.0 15.7 %copy-start.3 = (s32[4,4]{1,0:T(4,128)S(1)}, s32[4,4]{1,0:T(4,128)}, u32[]{:S(2)}) copy-start(s32[4,4]{1,0:T(4,128)} %param.12) | copy-start | bytes 196
  0.0 16.1 %copy-start.1 = (bf16[512,512]{1,0:T(8,128)(2,1)S(1)}, bf16[512,512]{1,0:T(8,128)(2,1)}, u32[]{:S(2)}) copy-start(bf16[512,512]{1,0:T(8,128)(2,1)} %param.8) | copy-start | bytes 1572868
  0.0 16.2 %copy-start = (bf16[512,512]{1,0:T(8,128)(2,1)S(1)}, bf16[512,512]{1,0:T(8,128)(2,1)}, u32[]{:S(2)}) copy-start(bf16[512,512]{1,0:T(8,128)(2,1)} %param.9) | copy-start | bytes 1572868
  2.0 39.9 %all-to-all-start = ((bf16[32,32,512]{2,1,0:T(8,128)(2,1)}), bf16[32,32,512]{2,1,0:T(8,128)(2,1)S(1)}, u32[]{:S(2)}, u32[]{:S(2)}) async-start(bf16[32,32,512]{2,1,0:T(8,128)(2,1)} %broadcast_in_dim.16), calls=%async_computation | async-start | bytes 2097152 | tf_op jit(solution)/shard_map/all_to_all | solution.py:33
  91.1 4.6 %copy-start.4 = (s32[4,4]{1,0:T(4,128)S(1)}, s32[4,4]{1,0:T(4,128)}, u32[]{:S(2)}) copy-start(s32[4,4]{1,0:T(4,128)} %param.13) | copy-start | bytes 196
  92.2 19.4 %all-to-all-start.3 = ((bf16[8,64,512]{2,1,0:T(8,128)(2,1)}), bf16[8,64,512]{2,1,0:T(8,128)(2,1)S(1)}, u32[]{:S(2)}, u32[]{:S(2)}) async-start(bf16[8,64,512]{2,1,0:T(8,128)(2,1)} %broadcast_in_dim.17), calls=%async_computation.3 | async-start | bytes 1048576 | tf_op jit(solution)/shard_map/all_to_all | solution.py:33
  111.7 7.1 %copy-start.5 = (bf16[512,512]{1,0:T(8,128)(2,1)S(1)}, bf16[512,512]{1,0:T(8,128)(2,1)}, u32[]{:S(2)}) copy-start(bf16[512,512]{1,0:T(8,128)(2,1)} %param.10) | copy-start | bytes 1572868

commit v5 on v4

--- a/solution.py
+++ b/solution.py
@@ -51,13 +51,16 @@
     share = rows // (n_y * n_c)
     by_core = all_tokens.reshape(n_y, n_c, share, feats).transpose(1, 0, 2, 3).reshape(rows, feats)
     partial = jnp.dot(by_core, both_weights, preferred_element_type=jnp.float32)
-    summed = scatter_sum_a2a(scatter_sum_a2a(partial, "c"), "y", sent=jnp.bfloat16)
+    summed = scatter_sum_a2a(scatter_sum_a2a(partial, "c"), "y")
     hidden_share = swiglu(summed, hidden_cols)
     half = gather_a2a(hidden_share, "y")
     both = gather_a2a(half, "c")
     hidden = both.reshape(n_c, n_y, share, -1).transpose(1, 0, 2, 3).reshape(rows, -1)
     partial_out = jnp.dot(hidden, down_eff, preferred_element_type=jnp.float32)
-    partial_out = scatter_sum_a2a(scatter_sum_a2a(partial_out, "z", sent=jnp.bfloat16), "x")
+    n_z, n_x = lax.axis_size("z"), lax.axis_size("x")
+    out_share = rows // (n_z * n_x)
+    partial_out = partial_out.reshape(n_z, n_x, out_share, -1).transpose(1, 0, 2, 3).reshape(rows, -1)
+    partial_out = scatter_sum_a2a(scatter_sum_a2a(partial_out, "x"), "z", sent=jnp.bfloat16)
     return partial_out.astype(jnp.bfloat16)
 
 

time: 162 us -> 188 us (1.16)
  blocking collectives: 93.3 us -> 117 us
    all_to_all x4, blocking collectives: 86.6 us -> 110 us  [scatter_sum_a2a(): got = lax.all_to_all(x.astype(sent), axis, 0, 0, tiled=True)]
where the time goes in v5:
time: 188 us; the launch traced here: 187 us
  blocking collectives  117 us (62%)
  waiting for transfers between devices  41.5 us (22%)
  starting transfers between devices  17.2 us (9%)
  other arithmetic  5.63 us (3%)
  local copies, waits for them, and re-layouts  3.92 us (2%)
  matrix products  1.96 us (1%)
    all_to_all x4, blocking collectives, scatter_sum_a2a(): got = lax.all_to_all(x.astype(sent), axis, 0, 0, tiled=True)  110 us
    all_to_all x2, waiting for transfers between devices, gather_a2a(): return lax.all_to_all(copies, axis, 0, 0, tiled=True)  41.5 us
    all_to_all x2, starting transfers between devices, gather_a2a(): return lax.all_to_all(copies, axis, 0, 0, tiled=True)  17.2 us
    all_to_all x1, blocking collectives, gather_a2a(): return lax.all_to_all(copies, axis, 0, 0, tiled=True)  6.77 us
    reduce_sum x4, other arithmetic, scatter_sum_a2a(): got.reshape((n, x.shape[0] // n) + x.shape[1:]).astype(jnp.float32)  5.41 us
  transfers between devices with their start and end apart: 2, of which 2 were waited for; matrix products, arithmetic and copies ran while one was open for 0% of the time, Pallas kernels for 0%

profile of v5, /device:TPU:1, one launch (start us, length us, event | category | flops | bytes accessed | tf_op | source)
XLA Modules:
  0.0 186.9 jit_solution(14789272675534399004)
XLA Ops:
  0.0 0.0 copy-start.3
  0.0 0.0 copy-start.4
  0.0 0.0 copy-start.1
  0.0 0.0 copy-start
  0.0 2.0 %broadcast_in_dim.16 = bf16[32,32,512]{2,1,0:T(8,128)(2,1)} broadcast(bf16[32,512]{1,0:T(8,128)(2,1)} %param.7), dimensions={1,2} | broadcast | bytes 1081344 | tf_op jit(solution)/shard_map/broadcast_in_dim | solution.py:32
  2.0 13.7 %all-to-all-start = ((bf16[32,32,512]{2,1,0:T(8,128)(2,1)}), bf16[32,32,512]{2,1,0:T(8,128)(2,1)S(1)}, u32[]{:S(2)}, u32[]{:S(2)}) async-start(bf16[32,32,512]{2,1,0:T(8,128)(2,1)} %broadcast_in_dim.16), calls=%async_computation | async-start | bytes 2097152 | tf_op jit(solution)/shard_map/all_to_all | solution.py:33
  15.7 0.0 copy-done.3
  15.7 0.0 copy-done.4
  15.7 0.2 broadcast_in_dim.14
  15.9 0.2 broadcast_in_dim.15
  16.2 0.0 copy-done.1
  16.2 0.0 copy-done
  16.2 0.2 bitcast_multiply_fusion.1
  16.3 25.6 %all-to-all-done = bf16[32,32,512]{2,1,0:T(8,128)(2,1)S(1)} async-done(((bf16[32,32,512]{2,1,0:T(8,128)(2,1)}), bf16[32,32,512]{2,1,0:T(8,128)(2,1)S(1)}, u32[]{:S(2)}, u32[]{:S(2)}) %all-to-all-start) | async-done | bytes 1048608 | tf_op jit(solution)/shard_map/all_to_all | solution.py:33
  41.9 0.1 copy.13
  42.0 1.2 fusion
  43.2 10.6 %all_to_all.51 = f32[2,512,1024]{2,1,0:T(8,128)} all-to-all(f32[2,512,1024]{2,1,0:T(8,128)S(1)} %bitcast.39), channel_id=1, replica_groups=mesh['y'=8,'c'=2,'z'=8,'x'=4] {'c'}, dimensions={0} | all-to-all | bytes 8388608 | tf_op jit(solution)/shard_map/all_to_all | solution.py:38
  53.8 2.8 %reduce_sum.39 = f32[512,1024]{1,0:T(8,128)S(1)} reduce(f32[2,512,1024]{2,1,0:T(8,128)} %all_to_all.51, f32[]{:T(128)} %constant.4.clone.1), dimensions={0}, to_apply=%region_0.0 | reduce | flops 524288 | bytes 6291460 | tf_op jit(solution)/shard_map/reduce_sum | solution.py:39
  56.6 57.2 %all_to_all.52 = f32[8,64,1024]{2,1,0:T(8,128)} all-to-all(f32[8,64,1024]{2,1,0:T(8,128)S(1)} %bitcast.40), channel_id=1, replica_groups=mesh['y'=8,'c'=2,'z'=8,'x'=4] {'y'}, dimensions={0} | all-to-all | bytes 4194304 | tf_op jit(solution)/shard_map/all_to_all | solution.py:38
  113.8 0.0 copy-start.5
  113.8 1.7 reduce_sum.40
  115.6 0.8 broadcast_in_dim.17
  116.4 3.5 %all-to-all-start.3 = ((bf16[8,64,512]{2,1,0:T(8,128)(2,1)}), bf16[8,64,512]{2,1,0:T(8,128)(2,1)S(1)}, u32[]{:S(2)}, u32[]{:S(2)}) async-start(bf16[8,64,512]{2,1,0:T(8,128)(2,1)} %broadcast_in_dim.17), calls=%async_computation.3 | async-start | bytes 1048576 | tf_op jit(solution)/shard_map/all_to_all | solution.py:33
  119.9 0.0 copy-done.5
  119.9 15.9 %all-to-all-done.3 = bf16[8,64,512]{2,1,0:T(8,128)(2,1)S(1)} async-done(((bf16[8,64,512]{2,1,0:T(8,128)(2,1)}), bf16[8,64,512]{2,1,0:T(8,128)(2,1)S(1)}, u32[]{:S(2)}, u32[]{:S(2)}) %all-to-all-start.3) | async-done | bytes 524320 | tf_op jit(solution)/shard_map/all_to_all | solution.py:33
  135.8 0.1 broadcast_in_dim.19
  135.9 0.0 copy-start.2
  135.9 6.8 %all_to_all.53 = bf16[2,512,512]{2,1,0:T(8,128)(2,1)S(1)} all-to-all(bf16[2,512,512]{2,1,0:T(8,128)(2,1)S(1)} %broadcast_in_dim.19), channel_id=1, replica_groups=mesh['y'=8,'c'=2,'z'=8,'x'=4] {'c'}, dimensions={0} | all-to-all | bytes 2097152 | tf_op jit(solution)/shard_map/all_to_all | solution.py:33
  142.7 0.1 copy.14
  142.8 0.2 broadcast_in_dim.20
  143.0 0.0 copy-done.2
  143.0 0.7 convolution_bitcast_fusion
  143.7 0.3 copy.15
  144.0 29.6 %all_to_all.54 = f32[4,256,512]{2,1,0:T(8,128)S(1)} all-to-all(f32[4,256,512]{2,1,0:T(8,128)S(1)} %bitcast.41), channel_id=1, replica_groups=mesh['y'=8,'c'=2,'z'=8,'x'=4] {'x'}, dimensions={0} | all-to-all | bytes 4194304 | tf_op jit(solution)/shard_map/all_to_all | solution.py:38
  173.6 0.2 reduce_sum.41
  173.8 12.4 %all_to_all.55 = bf16[8,32,512]{2,1,0:T(8,128)(2,1)S(1)} all-to-all(bf16[8,32,512]{2,1,0:T(8,128)(2,1)S(1)} %bitcast.50), channel_id=1, replica_groups=mesh['y'=8,'c'=2,'z'=8,'x'=4] {'z'}, dimensions={0} | all-to-all | bytes 524288 | tf_op jit(solution)/shard_map/all_to_all | solution.py:38
  186.2 0.7 reduce_sum.42
  (4 shorter events, 0.1 us)
Async XLA Ops:
  0.0 15.7 %copy-start.3 = (s32[4,4]{1,0:T(4,128)S(1)}, s32[4,4]{1,0:T(4,128)}, u32[]{:S(2)}) copy-start(s32[4,4]{1,0:T(4,128)} %param.11) | copy-start | bytes 196
  0.0 15.7 %copy-start.4 = (s32[4,4]{1,0:T(4,128)S(1)}, s32[4,4]{1,0:T(4,128)}, u32[]{:S(2)}) copy-start(s32[4,4]{1,0:T(4,128)} %param.12) | copy-start | bytes 196
  0.0 16.1 %copy-start.1 = (bf16[512,512]{1,0:T(8,128)(2,1)S(1)}, bf16[512,512]{1,0:T(8,128)(2,1)}, u32[]{:S(2)}) copy-start(bf16[512,512]{1,0:T(8,128)(2,1)} %param.8) | copy-start | bytes 1572868
  0.0 16.2 %copy-start = (bf16[512,512]{1,0:T(8,128)(2,1)S(1)}, bf16[512,512]{1,0:T(8,128)(2,1)}, u32[]{:S(2)}) copy-start(bf16[512,512]{1,0:T(8,128)(2,1)} %param.9) | copy-start | bytes 1572868
  2.0 39.9 %all-to-all-start = ((bf16[32,32,512]{2,1,0:T(8,128)(2,1)}), bf16[32,32,512]{2,1,0:T(8,128)(2,1)S(1)}, u32[]{:S(2)}, u32[]{:S(2)}) async-start(bf16[32,32,512]{2,1,0:T(8,128)(2,1)} %broadcast_in_dim.16), calls=%async_computation | async-start | bytes 2097152 | tf_op jit(solution)/shard_map/all_to_all | solution.py:33
  113.8 6.1 %copy-start.5 = (s32[4,4]{1,0:T(4,128)S(1)}, s32[4,4]{1,0:T(4,128)}, u32[]{:S(2)}) copy-start(s32[4,4]{1,0:T(4,128)} %param.13) | copy-start | bytes 196
  116.4 19.4 %all-to-all-start.3 = ((bf16[8,64,512]{2,1,0:T(8,128)(2,1)}), bf16[8,64,512]{2,1,0:T(8,128)(2,1)S(1)}, u32[]{:S(2)}, u32[]{:S(2)}) async-start(bf16[8,64,512]{2,1,0:T(8,128)(2,1)} %broadcast_in_dim.17), calls=%async_computation.3 | async-start | bytes 1048576 | tf_op jit(solution)/shard_map/all_to_all | solution.py:33
  135.9 7.1 %copy-start.2 = (bf16[512,512]{1,0:T(8,128)(2,1)S(1)}, bf16[512,512]{1,0:T(8,128)(2,1)}, u32[]{:S(2)}) copy-start(bf16[512,512]{1,0:T(8,128)(2,1)} %param.10) | copy-start | bytes 1572868

commit v6 on v5

--- a/solution.py
+++ b/solution.py
@@ -16,6 +16,13 @@
     rows_blocks, cols_blocks = block_mask.shape
     spread = jnp.broadcast_to(block_mask[:, None, :, None], (rows_blocks, BLK, cols_blocks, BLK))
     return spread.reshape(rows_blocks * BLK, cols_blocks * BLK).astype(jnp.bfloat16)
+
+
+def scatter_sum_split(x, axis):
+    cut = x.shape[-1] // 2
+    first = lax.psum_scatter(x[..., :cut], axis, scatter_dimension=0, tiled=True)
+    second = scatter_sum_a2a(x[..., cut:], axis)
+    return jnp.concatenate([first, second], axis=-1)
 
 
 def swiglu(summed, hidden_cols):
@@ -51,7 +58,7 @@
     share = rows // (n_y * n_c)
     by_core = all_tokens.reshape(n_y, n_c, share, feats).transpose(1, 0, 2, 3).reshape(rows, feats)
     partial = jnp.dot(by_core, both_weights, preferred_element_type=jnp.float32)
-    summed = scatter_sum_a2a(scatter_sum_a2a(partial, "c"), "y")
+    summed = scatter_sum_split(scatter_sum_a2a(partial, "c"), "y")
     hidden_share = swiglu(summed, hidden_cols)
     half = gather_a2a(hidden_share, "y")
     both = gather_a2a(half, "c")
@@ -60,7 +67,7 @@
     n_z, n_x = lax.axis_size("z"), lax.axis_size("x")
     out_share = rows // (n_z * n_x)
     partial_out = partial_out.reshape(n_z, n_x, out_share, -1).transpose(1, 0, 2, 3).reshape(rows, -1)
-    partial_out = scatter_sum_a2a(scatter_sum_a2a(partial_out, "x"), "z", sent=jnp.bfloat16)
+    partial_out = scatter_sum_a2a(scatter_sum_split(partial_out, "x"), "z", sent=jnp.bfloat16)
     return partial_out.astype(jnp.bfloat16)
 
 

time: 188 us -> 193 us (1.027)
  blocking collectives: 117 us -> 99.4 us
  between operations: 0.19 us -> 13.6 us
  waiting for transfers between devices: 41.5 us -> 45.9 us
  starting transfers between devices: 17.2 us -> 19.5 us
  local copies, waits for them, and re-layouts: 3.92 us -> 6.19 us
    all_to_all x4, blocking collectives: 110 us -> 91.4 us  [scatter_sum_a2a(): got = lax.all_to_all(x.astype(sent), axis, 0, 0, tiled=True)]
    reduce_scatter x0 -> x2, waiting for transfers between devices: none -> 5.6 us  [scatter_sum_split(): lax.psum_scatter(x[..., :cut], axis, scatter_dimension=0, tiled=True)]
    slice x0 -> x2, local copies, waits for them, and re-layouts: none -> 2.3 us  [scatter_sum_split(): x[..., :cut]]
    all_to_all x2, starting transfers between devices: 17.2 us -> 19.5 us  [gather_a2a(): return lax.all_to_all(copies, axis, 0, 0, tiled=True)]
  transfers between devices with their start and end apart: 2 -> 4, of which waited for: 2 -> 4; matrix products, arithmetic and copies ran while one was open for 0% -> 0% of each run, Pallas kernels for 0% -> 0%
where the time goes in v6:
time: 193 us; the launch traced here: 192 us
  blocking collectives  99.4 us (52%)
  waiting for transfers between devices  45.9 us (24%)
  starting transfers between devices  19.5 us (10%)
  between operations  13.6 us (7%)
  local copies, waits for them, and re-layouts  6.19 us (3%)
  other arithmetic  5.68 us (3%)
  matrix products  1.97 us (1%)
    all_to_all x4, blocking collectives, scatter_sum_a2a(): got = lax.all_to_all(x.astype(sent), axis, 0, 0, tiled=True)  91.4 us
    all_to_all x2, waiting for transfers between devices, gather_a2a(): return lax.all_to_all(copies, axis, 0, 0, tiled=True)  40.2 us
    all_to_all x2, starting transfers between devices, gather_a2a(): return lax.all_to_all(copies, axis, 0, 0, tiled=True)  19.5 us
    all_to_all x1, blocking collectives, gather_a2a(): return lax.all_to_all(copies, axis, 0, 0, tiled=True)  7.99 us
    reduce_scatter x2, waiting for transfers between devices, scatter_sum_split(): lax.psum_scatter(x[..., :cut], axis, scatter_dimension=0, tiled=True)  5.6 us
  transfers between devices with their start and end apart: 4, of which 4 were waited for; matrix products, arithmetic and copies ran while one was open for 0% of the time, Pallas kernels for 0%

profile of v6, /device:TPU:1, one launch (start us, length us, event | category | flops | bytes accessed | tf_op | source)
XLA Modules:
  0.0 192.3 jit_solution(14645788823805523175)
XLA Ops:
  6.5 0.0 copy-start.3
  6.5 0.0 copy-start.4
  6.5 0.0 copy-start.1
  6.5 0.0 copy-start
  6.5 1.9 %broadcast_in_dim.16 = bf16[32,32,512]{2,1,0:T(8,128)(2,1)} broadcast(bf16[32,512]{1,0:T(8,128)(2,1)} %param.7), dimensions={1,2} | broadcast | bytes 1081344 | tf_op jit(solution)/shard_map/broadcast_in_dim | solution.py:39
  8.5 13.7 %all-to-all-start = ((bf16[32,32,512]{2,1,0:T(8,128)(2,1)}), bf16[32,32,512]{2,1,0:T(8,128)(2,1)S(1)}, u32[]{:S(2)}, u32[]{:S(2)}) async-start(bf16[32,32,512]{2,1,0:T(8,128)(2,1)} %broadcast_in_dim.16), calls=%async_computation | async-start | bytes 2097152 | tf_op jit(solution)/shard_map/all_to_all | solution.py:40
  22.2 0.0 reduce-scatter.3.cloned.1.call-start
  22.2 0.0 copy-done.3
  22.3 0.0 copy-done.4
  22.3 0.2 broadcast_in_dim.14
  22.5 0.2 broadcast_in_dim.15
  22.7 0.0 copy-done.1
  22.7 0.0 copy-done
  22.7 0.2 bitcast_multiply_fusion.1
  22.9 25.5 %all-to-all-done = bf16[32,32,512]{2,1,0:T(8,128)(2,1)S(1)} async-done(((bf16[32,32,512]{2,1,0:T(8,128)(2,1)}), bf16[32,32,512]{2,1,0:T(8,128)(2,1)S(1)}, u32[]{:S(2)}, u32[]{:S(2)}) %all-to-all-start) | async-done | bytes 1048608 | tf_op jit(solution)/shard_map/all_to_all | solution.py:40
  48.4 0.1 copy.10
  48.5 1.2 fusion
  49.7 10.6 %all_to_all.51 = f32[2,512,1024]{2,1,0:T(8,128)} all-to-all(f32[2,512,1024]{2,1,0:T(8,128)S(1)} %bitcast.41), channel_id=1, replica_groups=mesh['y'=8,'c'=2,'z'=8,'x'=4] {'c'}, dimensions={0} | all-to-all | bytes 8388608 | tf_op jit(solution)/shard_map/all_to_all | solution.py:45
  60.3 2.8 %reduce_sum.39 = f32[512,1024]{1,0:T(8,128)S(1)} reduce(f32[2,512,1024]{2,1,0:T(8,128)} %all_to_all.51, f32[]{:T(128)} %constant.4.clone.1), dimensions={0}, to_apply=%region_0.0 | reduce | flops 524288 | bytes 6291460 | tf_op jit(solution)/shard_map/reduce_sum | solution.py:46
  63.1 1.2 fusion.9
  64.3 0.0 reduce-scatter.3.cloned.1.call-update
  64.3 41.7 %all_to_all.52 = f32[8,64,512]{2,1,0:T(8,128)S(1)} all-to-all(f32[8,64,512]{2,1,0:T(8,128)S(1)} %bitcast.46), channel_id=1, replica_groups=mesh['y'=8,'c'=2,'z'=8,'x'=4] {'y'}, dimensions={0} | all-to-all | bytes 2097152 | tf_op jit(solution)/shard_map/all_to_all | solution.py:45
  106.0 0.0 copy-start.5
  106.0 0.1 reduce_sum.40
  106.1 3.0 %reduce-scatter.3.cloned.1.call-done = f32[64,512]{1,0:T(8,128)} async-done(((f32[512,512]{1,0:T(8,128)}), f32[64,512]{1,0:T(8,128)}) %reduce-scatter.3.cloned.1.call-update) | async-done | bytes 131088 | tf_op jit(solution)/shard_map/reduce_scatter | solution.py:23
  109.1 1.0 multiply_convert_fusion
  110.0 0.8 broadcast_in_dim.17
  110.8 5.8 %all-to-all-start.3 = ((bf16[8,64,512]{2,1,0:T(8,128)(2,1)}), bf16[8,64,512]{2,1,0:T(8,128)(2,1)S(1)}, u32[]{:S(2)}, u32[]{:S(2)}) async-start(bf16[8,64,512]{2,1,0:T(8,128)(2,1)} %broadcast_in_dim.17), calls=%async_computation.4 | async-start | bytes 1048576 | tf_op jit(solution)/shard_map/all_to_all | solution.py:40
  116.6 0.0 reduce-scatter.5.cloned.1.call-start
  116.6 0.0 copy-done.5
  116.6 14.7 %all-to-all-done.3 = bf16[8,64,512]{2,1,0:T(8,128)(2,1)S(1)} async-done(((bf16[8,64,512]{2,1,0:T(8,128)(2,1)}), bf16[8,64,512]{2,1,0:T(8,128)(2,1)S(1)}, u32[]{:S(2)}, u32[]{:S(2)}) %all-to-all-start.3) | async-done | bytes 524320 | tf_op jit(solution)/shard_map/all_to_all | solution.py:40
  131.4 0.1 broadcast_in_dim.19
  131.5 0.0 copy-start.2
  131.5 8.0 %all_to_all.53 = bf16[2,512,512]{2,1,0:T(8,128)(2,1)S(1)} all-to-all(bf16[2,512,512]{2,1,0:T(8,128)(2,1)S(1)} %broadcast_in_dim.19), channel_id=1, replica_groups=mesh['y'=8,'c'=2,'z'=8,'x'=4] {'c'}, dimensions={0} | all-to-all | bytes 2097152 | tf_op jit(solution)/shard_map/all_to_all | solution.py:40
  139.5 0.1 copy.11
  139.5 0.2 broadcast_in_dim.20
  139.8 0.0 copy-done.2
  139.8 0.7 convolution_bitcast_fusion
  140.5 0.3 copy.12
  140.8 1.1 fusion.8
  141.9 0.0 reduce-scatter.5.cloned.1.call-update
  141.9 26.4 %all_to_all.54 = f32[4,256,256]{2,1,0:T(8,128)S(1)} all-to-all(f32[4,256,256]{2,1,0:T(8,128)S(1)} %bitcast.47), channel_id=1, replica_groups=mesh['y'=8,'c'=2,'z'=8,'x'=4] {'x'}, dimensions={0} | all-to-all | bytes 2097152 | tf_op jit(solution)/shard_map/all_to_all | solution.py:45
  168.3 0.1 reduce_sum.41
  168.4 2.6 %reduce-scatter.5.cloned.1.call-done = f32[256,256]{1,0:T(8,128)} async-done(((f32[1024,256]{1,0:T(8,128)}), f32[256,256]{1,0:T(8,128)}) %reduce-scatter.5.cloned.1.call-update) | async-done | bytes 262160 | tf_op jit(solution)/shard_map/reduce_scatter | solution.py:23
  171.1 1.0 convert.9
  172.1 12.7 %all_to_all.55 = bf16[8,32,512]{2,1,0:T(8,128)(2,1)S(1)} all-to-all(bf16[8,32,512]{2,1,0:T(8,128)(2,1)S(1)} %pad_maximum_fusion), channel_id=1, replica_groups=mesh['y'=8,'c'=2,'z'=8,'x'=4] {'z'}, dimensions={0} | all-to-all | bytes 524288 | tf_op jit(solution)/shard_map/all_to_all | solution.py:45
  184.8 0.7 reduce_sum.42
  (4 shorter events, 0.0 us)
Async XLA Ops:
  6.5 15.7 %copy-start.3 = (s32[4,4]{1,0:T(4,128)S(1)}, s32[4,4]{1,0:T(4,128)}, u32[]{:S(2)}) copy-start(s32[4,4]{1,0:T(4,128)} %param.11) | copy-start | bytes 196
  6.5 15.7 %copy-start.4 = (s32[4,4]{1,0:T(4,128)S(1)}, s32[4,4]{1,0:T(4,128)}, u32[]{:S(2)}) copy-start(s32[4,4]{1,0:T(4,128)} %param.12) | copy-start | bytes 196
  6.5 16.2 %copy-start.1 = (bf16[512,512]{1,0:T(8,128)(2,1)S(1)}, bf16[512,512]{1,0:T(8,128)(2,1)}, u32[]{:S(2)}) copy-start(bf16[512,512]{1,0:T(8,128)(2,1)} %param.8) | copy-start | bytes 1572868
  6.5 16.2 %copy-start = (bf16[512,512]{1,0:T(8,128)(2,1)S(1)}, bf16[512,512]{1,0:T(8,128)(2,1)}, u32[]{:S(2)}) copy-start(bf16[512,512]{1,0:T(8,128)(2,1)} %param.9) | copy-start | bytes 1572868
  8.5 39.9 %all-to-all-start = ((bf16[32,32,512]{2,1,0:T(8,128)(2,1)}), bf16[32,32,512]{2,1,0:T(8,128)(2,1)S(1)}, u32[]{:S(2)}, u32[]{:S(2)}) async-start(bf16[32,32,512]{2,1,0:T(8,128)(2,1)} %broadcast_in_dim.16), calls=%async_computation | async-start | bytes 2097152 | tf_op jit(solution)/shard_map/all_to_all | solution.py:40
  22.2 86.9 %reduce-scatter.3.cloned.1.call-start = ((), (), s32[]{:S(2)}) async-start(), calls=%async_computation.9 | async-start | bytes 1179648 | tf_op jit(solution)/shard_map/reduce_scatter | solution.py:23
  106.0 10.6 %copy-start.5 = (s32[4,4]{1,0:T(4,128)S(1)}, s32[4,4]{1,0:T(4,128)}, u32[]{:S(2)}) copy-start(s32[4,4]{1,0:T(4,128)} %param.13) | copy-start | bytes 196
  110.8 20.6 %all-to-all-start.3 = ((bf16[8,64,512]{2,1,0:T(8,128)(2,1)}), bf16[8,64,512]{2,1,0:T(8,128)(2,1)S(1)}, u32[]{:S(2)}, u32[]{:S(2)}) async-start(bf16[8,64,512]{2,1,0:T(8,128)(2,1)} %broadcast_in_dim.17), calls=%async_computation.4 | async-start | bytes 1048576 | tf_op jit(solution)/shard_map/all_to_all | solution.py:40
  116.6 54.5 %reduce-scatter.5.cloned.1.call-start = ((), (), s32[]{:S(2)}) async-start(), calls=%async_computation.10 | async-start | bytes 1310720 | tf_op jit(solution)/shard_map/reduce_scatter | solution.py:23
  131.5 8.3 %copy-start.2 = (bf16[512,512]{1,0:T(8,128)(2,1)S(1)}, bf16[512,512]{1,0:T(8,128)(2,1)}, u32[]{:S(2)}) copy-start(bf16[512,512]{1,0:T(8,128)(2,1)} %param.10) | copy-start | bytes 1572868
Sparse Core Ops, SparseCore 0:
  64.4 44.5 reduce-scatter.2
  142.0 28.9 reduce-scatter.4

commit v7 on v6

--- a/solution.py
+++ b/solution.py
@@ -46,19 +46,17 @@
     return got.reshape((n, x.shape[0] // n) + x.shape[1:]).astype(jnp.float32).sum(axis=0)
 
 
-def on_device(tokens, gate_weight, up_weight, down_weight, gate_mask, up_mask, down_mask):
-    hidden_cols = gate_weight.shape[1]
-    both_weights = jnp.concatenate(
-        [gate_weight * widen(gate_mask), up_weight * widen(up_mask)], axis=1
-    )
-    down_eff = down_weight * widen(down_mask)
+N_CHUNK = 2
+
+
+def layer_chunk(tokens, both_weights, down_eff, hidden_cols):
     all_tokens = gather_a2a(tokens, COL)
     n_y, n_c = lax.axis_size("y"), lax.axis_size("c")
     rows, feats = all_tokens.shape
     share = rows // (n_y * n_c)
     by_core = all_tokens.reshape(n_y, n_c, share, feats).transpose(1, 0, 2, 3).reshape(rows, feats)
     partial = jnp.dot(by_core, both_weights, preferred_element_type=jnp.float32)
-    summed = scatter_sum_split(scatter_sum_a2a(partial, "c"), "y")
+    summed = lax.psum_scatter(scatter_sum_a2a(partial, "c"), "y", scatter_dimension=0, tiled=True)
     hidden_share = swiglu(summed, hidden_cols)
     half = gather_a2a(hidden_share, "y")
     both = gather_a2a(half, "c")
@@ -67,8 +65,21 @@
     n_z, n_x = lax.axis_size("z"), lax.axis_size("x")
     out_share = rows // (n_z * n_x)
     partial_out = partial_out.reshape(n_z, n_x, out_share, -1).transpose(1, 0, 2, 3).reshape(rows, -1)
-    partial_out = scatter_sum_a2a(scatter_sum_split(partial_out, "x"), "z", sent=jnp.bfloat16)
-    return partial_out.astype(jnp.bfloat16)
+    return scatter_sum_a2a(scatter_sum_a2a(partial_out, "x"), "z", sent=jnp.bfloat16)
+
+
+def on_device(tokens, gate_weight, up_weight, down_weight, gate_mask, up_mask, down_mask):
+    hidden_cols = gate_weight.shape[1]
+    both_weights = jnp.concatenate(
+        [gate_weight * widen(gate_mask), up_weight * widen(up_mask)], axis=1
+    )
+    down_eff = down_weight * widen(down_mask)
+    step = tokens.shape[0] // N_CHUNK
+    outs = [
+        layer_chunk(tokens[k * step:(k + 1) * step], both_weights, down_eff, hidden_cols)
+        for k in range(N_CHUNK)
+    ]
+    return jnp.concatenate(outs, axis=0).astype(jnp.bfloat16)
 
 
 def solution(mesh):

time: 193 us -> 228 us (1.18); the launches traced: 192 us -> 225 us
  waiting for transfers between devices: 45.9 us -> 104 us
  blocking collectives: 99.4 us -> 50.5 us
  starting transfers between devices: 19.5 us -> 40.3 us
  other arithmetic: 5.68 us -> 7.98 us
    all_to_all x4 -> x2, blocking collectives: 91.4 us -> 14.7 us  [scatter_sum_a2a(): got = lax.all_to_all(x.astype(sent), axis, 0, 0, tiled=True)]
    all_to_all x0 -> x4, waiting for transfers between devices: none -> 40.8 us  [scatter_sum_a2a(): got = lax.all_to_all(x.astype(sent), axis, 0, 0, tiled=True)]
    reduce_scatter x2, waiting for transfers between devices: 5.6 us -> 39.5 us  [layer_chunk(): lax.psum_scatter(scatter_sum_a2a(partial, 'c'), 'y', scatter_dimension=0,...]
    all_to_all x1 -> x3, blocking collectives: 7.99 us -> 35.9 us  [gather_a2a(): return lax.all_to_all(copies, axis, 0, 0, tiled=True)]
    all_to_all x0 -> x4, starting transfers between devices: none -> 18 us  [scatter_sum_a2a(): got = lax.all_to_all(x.astype(sent), axis, 0, 0, tiled=True)]
    all_to_all x2 -> x3, waiting for transfers between devices: 40.2 us -> 23.5 us  [gather_a2a(): return lax.all_to_all(copies, axis, 0, 0, tiled=True)]
    all_to_all x2 -> x3, starting transfers between devices: 19.5 us -> 22.3 us  [gather_a2a(): return lax.all_to_all(copies, axis, 0, 0, tiled=True)]
  transfers between devices with their start and end apart: 4 -> 9, of which waited for: 4 -> 8; matrix products, arithmetic and copies ran while one was open for 0% -> 5% of each run, Pallas kernels for 0% -> 0%
where the time goes in v7:
time: 228 us; the launch traced here: 225 us
  waiting for transfers between devices  104 us (46%)
  blocking collectives  50.5 us (22%)
  starting transfers between devices  40.3 us (18%)
  between operations  13.6 us (6%)
  other arithmetic  7.98 us (4%)
  local copies, waits for them, and re-layouts  6.23 us (3%)
  matrix products  2.32 us (1%)
    all_to_all x4, waiting for transfers between devices, scatter_sum_a2a(): got = lax.all_to_all(x.astype(sent), axis, 0, 0, tiled=True)  40.8 us
    reduce_scatter x2, waiting for transfers between devices, layer_chunk(): lax.psum_scatter(scatter_sum_a2a(partial, 'c'), 'y', scatter_dimension=0,...  39.5 us
    all_to_all x3, blocking collectives, gather_a2a(): return lax.all_to_all(copies, axis, 0, 0, tiled=True)  35.9 us
    all_to_all x3, waiting for transfers between devices, gather_a2a(): return lax.all_to_all(copies, axis, 0, 0, tiled=True)  23.5 us
    all_to_all x3, starting transfers between devices, gather_a2a(): return lax.all_to_all(copies, axis, 0, 0, tiled=True)  22.3 us
    all_to_all x4, starting transfers between devices, scatter_sum_a2a(): got = lax.all_to_all(x.astype(sent), axis, 0, 0, tiled=True)  18 us
    all_to_all x2, blocking collectives, scatter_sum_a2a(): got = lax.all_to_all(x.astype(sent), axis, 0, 0, tiled=True)  14.7 us
  transfers between devices with their start and end apart: 9, of which 8 were waited for; matrix products, arithmetic and copies ran while one was open for 5% of the time, Pallas kernels for 0%

profile of v7, /device:TPU:1, one launch (start us, length us, event | category | flops | bytes accessed | tf_op | source)
XLA Modules:
  0.0 224.9 jit_solution(12533135249457068737)
XLA Ops:
  6.5 0.8 fusion.9
  7.4 0.9 broadcast_in_dim.24
  8.2 13.7 %all-to-all-start = ((bf16[32,16,512]{2,1,0:T(8,128)(2,1)}), bf16[32,16,512]{2,1,0:T(8,128)(2,1)S(1)}, u32[]{:S(2)}, u32[]{:S(2)}) async-start(bf16[32,16,512]{2,1,0:T(8,128)(2,1)} %broadcast_in_dim.24), calls=%async_computation | async-start | bytes 1048576 | tf_op jit(solution)/shard_map/all_to_all | solution.py:40
  21.9 0.0 reduce-scatter.3.cloned.1.call-start
  22.0 0.7 convert_element_type.48
  22.7 0.7 convert_element_type.50
  23.4 0.2 broadcast_in_dim.22
  23.6 0.2 broadcast_in_dim.23
  23.8 0.2 bitcast_multiply_fusion.1
  23.9 14.3 %all-to-all-done = bf16[32,16,512]{2,1,0:T(8,128)(2,1)S(1)} async-done(((bf16[32,16,512]{2,1,0:T(8,128)(2,1)}), bf16[32,16,512]{2,1,0:T(8,128)(2,1)S(1)}, u32[]{:S(2)}, u32[]{:S(2)}) %all-to-all-start) | async-done | bytes 524320 | tf_op jit(solution)/shard_map/all_to_all | solution.py:40
  38.3 0.7 fusion
  39.0 7.5 %all_to_all.84 = f32[2,256,1024]{2,1,0:T(8,128)S(1)} all-to-all(f32[2,256,1024]{2,1,0:T(8,128)S(1)} %bitcast.59), channel_id=1, replica_groups=mesh['y'=8,'c'=2,'z'=8,'x'=4] {'c'}, dimensions={0} | all-to-all | bytes 4194304 | tf_op jit(solution)/shard_map/all_to_all | solution.py:45
  46.4 1.3 reduce_sum.54
  47.7 0.0 reduce-scatter.3.cloned.1.call-update
  47.7 0.0 reduce-scatter.5.cloned.1.call-start
  47.8 0.1 broadcast_in_dim.29
  47.8 20.8 %all_to_all.85 = bf16[32,16,512]{2,1,0:T(8,128)(2,1)S(1)} all-to-all(bf16[32,16,512]{2,1,0:T(8,128)(2,1)S(1)} %broadcast_in_dim.29), channel_id=1, replica_groups=mesh['y'=8,'c'=2,'z'=8,'x'=4] {'z','x'}, dimensions={0} | all-to-all | bytes 1048576 | tf_op jit(solution)/shard_map/all_to_all | solution.py:40
  68.7 0.7 fusion.1
  69.4 7.2 %all_to_all.86 = f32[2,256,1024]{2,1,0:T(8,128)S(1)} all-to-all(f32[2,256,1024]{2,1,0:T(8,128)S(1)} %bitcast.58), channel_id=1, replica_groups=mesh['y'=8,'c'=2,'z'=8,'x'=4] {'c'}, dimensions={0} | all-to-all | bytes 4194304 | tf_op jit(solution)/shard_map/all_to_all | solution.py:45
  76.6 1.2 reduce_sum.57
  77.8 0.0 reduce-scatter.5.cloned.1.call-update
  77.8 3.2 %reduce-scatter.3.cloned.1.call-done = f32[32,1024]{1,0:T(8,128)} async-done(((f32[256,1024]{1,0:T(8,128)}), f32[32,1024]{1,0:T(8,128)}) %reduce-scatter.3.cloned.1.call-update) | async-done | bytes 131088 | tf_op jit(solution)/shard_map/reduce_scatter | solution.py:59
  81.0 0.9 fusion.6
  81.9 0.7 broadcast_in_dim.25
  82.6 4.3 %all-to-all-start.2 = ((bf16[8,32,512]{2,1,0:T(8,128)(2,1)}), bf16[8,32,512]{2,1,0:T(8,128)(2,1)S(1)}, u32[]{:S(2)}, u32[]{:S(2)}) async-start(bf16[8,32,512]{2,1,0:T(8,128)(2,1)} %broadcast_in_dim.25), calls=%async_computation.3 | async-start | bytes 524288 | tf_op jit(solution)/shard_map/all_to_all | solution.py:40
  87.0 36.3 %reduce-scatter.5.cloned.1.call-done = f32[32,1024]{1,0:T(8,128)} async-done(((f32[256,1024]{1,0:T(8,128)}), f32[32,1024]{1,0:T(8,128)}) %reduce-scatter.5.cloned.1.call-update) | async-done | bytes 131088 | tf_op jit(solution)/shard_map/reduce_scatter | solution.py:59
  123.3 0.9 fusion.5
  124.3 9.6 %all_to_all.87 = bf16[2,256,512]{2,1,0:T(8,128)(2,1)S(1)} all-to-all(bf16[2,256,512]{2,1,0:T(8,128)(2,1)S(1)} %broadcast_in_dim.27), channel_id=1, replica_groups=mesh['y'=8,'c'=2,'z'=8,'x'=4] {'c'}, dimensions={0} | all-to-all | bytes 1048576 | tf_op jit(solution)/shard_map/all_to_all | solution.py:40
  133.8 0.7 broadcast_in_dim.30
  134.6 4.2 %all-to-all-start.8 = ((bf16[8,32,512]{2,1,0:T(8,128)(2,1)}), bf16[8,32,512]{2,1,0:T(8,128)(2,1)S(1)}, u32[]{:S(2)}, u32[]{:S(2)}) async-start(bf16[8,32,512]{2,1,0:T(8,128)(2,1)} %broadcast_in_dim.30), calls=%async_computation.10 | async-start | bytes 524288 | tf_op jit(solution)/shard_map/all_to_all | solution.py:40
  138.9 0.2 broadcast_in_dim.28
  139.1 0.5 convolution_bitcast_fusion.1
  139.5 1.1 copy.20
  140.7 9.2 %all-to-all-done.8 = bf16[8,32,512]{2,1,0:T(8,128)(2,1)S(1)} async-done(((bf16[8,32,512]{2,1,0:T(8,128)(2,1)}), bf16[8,32,512]{2,1,0:T(8,128)(2,1)S(1)}, u32[]{:S(2)}, u32[]{:S(2)}) %all-to-all-start.8) | async-done | bytes 262176 | tf_op jit(solution)/shard_map/all_to_all | solution.py:40
  149.9 5.5 %all_to_all.88 = bf16[2,256,512]{2,1,0:T(8,128)(2,1)S(1)} all-to-all(bf16[2,256,512]{2,1,0:T(8,128)(2,1)S(1)} %broadcast_in_dim.32), channel_id=1, replica_groups=mesh['y'=8,'c'=2,'z'=8,'x'=4] {'c'}, dimensions={0} | all-to-all | bytes 1048576 | tf_op jit(solution)/shard_map/all_to_all | solution.py:40
  155.5 4.0 %all-to-all-start.4 = ((f32[4,128,512]{2,1,0:T(8,128)}), f32[4,128,512]{2,1,0:T(8,128)S(1)}, u32[]{:S(2)}, u32[]{:S(2)}) async-start(f32[4,128,512]{2,1,0:T(8,128)} %bitcast.12), calls=%async_computation.5 | async-start | bytes 2097152 | tf_op jit(solution)/shard_map/all_to_all | solution.py:45
  159.5 0.5 convolution_bitcast_fusion
  159.9 1.1 copy.23
  161.0 13.0 %all-to-all-done.4 = f32[4,128,512]{2,1,0:T(8,128)S(1)} async-done(((f32[4,128,512]{2,1,0:T(8,128)}), f32[4,128,512]{2,1,0:T(8,128)S(1)}, u32[]{:S(2)}, u32[]{:S(2)}) %all-to-all-start.4) | async-done | bytes 1048608 | tf_op jit(solution)/shard_map/all_to_all | solution.py:45
  174.0 3.5 %all-to-all-start.10 = ((f32[4,128,512]{2,1,0:T(8,128)}), f32[4,128,512]{2,1,0:T(8,128)S(1)}, u32[]{:S(2)}, u32[]{:S(2)}) async-start(f32[4,128,512]{2,1,0:T(8,128)} %bitcast.62), calls=%async_computation.12 | async-start | bytes 2097152 | tf_op jit(solution)/shard_map/all_to_all | solution.py:45
  177.5 0.8 reduce_sum.55
  178.2 12.9 %all-to-all-done.10 = f32[4,128,512]{2,1,0:T(8,128)S(1)} async-done(((f32[4,128,512]{2,1,0:T(8,128)}), f32[4,128,512]{2,1,0:T(8,128)S(1)}, u32[]{:S(2)}, u32[]{:S(2)}) %all-to-all-start.10) | async-done | bytes 1048608 | tf_op jit(solution)/shard_map/all_to_all | solution.py:45
  191.1 7.1 %all-to-all-start.5 = ((bf16[8,16,512]{2,1,0:T(8,128)(2,1)}), bf16[8,16,512]{2,1,0:T(8,128)(2,1)S(1)}, u32[]{:S(2)}, u32[]{:S(2)}) async-start(bf16[8,16,512]{2,1,0:T(8,128)(2,1)} %bitcast.13), calls=%async_computation.6 | async-start | bytes 262144 | tf_op jit(solution)/shard_map/all_to_all | solution.py:45
  198.2 0.7 reduce_sum.58
  199.0 7.2 %all-to-all-done.5 = bf16[8,16,512]{2,1,0:T(8,128)(2,1)S(1)} async-done(((bf16[8,16,512]{2,1,0:T(8,128)(2,1)}), bf16[8,16,512]{2,1,0:T(8,128)(2,1)S(1)}, u32[]{:S(2)}, u32[]{:S(2)}) %all-to-all-start.5) | async-done | bytes 131104 | tf_op jit(solution)/shard_map/all_to_all | solution.py:45
  206.2 3.4 %all-to-all-start.11 = ((bf16[8,16,512]{2,1,0:T(8,128)(2,1)}), bf16[8,16,512]{2,1,0:T(8,128)(2,1)S(1)}, u32[]{:S(2)}, u32[]{:S(2)}) async-start(bf16[8,16,512]{2,1,0:T(8,128)(2,1)} %bitcast.26), calls=%async_computation.13 | async-start | bytes 262144 | tf_op jit(solution)/shard_map/all_to_all | solution.py:45
  209.6 7.8 %all-to-all-done.11 = bf16[8,16,512]{2,1,0:T(8,128)(2,1)S(1)} async-done(((bf16[8,16,512]{2,1,0:T(8,128)(2,1)}), bf16[8,16,512]{2,1,0:T(8,128)(2,1)S(1)}, u32[]{:S(2)}, u32[]{:S(2)}) %all-to-all-start.11) | async-done | bytes 131104 | tf_op jit(solution)/shard_map/all_to_all | solution.py:45
  217.4 0.6 pad_maximum_fusion.3
  (18 shorter events, 0.3 us)
Async XLA Ops:
  6.5 17.2 %copy-start.2 = (bf16[512,512]{1,0:T(8,128)(2,1)S(1)}, bf16[512,512]{1,0:T(8,128)(2,1)}, u32[]{:S(2)}) copy-start(bf16[512,512]{1,0:T(8,128)(2,1)} %param.8) | copy-start | bytes 1572868
  6.5 17.2 %copy-start.1 = (bf16[512,512]{1,0:T(8,128)(2,1)S(1)}, bf16[512,512]{1,0:T(8,128)(2,1)}, u32[]{:S(2)}) copy-start(bf16[512,512]{1,0:T(8,128)(2,1)} %param.9) | copy-start | bytes 1572868
  8.2 30.0 %all-to-all-start = ((bf16[32,16,512]{2,1,0:T(8,128)(2,1)}), bf16[32,16,512]{2,1,0:T(8,128)(2,1)S(1)}, u32[]{:S(2)}, u32[]{:S(2)}) async-start(bf16[32,16,512]{2,1,0:T(8,128)(2,1)} %broadcast_in_dim.24), calls=%async_computation | async-start | bytes 1048576 | tf_op jit(solution)/shard_map/all_to_all | solution.py:40
  21.9 59.1 %reduce-scatter.3.cloned.1.call-start = ((), (), s32[]{:S(2)}) async-start(), calls=%async_computation.14 | async-start | bytes 1179648 | tf_op jit(solution)/shard_map/reduce_scatter | solution.py:59
  47.7 75.6 %reduce-scatter.5.cloned.1.call-start = ((), (), s32[]{:S(2)}) async-start(), calls=%async_computation.15 | async-start | bytes 1179648 | tf_op jit(solution)/shard_map/reduce_scatter | solution.py:59
  77.8 61.0 %copy-start.3 = (s32[4,4]{1,0:T(4,128)S(1)}, s32[4,4]{1,0:T(4,128)}, u32[]{:S(2)}) copy-start(s32[4,4]{1,0:T(4,128)} %param.13) | copy-start | bytes 196
  82.6 41.6 %all-to-all-start.2 = ((bf16[8,32,512]{2,1,0:T(8,128)(2,1)}), bf16[8,32,512]{2,1,0:T(8,128)(2,1)S(1)}, u32[]{:S(2)}, u32[]{:S(2)}) async-start(bf16[8,32,512]{2,1,0:T(8,128)(2,1)} %broadcast_in_dim.25), calls=%async_computation.3 | async-start | bytes 524288 | tf_op jit(solution)/shard_map/all_to_all | solution.py:40
  124.2 14.9 %copy-start = (bf16[512,512]{1,0:T(8,128)(2,1)S(1)}, bf16[512,512]{1,0:T(8,128)(2,1)}, u32[]{:S(2)}) copy-start(bf16[512,512]{1,0:T(8,128)(2,1)} %param.10) | copy-start | bytes 1572868
  134.6 15.4 %all-to-all-start.8 = ((bf16[8,32,512]{2,1,0:T(8,128)(2,1)}), bf16[8,32,512]{2,1,0:T(8,128)(2,1)S(1)}, u32[]{:S(2)}, u32[]{:S(2)}) async-start(bf16[8,32,512]{2,1,0:T(8,128)(2,1)} %broadcast_in_dim.30), calls=%async_computation.10 | async-start | bytes 524288 | tf_op jit(solution)/shard_map/all_to_all | solution.py:40
  155.5 18.5 %all-to-all-start.4 = ((f32[4,128,512]{2,1,0:T(8,128)}), f32[4,128,512]{2,1,0:T(8,128)S(1)}, u32[]{:S(2)}, u32[]{:S(2)}) async-start(f32[4,128,512]{2,1,0:T(8,128)} %bitcast.12), calls=%async_computation.5 | async-start | bytes 2097152 | tf_op jit(solution)/shard_map/all_to_all | solution.py:45
  174.0 17.2 %all-to-all-start.10 = ((f32[4,128,512]{2,1,0:T(8,128)}), f32[4,128,512]{2,1,0:T(8,128)S(1)}, u32[]{:S(2)}, u32[]{:S(2)}) async-start(f32[4,128,512]{2,1,0:T(8,128)} %bitcast.62), calls=%async_computation.12 | async-start | bytes 2097152 | tf_op jit(solution)/shard_map/all_to_all | solution.py:45
  191.1 15.0 %all-to-all-start.5 = ((bf16[8,16,512]{2,1,0:T(8,128)(2,1)}), bf16[8,16,512]{2,1,0:T(8,128)(2,1)S(1)}, u32[]{:S(2)}, u32[]{:S(2)}) async-start(bf16[8,16,512]{2,1,0:T(8,128)(2,1)} %bitcast.13), calls=%async_computation.6 | async-start | bytes 262144 | tf_op jit(solution)/shard_map/all_to_all | solution.py:45
  206.2 11.2 %all-to-all-start.11 = ((bf16[8,16,512]{2,1,0:T(8,128)(2,1)}), bf16[8,16,512]{2,1,0:T(8,128)(2,1)S(1)}, u32[]{:S(2)}, u32[]{:S(2)}) async-start(bf16[8,16,512]{2,1,0:T(8,128)(2,1)} %bitcast.26), calls=%async_computation.13 | async-start | bytes 262144 | tf_op jit(solution)/shard_map/all_to_all | solution.py:45
Sparse Core Ops, SparseCore 0:
  47.9 33.0 reduce-scatter.2
  83.8 39.4 reduce-scatter.4

commit v8 on v4

--- a/solution.py
+++ b/solution.py
@@ -51,13 +51,13 @@
     share = rows // (n_y * n_c)
     by_core = all_tokens.reshape(n_y, n_c, share, feats).transpose(1, 0, 2, 3).reshape(rows, feats)
     partial = jnp.dot(by_core, both_weights, preferred_element_type=jnp.float32)
-    summed = scatter_sum_a2a(scatter_sum_a2a(partial, "c"), "y", sent=jnp.bfloat16)
+    summed = scatter_sum_a2a(scatter_sum_a2a(partial, "c"), "y")
     hidden_share = swiglu(summed, hidden_cols)
     half = gather_a2a(hidden_share, "y")
     both = gather_a2a(half, "c")
     hidden = both.reshape(n_c, n_y, share, -1).transpose(1, 0, 2, 3).reshape(rows, -1)
     partial_out = jnp.dot(hidden, down_eff, preferred_element_type=jnp.float32)
-    partial_out = scatter_sum_a2a(scatter_sum_a2a(partial_out, "z", sent=jnp.bfloat16), "x")
+    partial_out = scatter_sum_a2a(partial_out, COL, sent=jnp.bfloat16)
     return partial_out.astype(jnp.bfloat16)
 
 

time: 162 us -> 178 us (1.099)
  blocking collectives: 93.3 us -> 106 us
    all_to_all x4 -> x3, blocking collectives: 86.6 us -> 99.2 us  [scatter_sum_a2a(): got = lax.all_to_all(x.astype(sent), axis, 0, 0, tiled=True)]
    reduce_sum x4 -> x3, other arithmetic: 3.69 us -> 5.3 us  [scatter_sum_a2a(): got.reshape((n, x.shape[0] // n) + x.shape[1:]).astype(jnp.float32)]
where the time goes in v8:
time: 178 us; the launch traced here: 176 us
  blocking collectives  106 us (60%)
  waiting for transfers between devices  41.5 us (23%)
  starting transfers between devices  17.2 us (10%)
  other arithmetic  5.51 us (3%)
  local copies, waits for them, and re-layouts  3.64 us (2%)
  matrix products  1.96 us (1%)
    all_to_all x3, blocking collectives, scatter_sum_a2a(): got = lax.all_to_all(x.astype(sent), axis, 0, 0, tiled=True)  99.2 us
    all_to_all x2, waiting for transfers between devices, gather_a2a(): return lax.all_to_all(copies, axis, 0, 0, tiled=True)  41.5 us
    all_to_all x2, starting transfers between devices, gather_a2a(): return lax.all_to_all(copies, axis, 0, 0, tiled=True)  17.2 us
    all_to_all x1, blocking collectives, gather_a2a(): return lax.all_to_all(copies, axis, 0, 0, tiled=True)  6.77 us
    reduce_sum x3, other arithmetic, scatter_sum_a2a(): got.reshape((n, x.shape[0] // n) + x.shape[1:]).astype(jnp.float32)  5.3 us
  transfers between devices with their start and end apart: 2, of which 2 were waited for; matrix products, arithmetic and copies ran while one was open for 0% of the time, Pallas kernels for 0%

profile of v8, /device:TPU:1, one launch (start us, length us, event | category | flops | bytes accessed | tf_op | source)
XLA Modules:
  0.0 175.9 jit_solution(3131945644512662683)
XLA Ops:
  0.0 0.0 copy-start.2
  0.0 0.0 copy-start.3
  0.0 0.0 copy-start.1
  0.0 0.0 copy-start
  0.0 1.9 %broadcast_in_dim.16 = bf16[32,32,512]{2,1,0:T(8,128)(2,1)} broadcast(bf16[32,512]{1,0:T(8,128)(2,1)} %param.7), dimensions={1,2} | broadcast | bytes 1081344 | tf_op jit(solution)/shard_map/broadcast_in_dim | solution.py:32
  2.0 13.7 %all-to-all-start = ((bf16[32,32,512]{2,1,0:T(8,128)(2,1)}), bf16[32,32,512]{2,1,0:T(8,128)(2,1)S(1)}, u32[]{:S(2)}, u32[]{:S(2)}) async-start(bf16[32,32,512]{2,1,0:T(8,128)(2,1)} %broadcast_in_dim.16), calls=%async_computation | async-start | bytes 2097152 | tf_op jit(solution)/shard_map/all_to_all | solution.py:33
  15.7 0.0 copy-done.2
  15.7 0.0 copy-done.3
  15.7 0.2 broadcast_in_dim.14
  15.9 0.2 broadcast_in_dim.15
  16.1 0.0 copy-done.1
  16.1 0.0 copy-done
  16.2 0.2 bitcast_multiply_fusion.2
  16.3 25.6 %all-to-all-done = bf16[32,32,512]{2,1,0:T(8,128)(2,1)S(1)} async-done(((bf16[32,32,512]{2,1,0:T(8,128)(2,1)}), bf16[32,32,512]{2,1,0:T(8,128)(2,1)S(1)}, u32[]{:S(2)}, u32[]{:S(2)}) %all-to-all-start) | async-done | bytes 1048608 | tf_op jit(solution)/shard_map/all_to_all | solution.py:33
  41.9 0.1 copy.10
  41.9 1.2 fusion
  43.2 10.6 %all_to_all.45 = f32[2,512,1024]{2,1,0:T(8,128)} all-to-all(f32[2,512,1024]{2,1,0:T(8,128)S(1)} %bitcast.29), channel_id=1, replica_groups=mesh['y'=8,'c'=2,'z'=8,'x'=4] {'c'}, dimensions={0} | all-to-all | bytes 8388608 | tf_op jit(solution)/shard_map/all_to_all | solution.py:38
  53.8 2.8 %reduce_sum.30 = f32[512,1024]{1,0:T(8,128)S(1)} reduce(f32[2,512,1024]{2,1,0:T(8,128)} %all_to_all.45, f32[]{:T(128)} %constant.4.clone.1), dimensions={0}, to_apply=%region_0.0 | reduce | flops 524288 | bytes 6291460 | tf_op jit(solution)/shard_map/reduce_sum | solution.py:39
  56.6 57.1 %all_to_all.46 = f32[8,64,1024]{2,1,0:T(8,128)} all-to-all(f32[8,64,1024]{2,1,0:T(8,128)S(1)} %bitcast.30), channel_id=1, replica_groups=mesh['y'=8,'c'=2,'z'=8,'x'=4] {'y'}, dimensions={0} | all-to-all | bytes 4194304 | tf_op jit(solution)/shard_map/all_to_all | solution.py:38
  113.7 0.0 copy-start.4
  113.7 1.7 reduce_sum.31
  115.5 0.8 broadcast_in_dim.17
  116.4 3.5 %all-to-all-start.3 = ((bf16[8,64,512]{2,1,0:T(8,128)(2,1)}), bf16[8,64,512]{2,1,0:T(8,128)(2,1)S(1)}, u32[]{:S(2)}, u32[]{:S(2)}) async-start(bf16[8,64,512]{2,1,0:T(8,128)(2,1)} %broadcast_in_dim.17), calls=%async_computation.3 | async-start | bytes 1048576 | tf_op jit(solution)/shard_map/all_to_all | solution.py:33
  119.9 0.0 copy-done.4
  119.9 15.9 %all-to-all-done.3 = bf16[8,64,512]{2,1,0:T(8,128)(2,1)S(1)} async-done(((bf16[8,64,512]{2,1,0:T(8,128)(2,1)}), bf16[8,64,512]{2,1,0:T(8,128)(2,1)S(1)}, u32[]{:S(2)}, u32[]{:S(2)}) %all-to-all-start.3) | async-done | bytes 524320 | tf_op jit(solution)/shard_map/all_to_all | solution.py:33
  135.8 0.1 broadcast_in_dim.19
  135.9 0.0 copy-start.5
  135.9 6.8 %all_to_all.47 = bf16[2,512,512]{2,1,0:T(8,128)(2,1)S(1)} all-to-all(bf16[2,512,512]{2,1,0:T(8,128)(2,1)S(1)} %broadcast_in_dim.19), channel_id=1, replica_groups=mesh['y'=8,'c'=2,'z'=8,'x'=4] {'c'}, dimensions={0} | all-to-all | bytes 2097152 | tf_op jit(solution)/shard_map/all_to_all | solution.py:33
  142.7 0.1 copy.11
  142.7 0.2 broadcast_in_dim.20
  143.0 0.0 copy-done.5
  143.0 0.7 convolution_convert_fusion
  143.7 31.5 %all_to_all.48 = bf16[32,32,512]{2,1,0:T(8,128)(2,1)S(1)} all-to-all(bf16[32,32,512]{2,1,0:T(8,128)(2,1)S(1)} %bitcast.38), channel_id=1, replica_groups=mesh['y'=8,'c'=2,'z'=8,'x'=4] {'z','x'}, dimensions={0} | all-to-all | bytes 2097152 | tf_op jit(solution)/shard_map/all_to_all | solution.py:38
  175.2 0.8 reduce_sum.32
  (4 shorter events, 0.1 us)
Async XLA Ops:
  0.0 15.7 %copy-start.2 = (s32[4,4]{1,0:T(4,128)S(1)}, s32[4,4]{1,0:T(4,128)}, u32[]{:S(2)}) copy-start(s32[4,4]{1,0:T(4,128)} %param.11) | copy-start | bytes 196
  0.0 15.7 %copy-start.3 = (s32[4,4]{1,0:T(4,128)S(1)}, s32[4,4]{1,0:T(4,128)}, u32[]{:S(2)}) copy-start(s32[4,4]{1,0:T(4,128)} %param.12) | copy-start | bytes 196
  0.0 16.1 %copy-start.1 = (bf16[512,512]{1,0:T(8,128)(2,1)S(1)}, bf16[512,512]{1,0:T(8,128)(2,1)}, u32[]{:S(2)}) copy-start(bf16[512,512]{1,0:T(8,128)(2,1)} %param.8) | copy-start | bytes 1572868
  0.0 16.1 %copy-start = (bf16[512,512]{1,0:T(8,128)(2,1)S(1)}, bf16[512,512]{1,0:T(8,128)(2,1)}, u32[]{:S(2)}) copy-start(bf16[512,512]{1,0:T(8,128)(2,1)} %param.9) | copy-start | bytes 1572868
  2.0 39.9 %all-to-all-start = ((bf16[32,32,512]{2,1,0:T(8,128)(2,1)}), bf16[32,32,512]{2,1,0:T(8,128)(2,1)S(1)}, u32[]{:S(2)}, u32[]{:S(2)}) async-start(bf16[32,32,512]{2,1,0:T(8,128)(2,1)} %broadcast_in_dim.16), calls=%async_computation | async-start | bytes 2097152 | tf_op jit(solution)/shard_map/all_to_all | solution.py:33
  113.7 6.1 %copy-start.4 = (s32[4,4]{1,0:T(4,128)S(1)}, s32[4,4]{1,0:T(4,128)}, u32[]{:S(2)}) copy-start(s32[4,4]{1,0:T(4,128)} %param.13) | copy-start | bytes 196
  116.4 19.4 %all-to-all-start.3 = ((bf16[8,64,512]{2,1,0:T(8,128)(2,1)}), bf16[8,64,512]{2,1,0:T(8,128)(2,1)S(1)}, u32[]{:S(2)}, u32[]{:S(2)}) async-start(bf16[8,64,512]{2,1,0:T(8,128)(2,1)} %broadcast_in_dim.17), calls=%async_computation.3 | async-start | bytes 1048576 | tf_op jit(solution)/shard_map/all_to_all | solution.py:33
  135.9 7.1 %copy-start.5 = (bf16[512,512]{1,0:T(8,128)(2,1)S(1)}, bf16[512,512]{1,0:T(8,128)(2,1)}, u32[]{:S(2)}) copy-start(bf16[512,512]{1,0:T(8,128)(2,1)} %param.10) | copy-start | bytes 1572868

commit v9 on v8

--- a/solution.py
+++ b/solution.py
@@ -16,6 +16,28 @@
     rows_blocks, cols_blocks = block_mask.shape
     spread = jnp.broadcast_to(block_mask[:, None, :, None], (rows_blocks, BLK, cols_blocks, BLK))
     return spread.reshape(rows_blocks * BLK, cols_blocks * BLK).astype(jnp.bfloat16)
+
+
+def shift(x, axis, step):
+    n = lax.axis_size(axis)
+    return lax.ppermute(x, axis, [(s, (s + step) % n) for s in range(n)])
+
+
+def scatter_sum_chains(x, axis):
+    n = lax.axis_size(axis)
+    i = lax.axis_index(axis)
+    blocks = x.reshape((n, x.shape[0] // n) + x.shape[1:])
+    own = lambda k: lax.dynamic_index_in_dim(blocks, k % n, axis=0, keepdims=False)
+    up_steps, down_steps = (n - 1) // 2, n // 2
+    acc_up = own(i + up_steps)
+    for s in range(1, up_steps + 1):
+        got = shift(acc_up, axis, 1)
+        acc_up = got + own(i + up_steps - s) if s < up_steps else got
+    acc_down = own(i - down_steps)
+    for s in range(1, down_steps + 1):
+        got = shift(acc_down, axis, -1)
+        acc_down = got + own(i - down_steps + s) if s < down_steps else got
+    return acc_up + acc_down + own(i)
 
 
 def swiglu(summed, hidden_cols):
@@ -51,7 +73,7 @@
     share = rows // (n_y * n_c)
     by_core = all_tokens.reshape(n_y, n_c, share, feats).transpose(1, 0, 2, 3).reshape(rows, feats)
     partial = jnp.dot(by_core, both_weights, preferred_element_type=jnp.float32)
-    summed = scatter_sum_a2a(scatter_sum_a2a(partial, "c"), "y")
+    summed = scatter_sum_chains(scatter_sum_a2a(partial, "c"), "y")
     hidden_share = swiglu(summed, hidden_cols)
     half = gather_a2a(hidden_share, "y")
     both = gather_a2a(half, "c")

time: 178 us -> 164 us (0.921)
  blocking collectives: 106 us -> 52.9 us
  starting transfers between devices: 17.2 us -> 44.3 us
  waiting for transfers between devices: 41.5 us -> 54.9 us
    all_to_all x3 -> x2, blocking collectives: 99.2 us -> 42.1 us  [scatter_sum_a2a(): got = lax.all_to_all(x.astype(sent), axis, 0, 0, tiled=True)]
    ppermute x0 -> x7, starting transfers between devices: none -> 26.1 us  [shift(): return lax.ppermute(x, axis, [(s, (s + step) % n) for s in range(n)])]
    ppermute x0 -> x7, waiting for transfers between devices: none -> 17.3 us  [shift(): return lax.ppermute(x, axis, [(s, (s + step) % n) for s in range(n)])]
    all_to_all x1, blocking collectives: 6.77 us -> 10.8 us  [gather_a2a(): return lax.all_to_all(copies, axis, 0, 0, tiled=True)]
    all_to_all x2, waiting for transfers between devices: 41.5 us -> 37.6 us  [gather_a2a(): return lax.all_to_all(copies, axis, 0, 0, tiled=True)]
    reduce_sum x3 -> x2, other arithmetic: 5.3 us -> 3.55 us  [scatter_sum_a2a(): got.reshape((n, x.shape[0] // n) + x.shape[1:]).astype(jnp.float32)]
  transfers between devices with their start and end apart: 2 -> 9, of which waited for: 2 -> 8; matrix products, arithmetic and copies ran while one was open for 0% -> 0% of each run, Pallas kernels for 0% -> 0%
where the time goes in v9:
time: 164 us; the launch traced here: 162 us
  waiting for transfers between devices  54.9 us (33%)
  blocking collectives  52.9 us (32%)
  starting transfers between devices  44.3 us (27%)
  other arithmetic  3.97 us (2%)
  local copies, waits for them, and re-layouts  3.69 us (2%)
  matrix products  1.97 us (1%)
    all_to_all x2, blocking collectives, scatter_sum_a2a(): got = lax.all_to_all(x.astype(sent), axis, 0, 0, tiled=True)  42.1 us
    all_to_all x2, waiting for transfers between devices, gather_a2a(): return lax.all_to_all(copies, axis, 0, 0, tiled=True)  37.6 us
    ppermute x7, starting transfers between devices, shift(): return lax.ppermute(x, axis, [(s, (s + step) % n) for s in range(n)])  26.1 us
    all_to_all x2, starting transfers between devices, gather_a2a(): return lax.all_to_all(copies, axis, 0, 0, tiled=True)  18.2 us
    ppermute x7, waiting for transfers between devices, shift(): return lax.ppermute(x, axis, [(s, (s + step) % n) for s in range(n)])  17.3 us
    all_to_all x1, blocking collectives, gather_a2a(): return lax.all_to_all(copies, axis, 0, 0, tiled=True)  10.8 us
    reduce_sum x2, other arithmetic, scatter_sum_a2a(): got.reshape((n, x.shape[0] // n) + x.shape[1:]).astype(jnp.float32)  3.55 us
  transfers between devices with their start and end apart: 9, of which 8 were waited for; matrix products, arithmetic and copies ran while one was open for 0% of the time, Pallas kernels for 0%

profile of v9, /device:TPU:1, one launch (start us, length us, event | category | flops | bytes accessed | tf_op | source)
XLA Modules:
  0.0 162.2 jit_solution(4460540614883700918)
XLA Ops:
  0.0 0.0 copy-start.2
  0.0 0.0 copy-start.3
  0.0 0.0 copy-start
  0.0 0.0 copy-start.1
  0.0 1.9 %broadcast_in_dim.16 = bf16[32,32,512]{2,1,0:T(8,128)(2,1)} broadcast(bf16[32,512]{1,0:T(8,128)(2,1)} %param.7), dimensions={1,2} | broadcast | bytes 1081344 | tf_op jit(solution)/shard_map/broadcast_in_dim | solution.py:54
  2.0 13.7 %all-to-all-start = ((bf16[32,32,512]{2,1,0:T(8,128)(2,1)}), bf16[32,32,512]{2,1,0:T(8,128)(2,1)S(1)}, u32[]{:S(2)}, u32[]{:S(2)}) async-start(bf16[32,32,512]{2,1,0:T(8,128)(2,1)} %broadcast_in_dim.16), calls=%async_computation | async-start | bytes 2097152 | tf_op jit(solution)/shard_map/all_to_all | solution.py:55
  15.7 0.0 copy-done.2
  15.7 0.0 copy-done.3
  15.8 0.2 broadcast_in_dim.15
  16.0 0.2 broadcast_in_dim.14
  16.2 0.0 copy-done
  16.2 0.0 copy-done.1
  16.2 0.2 bitcast_multiply_fusion.2
  16.4 25.5 %all-to-all-done = bf16[32,32,512]{2,1,0:T(8,128)(2,1)S(1)} async-done(((bf16[32,32,512]{2,1,0:T(8,128)(2,1)}), bf16[32,32,512]{2,1,0:T(8,128)(2,1)S(1)}, u32[]{:S(2)}, u32[]{:S(2)}) %all-to-all-start) | async-done | bytes 1048608 | tf_op jit(solution)/shard_map/all_to_all | solution.py:55
  41.9 0.1 copy.8
  41.9 1.2 fusion
  43.2 10.6 %all_to_all.36 = f32[2,512,1024]{2,1,0:T(8,128)} all-to-all(f32[2,512,1024]{2,1,0:T(8,128)S(1)} %bitcast.45), channel_id=1, replica_groups=mesh['y'=8,'c'=2,'z'=8,'x'=4] {'c'}, dimensions={0} | all-to-all | bytes 8388608 | tf_op jit(solution)/shard_map/all_to_all | solution.py:60
  53.8 2.8 %reduce_sum.21 = f32[512,1024]{1,0:T(8,128)S(1)} reduce(f32[2,512,1024]{2,1,0:T(8,128)} %all_to_all.36, f32[]{:T(128)} %constant.76.clone.1), dimensions={0}, to_apply=%region_0.0 | reduce | flops 524288 | bytes 6291460 | tf_op jit(solution)/shard_map/reduce_sum | solution.py:61
  56.6 5.1 %collective-permute-start.3 = (f32[64,1024]{1,0:T(8,128)S(1)}, f32[64,1024]{1,0:T(8,128)S(1)}, u32[]{:S(2)}, u32[]{:S(2)}) collective-permute-start(f32[64,1024]{1,0:T(8,128)S(1)} %get-tuple-element.9), channel_id=1, source_target_pairs={{0,448},{64,0},{128,64},{192,128},{256,192},{320,256},{384,320},{4... | collective-permute-start | bytes 786440 | tf_op jit(solution)/shard_map/ppermute | solution.py:23
  61.8 1.9 %collective-permute-start = (f32[64,1024]{1,0:T(8,128)S(1)}, f32[64,1024]{1,0:T(8,128)S(1)}, u32[]{:S(2)}, u32[]{:S(2)}) collective-permute-start(f32[64,1024]{1,0:T(8,128)S(1)} %get-tuple-element.10), channel_id=1, source_target_pairs={{0,64},{64,128},{128,192},{192,256},{256,320},{320,384},{384,448},... | collective-permute-start | bytes 786440 | tf_op jit(solution)/shard_map/ppermute | solution.py:23
  63.7 3.3 %collective-permute-done.3 = f32[64,1024]{1,0:T(8,128)S(1)} collective-permute-done((f32[64,1024]{1,0:T(8,128)S(1)}, f32[64,1024]{1,0:T(8,128)S(1)}, u32[]{:S(2)}, u32[]{:S(2)}) %collective-permute-start.3) | collective-permute-done | bytes 262176 | tf_op jit(solution)/shard_map/ppermute | solution.py:23
  67.0 5.3 %collective-permute-start.4 = (f32[64,1024]{1,0:T(8,128)S(1)}, f32[64,1024]{1,0:T(8,128)S(1)}, u32[]{:S(2)}, u32[]{:S(2)}) collective-permute-start(f32[64,1024]{1,0:T(8,128)S(1)} %bitcast_add_fusion.3), channel_id=1, source_target_pairs={{0,448},{64,0},{128,64},{192,128},{256,192},{320,256},{384,320},{4... | collective-permute-start | bytes 786440 | tf_op jit(solution)/shard_map/ppermute | solution.py:23
  72.4 0.0 collective-permute-done
  72.4 4.4 %collective-permute-done.4 = f32[64,1024]{1,0:T(8,128)S(1)} collective-permute-done((f32[64,1024]{1,0:T(8,128)S(1)}, f32[64,1024]{1,0:T(8,128)S(1)}, u32[]{:S(2)}, u32[]{:S(2)}) %collective-permute-start.4) | collective-permute-done | bytes 262176 | tf_op jit(solution)/shard_map/ppermute | solution.py:23
  76.8 0.1 bitcast_add_fusion.2
  76.9 5.3 %collective-permute-start.5 = (f32[64,1024]{1,0:T(8,128)S(1)}, f32[64,1024]{1,0:T(8,128)S(1)}, u32[]{:S(2)}, u32[]{:S(2)}) collective-permute-start(f32[64,1024]{1,0:T(8,128)S(1)} %get-tuple-element.7), channel_id=1, source_target_pairs={{0,448},{64,0},{128,64},{192,128},{256,192},{320,256},{384,320},{4... | collective-permute-start | bytes 786440 | tf_op jit(solution)/shard_map/ppermute | solution.py:23
  82.2 1.9 %collective-permute-start.1 = (f32[64,1024]{1,0:T(8,128)S(1)}, f32[64,1024]{1,0:T(8,128)S(1)}, u32[]{:S(2)}, u32[]{:S(2)}) collective-permute-start(f32[64,1024]{1,0:T(8,128)S(1)} %get-tuple-element.8), channel_id=1, source_target_pairs={{0,64},{64,128},{128,192},{192,256},{256,320},{320,384},{384,448},... | collective-permute-start | bytes 786440 | tf_op jit(solution)/shard_map/ppermute | solution.py:23
  84.2 0.0 copy-start.4
  84.2 1.6 collective-permute-done.5
  85.7 4.8 %collective-permute-done.1 = f32[64,1024]{1,0:T(8,128)S(1)} collective-permute-done((f32[64,1024]{1,0:T(8,128)S(1)}, f32[64,1024]{1,0:T(8,128)S(1)}, u32[]{:S(2)}, u32[]{:S(2)}) %collective-permute-start.1) | collective-permute-done | bytes 262176 | tf_op jit(solution)/shard_map/ppermute | solution.py:23
  90.5 0.1 bitcast_add_fusion.1
  90.6 1.9 %collective-permute-start.2 = (f32[64,1024]{1,0:T(8,128)S(1)}, f32[64,1024]{1,0:T(8,128)S(1)}, u32[]{:S(2)}, u32[]{:S(2)}) collective-permute-start(f32[64,1024]{1,0:T(8,128)S(1)} %get-tuple-element.6), channel_id=1, source_target_pairs={{0,64},{64,128},{128,192},{192,256},{256,320},{320,384},{384,448},... | collective-permute-start | bytes 786440 | tf_op jit(solution)/shard_map/ppermute | solution.py:23
  92.5 4.6 %collective-permute-start.6 = (f32[64,1024]{1,0:T(8,128)S(1)}, f32[64,1024]{1,0:T(8,128)S(1)}, u32[]{:S(2)}, u32[]{:S(2)}) collective-permute-start(f32[64,1024]{1,0:T(8,128)S(1)} %get-tuple-element.5), channel_id=1, source_target_pairs={{0,448},{64,0},{128,64},{192,128},{256,192},{320,256},{384,320},{4... | collective-permute-start | bytes 786440 | tf_op jit(solution)/shard_map/ppermute | solution.py:23
  97.1 1.8 %collective-permute-done.2 = f32[64,1024]{1,0:T(8,128)S(1)} collective-permute-done((f32[64,1024]{1,0:T(8,128)S(1)}, f32[64,1024]{1,0:T(8,128)S(1)}, u32[]{:S(2)}, u32[]{:S(2)}) %collective-permute-start.2) | collective-permute-done | bytes 262176 | tf_op jit(solution)/shard_map/ppermute | solution.py:23
  98.9 1.5 collective-permute-done.6
  100.5 0.8 broadcast_in_dim.17
  101.3 4.5 %all-to-all-start.2 = ((bf16[8,64,512]{2,1,0:T(8,128)(2,1)}), bf16[8,64,512]{2,1,0:T(8,128)(2,1)S(1)}, u32[]{:S(2)}, u32[]{:S(2)}) async-start(bf16[8,64,512]{2,1,0:T(8,128)(2,1)} %broadcast_in_dim.17), calls=%async_computation.2 | async-start | bytes 1048576 | tf_op jit(solution)/shard_map/all_to_all | solution.py:55
  105.9 0.0 copy-done.4
  105.9 12.1 %all-to-all-done.2 = bf16[8,64,512]{2,1,0:T(8,128)(2,1)S(1)} async-done(((bf16[8,64,512]{2,1,0:T(8,128)(2,1)}), bf16[8,64,512]{2,1,0:T(8,128)(2,1)S(1)}, u32[]{:S(2)}, u32[]{:S(2)}) %all-to-all-start.2) | async-done | bytes 524320 | tf_op jit(solution)/shard_map/all_to_all | solution.py:55
  118.0 0.1 broadcast_in_dim.19
  118.0 0.0 copy-start.5
  118.0 10.8 %all_to_all.37 = bf16[2,512,512]{2,1,0:T(8,128)(2,1)S(1)} all-to-all(bf16[2,512,512]{2,1,0:T(8,128)(2,1)S(1)} %broadcast_in_dim.19), channel_id=1, replica_groups=mesh['y'=8,'c'=2,'z'=8,'x'=4] {'c'}, dimensions={0} | all-to-all | bytes 2097152 | tf_op jit(solution)/shard_map/all_to_all | solution.py:55
  128.9 0.1 copy.9
  129.0 0.2 broadcast_in_dim.20
  129.2 0.0 copy-done.5
  129.2 0.7 convolution_convert_fusion
  129.9 31.5 %all_to_all.38 = bf16[32,32,512]{2,1,0:T(8,128)(2,1)S(1)} all-to-all(bf16[32,32,512]{2,1,0:T(8,128)(2,1)S(1)} %bitcast.58), channel_id=1, replica_groups=mesh['y'=8,'c'=2,'z'=8,'x'=4] {'z','x'}, dimensions={0} | all-to-all | bytes 2097152 | tf_op jit(solution)/shard_map/all_to_all | solution.py:60
  161.4 0.8 reduce_sum.22
  (7 shorter events, 0.2 us)
Async XLA Ops:
  0.0 15.7 %copy-start.2 = (s32[4,4]{1,0:T(4,128)S(1)}, s32[4,4]{1,0:T(4,128)}, u32[]{:S(2)}) copy-start(s32[4,4]{1,0:T(4,128)} %param.12) | copy-start | bytes 196
  0.0 15.7 %copy-start.3 = (s32[4,4]{1,0:T(4,128)S(1)}, s32[4,4]{1,0:T(4,128)}, u32[]{:S(2)}) copy-start(s32[4,4]{1,0:T(4,128)} %param.11) | copy-start | bytes 196
  0.0 16.2 %copy-start = (bf16[512,512]{1,0:T(8,128)(2,1)S(1)}, bf16[512,512]{1,0:T(8,128)(2,1)}, u32[]{:S(2)}) copy-start(bf16[512,512]{1,0:T(8,128)(2,1)} %param.9) | copy-start | bytes 1572868
  0.0 16.2 %copy-start.1 = (bf16[512,512]{1,0:T(8,128)(2,1)S(1)}, bf16[512,512]{1,0:T(8,128)(2,1)}, u32[]{:S(2)}) copy-start(bf16[512,512]{1,0:T(8,128)(2,1)} %param.8) | copy-start | bytes 1572868
  2.0 39.9 %all-to-all-start = ((bf16[32,32,512]{2,1,0:T(8,128)(2,1)}), bf16[32,32,512]{2,1,0:T(8,128)(2,1)S(1)}, u32[]{:S(2)}, u32[]{:S(2)}) async-start(bf16[32,32,512]{2,1,0:T(8,128)(2,1)} %broadcast_in_dim.16), calls=%async_computation | async-start | bytes 2097152 | tf_op jit(solution)/shard_map/all_to_all | solution.py:55
  56.6 10.4 %collective-permute-start.3 = (f32[64,1024]{1,0:T(8,128)S(1)}, f32[64,1024]{1,0:T(8,128)S(1)}, u32[]{:S(2)}, u32[]{:S(2)}) collective-permute-start(f32[64,1024]{1,0:T(8,128)S(1)} %get-tuple-element.9), channel_id=1, source_target_pairs={{0,448},{64,0},{128,64},{192,128},{256,192},{320,256},{384,320},{4... | collective-permute-start | bytes 786440 | tf_op jit(solution)/shard_map/ppermute | solution.py:23
  61.8 10.6 %collective-permute-start = (f32[64,1024]{1,0:T(8,128)S(1)}, f32[64,1024]{1,0:T(8,128)S(1)}, u32[]{:S(2)}, u32[]{:S(2)}) collective-permute-start(f32[64,1024]{1,0:T(8,128)S(1)} %get-tuple-element.10), channel_id=1, source_target_pairs={{0,64},{64,128},{128,192},{192,256},{256,320},{320,384},{384,448},... | collective-permute-start | bytes 786440 | tf_op jit(solution)/shard_map/ppermute | solution.py:23
  67.0 9.7 %collective-permute-start.4 = (f32[64,1024]{1,0:T(8,128)S(1)}, f32[64,1024]{1,0:T(8,128)S(1)}, u32[]{:S(2)}, u32[]{:S(2)}) collective-permute-start(f32[64,1024]{1,0:T(8,128)S(1)} %bitcast_add_fusion.3), channel_id=1, source_target_pairs={{0,448},{64,0},{128,64},{192,128},{256,192},{320,256},{384,320},{4... | collective-permute-start | bytes 786440 | tf_op jit(solution)/shard_map/ppermute | solution.py:23
  76.9 8.9 %collective-permute-start.5 = (f32[64,1024]{1,0:T(8,128)S(1)}, f32[64,1024]{1,0:T(8,128)S(1)}, u32[]{:S(2)}, u32[]{:S(2)}) collective-permute-start(f32[64,1024]{1,0:T(8,128)S(1)} %get-tuple-element.7), channel_id=1, source_target_pairs={{0,448},{64,0},{128,64},{192,128},{256,192},{320,256},{384,320},{4... | collective-permute-start | bytes 786440 | tf_op jit(solution)/shard_map/ppermute | solution.py:23
  82.2 8.3 %collective-permute-start.1 = (f32[64,1024]{1,0:T(8,128)S(1)}, f32[64,1024]{1,0:T(8,128)S(1)}, u32[]{:S(2)}, u32[]{:S(2)}) collective-permute-start(f32[64,1024]{1,0:T(8,128)S(1)} %get-tuple-element.8), channel_id=1, source_target_pairs={{0,64},{64,128},{128,192},{192,256},{256,320},{320,384},{384,448},... | collective-permute-start | bytes 786440 | tf_op jit(solution)/shard_map/ppermute | solution.py:23
  84.2 21.7 %copy-start.4 = (s32[4,4]{1,0:T(4,128)S(1)}, s32[4,4]{1,0:T(4,128)}, u32[]{:S(2)}) copy-start(s32[4,4]{1,0:T(4,128)} %param.13) | copy-start | bytes 196
  90.6 8.3 %collective-permute-start.2 = (f32[64,1024]{1,0:T(8,128)S(1)}, f32[64,1024]{1,0:T(8,128)S(1)}, u32[]{:S(2)}, u32[]{:S(2)}) collective-permute-start(f32[64,1024]{1,0:T(8,128)S(1)} %get-tuple-element.6), channel_id=1, source_target_pairs={{0,64},{64,128},{128,192},{192,256},{256,320},{320,384},{384,448},... | collective-permute-start | bytes 786440 | tf_op jit(solution)/shard_map/ppermute | solution.py:23
  92.5 7.9 %collective-permute-start.6 = (f32[64,1024]{1,0:T(8,128)S(1)}, f32[64,1024]{1,0:T(8,128)S(1)}, u32[]{:S(2)}, u32[]{:S(2)}) collective-permute-start(f32[64,1024]{1,0:T(8,128)S(1)} %get-tuple-element.5), channel_id=1, source_target_pairs={{0,448},{64,0},{128,64},{192,128},{256,192},{320,256},{384,320},{4... | collective-permute-start | bytes 786440 | tf_op jit(solution)/shard_map/ppermute | solution.py:23
  101.3 16.6 %all-to-all-start.2 = ((bf16[8,64,512]{2,1,0:T(8,128)(2,1)}), bf16[8,64,512]{2,1,0:T(8,128)(2,1)S(1)}, u32[]{:S(2)}, u32[]{:S(2)}) async-start(bf16[8,64,512]{2,1,0:T(8,128)(2,1)} %broadcast_in_dim.17), calls=%async_computation.2 | async-start | bytes 1048576 | tf_op jit(solution)/shard_map/all_to_all | solution.py:55
  118.0 11.1 %copy-start.5 = (bf16[512,512]{1,0:T(8,128)(2,1)S(1)}, bf16[512,512]{1,0:T(8,128)(2,1)}, u32[]{:S(2)}) copy-start(bf16[512,512]{1,0:T(8,128)(2,1)} %param.10) | copy-start | bytes 1572868

commit v10 on v9

--- a/solution.py
+++ b/solution.py
@@ -40,6 +40,20 @@
     return acc_up + acc_down + own(i)
 
 
+def scatter_sum_pair(x, axis):
+    i = lax.axis_index(axis)
+    halves = x.reshape((2, x.shape[0] // 2) + x.shape[1:])
+    mine = lax.dynamic_index_in_dim(halves, i, axis=0, keepdims=False)
+    theirs = lax.dynamic_index_in_dim(halves, 1 - i, axis=0, keepdims=False)
+    return mine + shift(theirs, axis, 1)
+
+
+def gather_pair(x, axis):
+    i = lax.axis_index(axis)
+    parts = jnp.stack([x, shift(x, axis, 1)])
+    return jnp.take(parts, (i - jnp.arange(2)) % 2, axis=0).reshape((2 * x.shape[0],) + x.shape[1:])
+
+
 def swiglu(summed, hidden_cols):
     return (jax.nn.silu(summed[:, :hidden_cols]) * summed[:, hidden_cols:]).astype(jnp.bfloat16)
 
@@ -73,10 +87,10 @@
     share = rows // (n_y * n_c)
     by_core = all_tokens.reshape(n_y, n_c, share, feats).transpose(1, 0, 2, 3).reshape(rows, feats)
     partial = jnp.dot(by_core, both_weights, preferred_element_type=jnp.float32)
-    summed = scatter_sum_chains(scatter_sum_a2a(partial, "c"), "y")
+    summed = scatter_sum_chains(scatter_sum_pair(partial, "c"), "y")
     hidden_share = swiglu(summed, hidden_cols)
     half = gather_a2a(hidden_share, "y")
-    both = gather_a2a(half, "c")
+    both = gather_pair(half, "c")
     hidden = both.reshape(n_c, n_y, share, -1).transpose(1, 0, 2, 3).reshape(rows, -1)
     partial_out = jnp.dot(hidden, down_eff, preferred_element_type=jnp.float32)
     partial_out = scatter_sum_a2a(partial_out, COL, sent=jnp.bfloat16)

time: 164 us -> 163 us (level)
  starting transfers between devices: 44.3 us -> 52.8 us
  waiting for transfers between devices: 54.9 us -> 48.2 us
  blocking collectives: 52.9 us -> 48 us
  local copies, waits for them, and re-layouts: 3.69 us -> 5.94 us
    ppermute x7 -> x9, starting transfers between devices: 26.1 us -> 39.1 us  [shift(): return lax.ppermute(x, axis, [(s, (s + step) % n) for s in range(n)])]
    all_to_all x2 -> x1, waiting for transfers between devices: 37.6 us -> 25.5 us  [gather_a2a(): return lax.all_to_all(copies, axis, 0, 0, tiled=True)]
    all_to_all x2 -> x1, blocking collectives: 42.1 us -> 31.5 us  [scatter_sum_a2a(): got = lax.all_to_all(x.astype(sent), axis, 0, 0, tiled=True)]
    all_to_all x1, blocking collectives: 10.8 us -> 16.5 us  [gather_a2a(): return lax.all_to_all(copies, axis, 0, 0, tiled=True)]
    ppermute x7 -> x9, waiting for transfers between devices: 17.3 us -> 22.6 us  [shift(): return lax.ppermute(x, axis, [(s, (s + step) % n) for s in range(n)])]
    all_to_all x2 -> x1, starting transfers between devices: 18.2 us -> 13.7 us  [gather_a2a(): return lax.all_to_all(copies, axis, 0, 0, tiled=True)]
    reduce_sum x2 -> x1, other arithmetic: 3.55 us -> 0.77 us  [scatter_sum_a2a(): got.reshape((n, x.shape[0] // n) + x.shape[1:]).astype(jnp.float32)]
    add x0 -> x1, other arithmetic: none -> 2.61 us  [scatter_sum_pair(): return mine + shift(theirs, axis, 1)]
  transfers between devices with their start and end apart: 9 -> 10, of which waited for: 8 -> 9; matrix products, arithmetic and copies ran while one was open for 0% -> 0% of each run, Pallas kernels for 0% -> 0%
where the time goes in v10:
time: 163 us; the launch traced here: 161 us
  starting transfers between devices  52.8 us (32%)
  waiting for transfers between devices  48.2 us (30%)
  blocking collectives  48 us (29%)
  local copies, waits for them, and re-layouts  5.94 us (4%)
  other arithmetic  4.1 us (3%)
  matrix products  1.97 us (1%)
    ppermute x9, starting transfers between devices, shift(): return lax.ppermute(x, axis, [(s, (s + step) % n) for s in range(n)])  39.1 us
    all_to_all x1, blocking collectives, scatter_sum_a2a(): got = lax.all_to_all(x.astype(sent), axis, 0, 0, tiled=True)  31.5 us
    all_to_all x1, waiting for transfers between devices, gather_a2a(): return lax.all_to_all(copies, axis, 0, 0, tiled=True)  25.5 us
    ppermute x9, waiting for transfers between devices, shift(): return lax.ppermute(x, axis, [(s, (s + step) % n) for s in range(n)])  22.6 us
    all_to_all x1, blocking collectives, gather_a2a(): return lax.all_to_all(copies, axis, 0, 0, tiled=True)  16.5 us
    all_to_all x1, starting transfers between devices, gather_a2a(): return lax.all_to_all(copies, axis, 0, 0, tiled=True)  13.7 us
  transfers between devices with their start and end apart: 10, of which 9 were waited for; matrix products, arithmetic and copies ran while one was open for 0% of the time, Pallas kernels for 0%

profile of v10, /device:TPU:1, one launch (start us, length us, event | category | flops | bytes accessed | tf_op | source)
XLA Modules:
  0.0 161.4 jit_solution(12971952438881221077)
XLA Ops:
  0.0 0.0 copy-start.2
  0.0 1.9 %broadcast_in_dim.20 = bf16[32,32,512]{2,1,0:T(8,128)(2,1)} broadcast(bf16[32,512]{1,0:T(8,128)(2,1)} %param.7), dimensions={1,2} | broadcast | bytes 1081344 | tf_op jit(solution)/shard_map/broadcast_in_dim | solution.py:68
  2.0 13.7 %all-to-all-start = ((bf16[32,32,512]{2,1,0:T(8,128)(2,1)}), bf16[32,32,512]{2,1,0:T(8,128)(2,1)S(1)}, u32[]{:S(2)}, u32[]{:S(2)}) async-start(bf16[32,32,512]{2,1,0:T(8,128)(2,1)} %broadcast_in_dim.20), calls=%async_computation | async-start | bytes 2097152 | tf_op jit(solution)/shard_map/all_to_all | solution.py:69
  15.7 0.0 copy-done.3
  15.7 0.0 copy-done.4
  15.7 0.2 broadcast_in_dim.19
  15.9 0.2 broadcast_in_dim.18
  16.1 0.0 copy-done.1
  16.2 0.0 copy-done.2
  16.2 0.2 bitcast_multiply_fusion.2
  16.3 25.5 %all-to-all-done = bf16[32,32,512]{2,1,0:T(8,128)(2,1)S(1)} async-done(((bf16[32,32,512]{2,1,0:T(8,128)(2,1)}), bf16[32,32,512]{2,1,0:T(8,128)(2,1)S(1)}, u32[]{:S(2)}, u32[]{:S(2)}) %all-to-all-start) | async-done | bytes 1048608 | tf_op jit(solution)/shard_map/all_to_all | solution.py:69
  41.9 0.1 copy.8
  41.9 1.2 fusion
  43.2 0.2 dynamic-slice_bitcast_fusion
  43.5 1.7 %copy-done = f32[1024,1024]{0,1:T(8,128)} copy-done((f32[1024,1024]{0,1:T(8,128)}, f32[1024,1024]{0,1:T(8,128)S(1)}, u32[]{:S(2)}) %copy-start) | copy-done | bytes 4194328
  45.2 4.7 %collective-permute-start = (f32[512,1024]{1,0:T(8,128)S(1)}, f32[512,1024]{1,0:T(8,128)}, u32[]{:S(2)}, u32[]{:S(2)}) collective-permute-start(f32[512,1024]{1,0:T(8,128)S(1)} %dynamic-slice_bitcast_fusion), channel_id=1, source_target_pairs={{0,32},{32,0},{1,33},{33,1},{2,34},{34,2},{3,35},{35,3},{4,36},{36... | collective-permute-start | bytes 6291464 | tf_op jit(solution)/shard_map/ppermute | solution.py:23
  49.9 3.9 %collective-permute-done = f32[512,1024]{1,0:T(8,128)} collective-permute-done((f32[512,1024]{1,0:T(8,128)S(1)}, f32[512,1024]{1,0:T(8,128)}, u32[]{:S(2)}, u32[]{:S(2)}) %collective-permute-start) | collective-permute-done | bytes 2097184 | tf_op jit(solution)/shard_map/ppermute | solution.py:23
  53.8 2.6 %bitcast_add_fusion = f32[512,1024]{1,0:T(8,128)S(1)} fusion(f32[512,1024]{1,0:T(8,128)} %collective-permute-done, f32[2,512,1024]{2,1,0:T(8,128)} %bitcast.54, s32[]{:T(128)S(6)} %select_n.107), kind=kLoop, calls=%fused_computation.1 | loop fusion | flops 524288 | bytes 6291460 | tf_op jit(solution)/shard_map/add | solution.py:48
  56.4 5.1 %collective-permute-start.4 = (f32[64,1024]{1,0:T(8,128)S(1)}, f32[64,1024]{1,0:T(8,128)S(1)}, u32[]{:S(2)}, u32[]{:S(2)}) collective-permute-start(f32[64,1024]{1,0:T(8,128)S(1)} %get-tuple-element.9), channel_id=1, source_target_pairs={{0,448},{64,0},{128,64},{192,128},{256,192},{320,256},{384,320},{4... | collective-permute-start | bytes 786440 | tf_op jit(solution)/shard_map/ppermute | solution.py:23
  61.6 1.9 %collective-permute-start.1 = (f32[64,1024]{1,0:T(8,128)S(1)}, f32[64,1024]{1,0:T(8,128)S(1)}, u32[]{:S(2)}, u32[]{:S(2)}) collective-permute-start(f32[64,1024]{1,0:T(8,128)S(1)} %get-tuple-element.10), channel_id=1, source_target_pairs={{0,64},{64,128},{128,192},{192,256},{256,320},{320,384},{384,448},... | collective-permute-start | bytes 786440 | tf_op jit(solution)/shard_map/ppermute | solution.py:23
  63.5 3.3 %collective-permute-done.4 = f32[64,1024]{1,0:T(8,128)S(1)} collective-permute-done((f32[64,1024]{1,0:T(8,128)S(1)}, f32[64,1024]{1,0:T(8,128)S(1)}, u32[]{:S(2)}, u32[]{:S(2)}) %collective-permute-start.4) | collective-permute-done | bytes 262176 | tf_op jit(solution)/shard_map/ppermute | solution.py:23
  66.8 5.3 %collective-permute-start.5 = (f32[64,1024]{1,0:T(8,128)S(1)}, f32[64,1024]{1,0:T(8,128)S(1)}, u32[]{:S(2)}, u32[]{:S(2)}) collective-permute-start(f32[64,1024]{1,0:T(8,128)S(1)} %bitcast_add_fusion.4), channel_id=1, source_target_pairs={{0,448},{64,0},{128,64},{192,128},{256,192},{320,256},{384,320},{4... | collective-permute-start | bytes 786440 | tf_op jit(solution)/shard_map/ppermute | solution.py:23
  72.2 0.0 collective-permute-done.1
  72.2 4.4 %collective-permute-done.5 = f32[64,1024]{1,0:T(8,128)S(1)} collective-permute-done((f32[64,1024]{1,0:T(8,128)S(1)}, f32[64,1024]{1,0:T(8,128)S(1)}, u32[]{:S(2)}, u32[]{:S(2)}) %collective-permute-start.5) | collective-permute-done | bytes 262176 | tf_op jit(solution)/shard_map/ppermute | solution.py:23
  76.6 0.1 bitcast_add_fusion.3
  76.7 5.3 %collective-permute-start.6 = (f32[64,1024]{1,0:T(8,128)S(1)}, f32[64,1024]{1,0:T(8,128)S(1)}, u32[]{:S(2)}, u32[]{:S(2)}) collective-permute-start(f32[64,1024]{1,0:T(8,128)S(1)} %get-tuple-element.7), channel_id=1, source_target_pairs={{0,448},{64,0},{128,64},{192,128},{256,192},{320,256},{384,320},{4... | collective-permute-start | bytes 786440 | tf_op jit(solution)/shard_map/ppermute | solution.py:23
  82.0 1.9 %collective-permute-start.2 = (f32[64,1024]{1,0:T(8,128)S(1)}, f32[64,1024]{1,0:T(8,128)S(1)}, u32[]{:S(2)}, u32[]{:S(2)}) collective-permute-start(f32[64,1024]{1,0:T(8,128)S(1)} %get-tuple-element.8), channel_id=1, source_target_pairs={{0,64},{64,128},{128,192},{192,256},{256,320},{320,384},{384,448},... | collective-permute-start | bytes 786440 | tf_op jit(solution)/shard_map/ppermute | solution.py:23
  83.9 0.0 copy-start.5
  84.0 1.6 collective-permute-done.6
  85.5 4.8 %collective-permute-done.2 = f32[64,1024]{1,0:T(8,128)S(1)} collective-permute-done((f32[64,1024]{1,0:T(8,128)S(1)}, f32[64,1024]{1,0:T(8,128)S(1)}, u32[]{:S(2)}, u32[]{:S(2)}) %collective-permute-start.2) | collective-permute-done | bytes 262176 | tf_op jit(solution)/shard_map/ppermute | solution.py:23
  90.3 0.1 bitcast_add_fusion.2
  90.4 1.9 %collective-permute-start.3 = (f32[64,1024]{1,0:T(8,128)S(1)}, f32[64,1024]{1,0:T(8,128)S(1)}, u32[]{:S(2)}, u32[]{:S(2)}) collective-permute-start(f32[64,1024]{1,0:T(8,128)S(1)} %get-tuple-element.6), channel_id=1, source_target_pairs={{0,64},{64,128},{128,192},{192,256},{256,320},{320,384},{384,448},... | collective-permute-start | bytes 786440 | tf_op jit(solution)/shard_map/ppermute | solution.py:23
  92.3 4.6 %collective-permute-start.7 = (f32[64,1024]{1,0:T(8,128)S(1)}, f32[64,1024]{1,0:T(8,128)S(1)}, u32[]{:S(2)}, u32[]{:S(2)}) collective-permute-start(f32[64,1024]{1,0:T(8,128)S(1)} %get-tuple-element.5), channel_id=1, source_target_pairs={{0,448},{64,0},{128,64},{192,128},{256,192},{320,256},{384,320},{4... | collective-permute-start | bytes 786440 | tf_op jit(solution)/shard_map/ppermute | solution.py:23
  96.9 1.8 %collective-permute-done.3 = f32[64,1024]{1,0:T(8,128)S(1)} collective-permute-done((f32[64,1024]{1,0:T(8,128)S(1)}, f32[64,1024]{1,0:T(8,128)S(1)}, u32[]{:S(2)}, u32[]{:S(2)}) %collective-permute-start.3) | collective-permute-done | bytes 262176 | tf_op jit(solution)/shard_map/ppermute | solution.py:23
  98.7 1.5 collective-permute-done.7
  100.3 16.5 %all_to_all.24 = bf16[8,64,512]{2,1,0:T(8,128)(2,1)S(1)} all-to-all(bf16[8,64,512]{2,1,0:T(8,128)(2,1)S(1)} %broadcast_in_dim.21), channel_id=1, replica_groups=mesh['y'=8,'c'=2,'z'=8,'x'=4] {'y'}, dimensions={0} | all-to-all | bytes 1048576 | tf_op jit(solution)/shard_map/all_to_all | solution.py:69
  116.8 8.3 %collective-permute-start.8 = (bf16[512,512]{1,0:T(8,128)(2,1)S(1)}, bf16[512,512]{1,0:T(8,128)(2,1)S(1)}, u32[]{:S(2)}, u32[]{:S(2)}) collective-permute-start(bf16[512,512]{1,0:T(8,128)(2,1)S(1)} %bitcast.63), channel_id=1, source_target_pairs={{0,32},{32,0},{1,33},{33,1},{2,34},{34,2},{3,35},{35,3},{4,36},{36... | collective-permute-start | bytes 1572872 | tf_op jit(solution)/shard_map/ppermute | solution.py:23
  125.2 1.4 collective-permute-done.8
  126.6 0.1 pad_maximum_fusion
  126.7 0.6 gather_fusion
  127.4 0.0 copy-start.6
  127.4 0.2 select_bitcast_fusion
  127.5 0.1 copy.9
  127.6 0.2 broadcast_in_dim.46
  127.8 0.6 copy-done.6
  128.4 0.7 convolution_convert_fusion
  129.1 31.5 %all_to_all.25 = bf16[32,32,512]{2,1,0:T(8,128)(2,1)S(1)} all-to-all(bf16[32,32,512]{2,1,0:T(8,128)(2,1)S(1)} %bitcast.68), channel_id=1, replica_groups=mesh['y'=8,'c'=2,'z'=8,'x'=4] {'z','x'}, dimensions={0} | all-to-all | bytes 2097152 | tf_op jit(solution)/shard_map/all_to_all | solution.py:74
  160.6 0.8 reduce_sum.12
  (16 shorter events, 0.3 us)
Async XLA Ops:
  0.0 15.7 %copy-start.3 = (s32[4,4]{1,0:T(4,128)S(1)}, s32[4,4]{1,0:T(4,128)}, u32[]{:S(2)}) copy-start(s32[4,4]{1,0:T(4,128)} %param.12) | copy-start | bytes 196
  0.0 15.7 %copy-start.4 = (s32[4,4]{1,0:T(4,128)S(1)}, s32[4,4]{1,0:T(4,128)}, u32[]{:S(2)}) copy-start(s32[4,4]{1,0:T(4,128)} %param.11) | copy-start | bytes 196
  0.0 16.1 %copy-start.1 = (bf16[512,512]{1,0:T(8,128)(2,1)S(1)}, bf16[512,512]{1,0:T(8,128)(2,1)}, u32[]{:S(2)}) copy-start(bf16[512,512]{1,0:T(8,128)(2,1)} %param.9) | copy-start | bytes 1572868
  0.0 16.1 %copy-start.2 = (bf16[512,512]{1,0:T(8,128)(2,1)S(1)}, bf16[512,512]{1,0:T(8,128)(2,1)}, u32[]{:S(2)}) copy-start(bf16[512,512]{1,0:T(8,128)(2,1)} %param.8) | copy-start | bytes 1572868
  2.0 39.9 %all-to-all-start = ((bf16[32,32,512]{2,1,0:T(8,128)(2,1)}), bf16[32,32,512]{2,1,0:T(8,128)(2,1)S(1)}, u32[]{:S(2)}, u32[]{:S(2)}) async-start(bf16[32,32,512]{2,1,0:T(8,128)(2,1)} %broadcast_in_dim.20), calls=%async_computation | async-start | bytes 2097152 | tf_op jit(solution)/shard_map/all_to_all | solution.py:69
  43.2 2.0 %copy-start = (f32[1024,1024]{0,1:T(8,128)}, f32[1024,1024]{0,1:T(8,128)S(1)}, u32[]{:S(2)}) copy-start(f32[1024,1024]{0,1:T(8,128)S(1)} %fusion) | copy-start | bytes 12582916
  45.2 8.6 %collective-permute-start = (f32[512,1024]{1,0:T(8,128)S(1)}, f32[512,1024]{1,0:T(8,128)}, u32[]{:S(2)}, u32[]{:S(2)}) collective-permute-start(f32[512,1024]{1,0:T(8,128)S(1)} %dynamic-slice_bitcast_fusion), channel_id=1, source_target_pairs={{0,32},{32,0},{1,33},{33,1},{2,34},{34,2},{3,35},{35,3},{4,36},{36... | collective-permute-start | bytes 6291464 | tf_op jit(solution)/shard_map/ppermute | solution.py:23
  56.4 10.4 %collective-permute-start.4 = (f32[64,1024]{1,0:T(8,128)S(1)}, f32[64,1024]{1,0:T(8,128)S(1)}, u32[]{:S(2)}, u32[]{:S(2)}) collective-permute-start(f32[64,1024]{1,0:T(8,128)S(1)} %get-tuple-element.9), channel_id=1, source_target_pairs={{0,448},{64,0},{128,64},{192,128},{256,192},{320,256},{384,320},{4... | collective-permute-start | bytes 786440 | tf_op jit(solution)/shard_map/ppermute | solution.py:23
  61.6 10.6 %collective-permute-start.1 = (f32[64,1024]{1,0:T(8,128)S(1)}, f32[64,1024]{1,0:T(8,128)S(1)}, u32[]{:S(2)}, u32[]{:S(2)}) collective-permute-start(f32[64,1024]{1,0:T(8,128)S(1)} %get-tuple-element.10), channel_id=1, source_target_pairs={{0,64},{64,128},{128,192},{192,256},{256,320},{320,384},{384,448},... | collective-permute-start | bytes 786440 | tf_op jit(solution)/shard_map/ppermute | solution.py:23
  66.8 9.7 %collective-permute-start.5 = (f32[64,1024]{1,0:T(8,128)S(1)}, f32[64,1024]{1,0:T(8,128)S(1)}, u32[]{:S(2)}, u32[]{:S(2)}) collective-permute-start(f32[64,1024]{1,0:T(8,128)S(1)} %bitcast_add_fusion.4), channel_id=1, source_target_pairs={{0,448},{64,0},{128,64},{192,128},{256,192},{320,256},{384,320},{4... | collective-permute-start | bytes 786440 | tf_op jit(solution)/shard_map/ppermute | solution.py:23
  76.7 8.9 %collective-permute-start.6 = (f32[64,1024]{1,0:T(8,128)S(1)}, f32[64,1024]{1,0:T(8,128)S(1)}, u32[]{:S(2)}, u32[]{:S(2)}) collective-permute-start(f32[64,1024]{1,0:T(8,128)S(1)} %get-tuple-element.7), channel_id=1, source_target_pairs={{0,448},{64,0},{128,64},{192,128},{256,192},{320,256},{384,320},{4... | collective-permute-start | bytes 786440 | tf_op jit(solution)/shard_map/ppermute | solution.py:23
  82.0 8.3 %collective-permute-start.2 = (f32[64,1024]{1,0:T(8,128)S(1)}, f32[64,1024]{1,0:T(8,128)S(1)}, u32[]{:S(2)}, u32[]{:S(2)}) collective-permute-start(f32[64,1024]{1,0:T(8,128)S(1)} %get-tuple-element.8), channel_id=1, source_target_pairs={{0,64},{64,128},{128,192},{192,256},{256,320},{320,384},{384,448},... | collective-permute-start | bytes 786440 | tf_op jit(solution)/shard_map/ppermute | solution.py:23
  83.9 41.2 %copy-start.5 = (s32[4,4]{1,0:T(4,128)S(1)}, s32[4,4]{1,0:T(4,128)}, u32[]{:S(2)}) copy-start(s32[4,4]{1,0:T(4,128)} %param.13) | copy-start | bytes 196
  90.4 8.3 %collective-permute-start.3 = (f32[64,1024]{1,0:T(8,128)S(1)}, f32[64,1024]{1,0:T(8,128)S(1)}, u32[]{:S(2)}, u32[]{:S(2)}) collective-permute-start(f32[64,1024]{1,0:T(8,128)S(1)} %get-tuple-element.6), channel_id=1, source_target_pairs={{0,64},{64,128},{128,192},{192,256},{256,320},{320,384},{384,448},... | collective-permute-start | bytes 786440 | tf_op jit(solution)/shard_map/ppermute | solution.py:23
  92.3 7.9 %collective-permute-start.7 = (f32[64,1024]{1,0:T(8,128)S(1)}, f32[64,1024]{1,0:T(8,128)S(1)}, u32[]{:S(2)}, u32[]{:S(2)}) collective-permute-start(f32[64,1024]{1,0:T(8,128)S(1)} %get-tuple-element.5), channel_id=1, source_target_pairs={{0,448},{64,0},{128,64},{192,128},{256,192},{320,256},{384,320},{4... | collective-permute-start | bytes 786440 | tf_op jit(solution)/shard_map/ppermute | solution.py:23
  116.8 9.8 %collective-permute-start.8 = (bf16[512,512]{1,0:T(8,128)(2,1)S(1)}, bf16[512,512]{1,0:T(8,128)(2,1)S(1)}, u32[]{:S(2)}, u32[]{:S(2)}) collective-permute-start(bf16[512,512]{1,0:T(8,128)(2,1)S(1)} %bitcast.63), channel_id=1, source_target_pairs={{0,32},{32,0},{1,33},{33,1},{2,34},{34,2},{3,35},{35,3},{4,36},{36... | collective-permute-start | bytes 1572872 | tf_op jit(solution)/shard_map/ppermute | solution.py:23
  127.4 1.0 copy-start.6

commit v11 on v10

--- a/solution.py
+++ b/solution.py
@@ -81,7 +81,7 @@
         [gate_weight * widen(gate_mask), up_weight * widen(up_mask)], axis=1
     )
     down_eff = down_weight * widen(down_mask)
-    all_tokens = gather_a2a(tokens, COL)
+    all_tokens = gather_a2a(gather_a2a(tokens, "z"), "x")
     n_y, n_c = lax.axis_size("y"), lax.axis_size("c")
     rows, feats = all_tokens.shape
     share = rows // (n_y * n_c)
@@ -93,7 +93,7 @@
     both = gather_pair(half, "c")
     hidden = both.reshape(n_c, n_y, share, -1).transpose(1, 0, 2, 3).reshape(rows, -1)
     partial_out = jnp.dot(hidden, down_eff, preferred_element_type=jnp.float32)
-    partial_out = scatter_sum_a2a(partial_out, COL, sent=jnp.bfloat16)
+    partial_out = scatter_sum_a2a(scatter_sum_a2a(partial_out, "x", sent=jnp.bfloat16), "z")
     return partial_out.astype(jnp.bfloat16)
 
 

time: 163 us -> 165 us (1.012)
  blocking collectives: 48 us -> 72.7 us
  waiting for transfers between devices: 48.2 us -> 34.3 us
  starting transfers between devices: 52.8 us -> 44 us
    all_to_all x1 -> x2, blocking collectives: 16.5 us -> 37.6 us  [gather_a2a(): return lax.all_to_all(copies, axis, 0, 0, tiled=True)]
    all_to_all x1, waiting for transfers between devices: 25.5 us -> 11.7 us  [gather_a2a(): return lax.all_to_all(copies, axis, 0, 0, tiled=True)]
    all_to_all x1, starting transfers between devices: 13.7 us -> 4.01 us  [gather_a2a(): return lax.all_to_all(copies, axis, 0, 0, tiled=True)]
    all_to_all x1 -> x2, blocking collectives: 31.5 us -> 35.1 us  [scatter_sum_a2a(): got = lax.all_to_all(x.astype(sent), axis, 0, 0, tiled=True)]
where the time goes in v11:
time: 165 us; the launch traced here: 163 us
  blocking collectives  72.7 us (44%)
  starting transfers between devices  44 us (27%)
  waiting for transfers between devices  34.3 us (21%)
  local copies, waits for them, and re-layouts  5.87 us (4%)
  other arithmetic  4.13 us (3%)
  matrix products  1.97 us (1%)
    ppermute x9, starting transfers between devices, shift(): return lax.ppermute(x, axis, [(s, (s + step) % n) for s in range(n)])  40 us
    all_to_all x2, blocking collectives, gather_a2a(): return lax.all_to_all(copies, axis, 0, 0, tiled=True)  37.6 us
    all_to_all x2, blocking collectives, scatter_sum_a2a(): got = lax.all_to_all(x.astype(sent), axis, 0, 0, tiled=True)  35.1 us
    ppermute x9, waiting for transfers between devices, shift(): return lax.ppermute(x, axis, [(s, (s + step) % n) for s in range(n)])  22.6 us
    all_to_all x1, waiting for transfers between devices, gather_a2a(): return lax.all_to_all(copies, axis, 0, 0, tiled=True)  11.7 us
    all_to_all x1, starting transfers between devices, gather_a2a(): return lax.all_to_all(copies, axis, 0, 0, tiled=True)  4.01 us
  transfers between devices with their start and end apart: 10, of which 9 were waited for; matrix products, arithmetic and copies ran while one was open for 0% of the time, Pallas kernels for 0%

profile of v11, /device:TPU:1, one launch (start us, length us, event | category | flops | bytes accessed | tf_op | source)
XLA Modules:
  0.0 163.4 jit_solution(10591164751202950805)
XLA Ops:
  0.0 0.8 broadcast_in_dim.24
  0.8 21.1 %all_to_all.39 = bf16[8,32,512]{2,1,0:T(8,128)(2,1)S(1)} all-to-all(bf16[8,32,512]{2,1,0:T(8,128)(2,1)S(1)} %broadcast_in_dim.24), channel_id=1, replica_groups=mesh['y'=8,'c'=2,'z'=8,'x'=4] {'z'}, dimensions={0} | all-to-all | bytes 524288 | tf_op jit(solution)/shard_map/all_to_all | solution.py:69
  22.0 1.1 broadcast_in_dim.26
  23.0 4.0 %all-to-all-start.1 = ((bf16[4,256,512]{2,1,0:T(8,128)(2,1)}), bf16[4,256,512]{2,1,0:T(8,128)(2,1)S(1)}, u32[]{:S(2)}, u32[]{:S(2)}) async-start(bf16[4,256,512]{2,1,0:T(8,128)(2,1)} %broadcast_in_dim.26), calls=%async_computation.1 | async-start | bytes 2097152 | tf_op jit(solution)/shard_map/all_to_all | solution.py:69
  27.0 0.0 copy-done.4
  27.1 0.2 broadcast_in_dim.23
  27.3 0.2 broadcast_in_dim.22
  27.5 0.2 bitcast_multiply_fusion.2
  27.7 11.7 %all-to-all-done.1 = bf16[4,256,512]{2,1,0:T(8,128)(2,1)S(1)} async-done(((bf16[4,256,512]{2,1,0:T(8,128)(2,1)}), bf16[4,256,512]{2,1,0:T(8,128)(2,1)S(1)}, u32[]{:S(2)}, u32[]{:S(2)}) %all-to-all-start.1) | async-done | bytes 1048608 | tf_op jit(solution)/shard_map/all_to_all | solution.py:69
  39.3 0.1 copy.10
  39.4 1.3 fusion
  40.7 0.2 dynamic-slice_bitcast_fusion
  40.9 1.7 %copy-done = f32[1024,1024]{0,1:T(8,128)} copy-done((f32[1024,1024]{0,1:T(8,128)}, f32[1024,1024]{0,1:T(8,128)S(1)}, u32[]{:S(2)}) %copy-start) | copy-done | bytes 4194328
  42.6 5.7 %collective-permute-start = (f32[512,1024]{1,0:T(8,128)S(1)}, f32[512,1024]{1,0:T(8,128)}, u32[]{:S(2)}, u32[]{:S(2)}) collective-permute-start(f32[512,1024]{1,0:T(8,128)S(1)} %dynamic-slice_bitcast_fusion), channel_id=1, source_target_pairs={{0,32},{32,0},{1,33},{33,1},{2,34},{34,2},{3,35},{35,3},{4,36},{36... | collective-permute-start | bytes 6291464 | tf_op jit(solution)/shard_map/ppermute | solution.py:23
  48.3 3.9 %collective-permute-done = f32[512,1024]{1,0:T(8,128)} collective-permute-done((f32[512,1024]{1,0:T(8,128)S(1)}, f32[512,1024]{1,0:T(8,128)}, u32[]{:S(2)}, u32[]{:S(2)}) %collective-permute-start) | collective-permute-done | bytes 2097184 | tf_op jit(solution)/shard_map/ppermute | solution.py:23
  52.2 2.6 %bitcast_add_fusion = f32[512,1024]{1,0:T(8,128)S(1)} fusion(f32[512,1024]{1,0:T(8,128)} %collective-permute-done, f32[2,512,1024]{2,1,0:T(8,128)} %bitcast.56, s32[]{:T(128)S(6)} %select_n.107), kind=kLoop, calls=%fused_computation.1 | loop fusion | flops 524288 | bytes 6291460 | tf_op jit(solution)/shard_map/add | solution.py:48
  54.9 5.1 %collective-permute-start.4 = (f32[64,1024]{1,0:T(8,128)S(1)}, f32[64,1024]{1,0:T(8,128)S(1)}, u32[]{:S(2)}, u32[]{:S(2)}) collective-permute-start(f32[64,1024]{1,0:T(8,128)S(1)} %get-tuple-element.9), channel_id=1, source_target_pairs={{0,448},{64,0},{128,64},{192,128},{256,192},{320,256},{384,320},{4... | collective-permute-start | bytes 786440 | tf_op jit(solution)/shard_map/ppermute | solution.py:23
  60.0 1.9 %collective-permute-start.1 = (f32[64,1024]{1,0:T(8,128)S(1)}, f32[64,1024]{1,0:T(8,128)S(1)}, u32[]{:S(2)}, u32[]{:S(2)}) collective-permute-start(f32[64,1024]{1,0:T(8,128)S(1)} %get-tuple-element.10), channel_id=1, source_target_pairs={{0,64},{64,128},{128,192},{192,256},{256,320},{320,384},{384,448},... | collective-permute-start | bytes 786440 | tf_op jit(solution)/shard_map/ppermute | solution.py:23
  61.9 3.3 %collective-permute-done.4 = f32[64,1024]{1,0:T(8,128)S(1)} collective-permute-done((f32[64,1024]{1,0:T(8,128)S(1)}, f32[64,1024]{1,0:T(8,128)S(1)}, u32[]{:S(2)}, u32[]{:S(2)}) %collective-permute-start.4) | collective-permute-done | bytes 262176 | tf_op jit(solution)/shard_map/ppermute | solution.py:23
  65.3 5.3 %collective-permute-start.5 = (f32[64,1024]{1,0:T(8,128)S(1)}, f32[64,1024]{1,0:T(8,128)S(1)}, u32[]{:S(2)}, u32[]{:S(2)}) collective-permute-start(f32[64,1024]{1,0:T(8,128)S(1)} %bitcast_add_fusion.4), channel_id=1, source_target_pairs={{0,448},{64,0},{128,64},{192,128},{256,192},{320,256},{384,320},{4... | collective-permute-start | bytes 786440 | tf_op jit(solution)/shard_map/ppermute | solution.py:23
  70.6 0.0 collective-permute-done.1
  70.6 4.4 %collective-permute-done.5 = f32[64,1024]{1,0:T(8,128)S(1)} collective-permute-done((f32[64,1024]{1,0:T(8,128)S(1)}, f32[64,1024]{1,0:T(8,128)S(1)}, u32[]{:S(2)}, u32[]{:S(2)}) %collective-permute-start.5) | collective-permute-done | bytes 262176 | tf_op jit(solution)/shard_map/ppermute | solution.py:23
  75.0 0.1 bitcast_add_fusion.3
  75.1 5.3 %collective-permute-start.6 = (f32[64,1024]{1,0:T(8,128)S(1)}, f32[64,1024]{1,0:T(8,128)S(1)}, u32[]{:S(2)}, u32[]{:S(2)}) collective-permute-start(f32[64,1024]{1,0:T(8,128)S(1)} %get-tuple-element.7), channel_id=1, source_target_pairs={{0,448},{64,0},{128,64},{192,128},{256,192},{320,256},{384,320},{4... | collective-permute-start | bytes 786440 | tf_op jit(solution)/shard_map/ppermute | solution.py:23
  80.4 1.9 %collective-permute-start.2 = (f32[64,1024]{1,0:T(8,128)S(1)}, f32[64,1024]{1,0:T(8,128)S(1)}, u32[]{:S(2)}, u32[]{:S(2)}) collective-permute-start(f32[64,1024]{1,0:T(8,128)S(1)} %get-tuple-element.8), channel_id=1, source_target_pairs={{0,64},{64,128},{128,192},{192,256},{256,320},{320,384},{384,448},... | collective-permute-start | bytes 786440 | tf_op jit(solution)/shard_map/ppermute | solution.py:23
  82.4 0.0 copy-start.5
  82.4 1.6 collective-permute-done.6
  84.0 4.8 %collective-permute-done.2 = f32[64,1024]{1,0:T(8,128)S(1)} collective-permute-done((f32[64,1024]{1,0:T(8,128)S(1)}, f32[64,1024]{1,0:T(8,128)S(1)}, u32[]{:S(2)}, u32[]{:S(2)}) %collective-permute-start.2) | collective-permute-done | bytes 262176 | tf_op jit(solution)/shard_map/ppermute | solution.py:23
  88.7 0.1 bitcast_add_fusion.2
  88.8 1.9 %collective-permute-start.3 = (f32[64,1024]{1,0:T(8,128)S(1)}, f32[64,1024]{1,0:T(8,128)S(1)}, u32[]{:S(2)}, u32[]{:S(2)}) collective-permute-start(f32[64,1024]{1,0:T(8,128)S(1)} %get-tuple-element.6), channel_id=1, source_target_pairs={{0,64},{64,128},{128,192},{192,256},{256,320},{320,384},{384,448},... | collective-permute-start | bytes 786440 | tf_op jit(solution)/shard_map/ppermute | solution.py:23
  90.7 4.6 %collective-permute-start.7 = (f32[64,1024]{1,0:T(8,128)S(1)}, f32[64,1024]{1,0:T(8,128)S(1)}, u32[]{:S(2)}, u32[]{:S(2)}) collective-permute-start(f32[64,1024]{1,0:T(8,128)S(1)} %get-tuple-element.5), channel_id=1, source_target_pairs={{0,448},{64,0},{128,64},{192,128},{256,192},{320,256},{384,320},{4... | collective-permute-start | bytes 786440 | tf_op jit(solution)/shard_map/ppermute | solution.py:23
  95.3 1.8 %collective-permute-done.3 = f32[64,1024]{1,0:T(8,128)S(1)} collective-permute-done((f32[64,1024]{1,0:T(8,128)S(1)}, f32[64,1024]{1,0:T(8,128)S(1)}, u32[]{:S(2)}, u32[]{:S(2)}) %collective-permute-start.3) | collective-permute-done | bytes 262176 | tf_op jit(solution)/shard_map/ppermute | solution.py:23
  97.1 1.5 collective-permute-done.7
  98.8 16.5 %all_to_all.40 = bf16[8,64,512]{2,1,0:T(8,128)(2,1)S(1)} all-to-all(bf16[8,64,512]{2,1,0:T(8,128)(2,1)S(1)} %broadcast_in_dim.54), channel_id=1, replica_groups=mesh['y'=8,'c'=2,'z'=8,'x'=4] {'y'}, dimensions={0} | all-to-all | bytes 1048576 | tf_op jit(solution)/shard_map/all_to_all | solution.py:69
  115.2 8.3 %collective-permute-start.8 = (bf16[512,512]{1,0:T(8,128)(2,1)S(1)}, bf16[512,512]{1,0:T(8,128)(2,1)S(1)}, u32[]{:S(2)}, u32[]{:S(2)}) collective-permute-start(bf16[512,512]{1,0:T(8,128)(2,1)S(1)} %bitcast.66), channel_id=1, source_target_pairs={{0,32},{32,0},{1,33},{33,1},{2,34},{34,2},{3,35},{35,3},{4,36},{36... | collective-permute-start | bytes 1572872 | tf_op jit(solution)/shard_map/ppermute | solution.py:23
  123.6 1.4 collective-permute-done.8
  125.1 0.1 pad_maximum_fusion
  125.2 0.6 gather_fusion
  125.8 0.0 copy-start.6
  125.8 0.2 select_bitcast_fusion
  126.0 0.1 copy.11
  126.1 0.2 broadcast_in_dim.56
  126.3 0.6 copy-done.6
  126.8 0.7 convolution_convert_fusion
  127.5 17.2 %all_to_all.41 = bf16[4,256,512]{2,1,0:T(8,128)(2,1)S(1)} all-to-all(bf16[4,256,512]{2,1,0:T(8,128)(2,1)S(1)} %bitcast.72), channel_id=1, replica_groups=mesh['y'=8,'c'=2,'z'=8,'x'=4] {'x'}, dimensions={0} | all-to-all | bytes 2097152 | tf_op jit(solution)/shard_map/all_to_all | solution.py:74
  144.8 0.1 convert_reduce_fusion
  144.9 17.9 %all_to_all.42 = f32[8,32,512]{2,1,0:T(8,128)S(1)} all-to-all(f32[8,32,512]{2,1,0:T(8,128)S(1)} %bitcast.65), channel_id=1, replica_groups=mesh['y'=8,'c'=2,'z'=8,'x'=4] {'z'}, dimensions={0} | all-to-all | bytes 1048576 | tf_op jit(solution)/shard_map/all_to_all | solution.py:74
  162.8 0.7 reduce_sum.19
  (20 shorter events, 0.3 us)
Async XLA Ops:
  0.0 27.0 %copy-start.3 = (s32[4,4]{1,0:T(4,128)S(1)}, s32[4,4]{1,0:T(4,128)}, u32[]{:S(2)}) copy-start(s32[4,4]{1,0:T(4,128)} %param.12) | copy-start | bytes 196
  0.0 27.0 %copy-start.4 = (s32[4,4]{1,0:T(4,128)S(1)}, s32[4,4]{1,0:T(4,128)}, u32[]{:S(2)}) copy-start(s32[4,4]{1,0:T(4,128)} %param.11) | copy-start | bytes 196
  22.0 5.5 %copy-start.1 = (bf16[512,512]{1,0:T(8,128)(2,1)S(1)}, bf16[512,512]{1,0:T(8,128)(2,1)}, u32[]{:S(2)}) copy-start(bf16[512,512]{1,0:T(8,128)(2,1)} %param.9) | copy-start | bytes 1572868
  22.0 5.5 %copy-start.2 = (bf16[512,512]{1,0:T(8,128)(2,1)S(1)}, bf16[512,512]{1,0:T(8,128)(2,1)}, u32[]{:S(2)}) copy-start(bf16[512,512]{1,0:T(8,128)(2,1)} %param.8) | copy-start | bytes 1572868
  23.0 16.3 %all-to-all-start.1 = ((bf16[4,256,512]{2,1,0:T(8,128)(2,1)}), bf16[4,256,512]{2,1,0:T(8,128)(2,1)S(1)}, u32[]{:S(2)}, u32[]{:S(2)}) async-start(bf16[4,256,512]{2,1,0:T(8,128)(2,1)} %broadcast_in_dim.26), calls=%async_computation.1 | async-start | bytes 2097152 | tf_op jit(solution)/shard_map/all_to_all | solution.py:69
  40.6 2.0 %copy-start = (f32[1024,1024]{0,1:T(8,128)}, f32[1024,1024]{0,1:T(8,128)S(1)}, u32[]{:S(2)}) copy-start(f32[1024,1024]{0,1:T(8,128)S(1)} %fusion) | copy-start | bytes 12582916
  42.6 9.6 %collective-permute-start = (f32[512,1024]{1,0:T(8,128)S(1)}, f32[512,1024]{1,0:T(8,128)}, u32[]{:S(2)}, u32[]{:S(2)}) collective-permute-start(f32[512,1024]{1,0:T(8,128)S(1)} %dynamic-slice_bitcast_fusion), channel_id=1, source_target_pairs={{0,32},{32,0},{1,33},{33,1},{2,34},{34,2},{3,35},{35,3},{4,36},{36... | collective-permute-start | bytes 6291464 | tf_op jit(solution)/shard_map/ppermute | solution.py:23
  54.9 10.4 %collective-permute-start.4 = (f32[64,1024]{1,0:T(8,128)S(1)}, f32[64,1024]{1,0:T(8,128)S(1)}, u32[]{:S(2)}, u32[]{:S(2)}) collective-permute-start(f32[64,1024]{1,0:T(8,128)S(1)} %get-tuple-element.9), channel_id=1, source_target_pairs={{0,448},{64,0},{128,64},{192,128},{256,192},{320,256},{384,320},{4... | collective-permute-start | bytes 786440 | tf_op jit(solution)/shard_map/ppermute | solution.py:23
  60.0 10.6 %collective-permute-start.1 = (f32[64,1024]{1,0:T(8,128)S(1)}, f32[64,1024]{1,0:T(8,128)S(1)}, u32[]{:S(2)}, u32[]{:S(2)}) collective-permute-start(f32[64,1024]{1,0:T(8,128)S(1)} %get-tuple-element.10), channel_id=1, source_target_pairs={{0,64},{64,128},{128,192},{192,256},{256,320},{320,384},{384,448},... | collective-permute-start | bytes 786440 | tf_op jit(solution)/shard_map/ppermute | solution.py:23
  65.3 9.7 %collective-permute-start.5 = (f32[64,1024]{1,0:T(8,128)S(1)}, f32[64,1024]{1,0:T(8,128)S(1)}, u32[]{:S(2)}, u32[]{:S(2)}) collective-permute-start(f32[64,1024]{1,0:T(8,128)S(1)} %bitcast_add_fusion.4), channel_id=1, source_target_pairs={{0,448},{64,0},{128,64},{192,128},{256,192},{320,256},{384,320},{4... | collective-permute-start | bytes 786440 | tf_op jit(solution)/shard_map/ppermute | solution.py:23
  75.1 8.9 %collective-permute-start.6 = (f32[64,1024]{1,0:T(8,128)S(1)}, f32[64,1024]{1,0:T(8,128)S(1)}, u32[]{:S(2)}, u32[]{:S(2)}) collective-permute-start(f32[64,1024]{1,0:T(8,128)S(1)} %get-tuple-element.7), channel_id=1, source_target_pairs={{0,448},{64,0},{128,64},{192,128},{256,192},{320,256},{384,320},{4... | collective-permute-start | bytes 786440 | tf_op jit(solution)/shard_map/ppermute | solution.py:23
  80.4 8.3 %collective-permute-start.2 = (f32[64,1024]{1,0:T(8,128)S(1)}, f32[64,1024]{1,0:T(8,128)S(1)}, u32[]{:S(2)}, u32[]{:S(2)}) collective-permute-start(f32[64,1024]{1,0:T(8,128)S(1)} %get-tuple-element.8), channel_id=1, source_target_pairs={{0,64},{64,128},{128,192},{192,256},{256,320},{320,384},{384,448},... | collective-permute-start | bytes 786440 | tf_op jit(solution)/shard_map/ppermute | solution.py:23
  82.4 41.2 %copy-start.5 = (s32[4,4]{1,0:T(4,128)S(1)}, s32[4,4]{1,0:T(4,128)}, u32[]{:S(2)}) copy-start(s32[4,4]{1,0:T(4,128)} %param.13) | copy-start | bytes 196
  88.8 8.3 %collective-permute-start.3 = (f32[64,1024]{1,0:T(8,128)S(1)}, f32[64,1024]{1,0:T(8,128)S(1)}, u32[]{:S(2)}, u32[]{:S(2)}) collective-permute-start(f32[64,1024]{1,0:T(8,128)S(1)} %get-tuple-element.6), channel_id=1, source_target_pairs={{0,64},{64,128},{128,192},{192,256},{256,320},{320,384},{384,448},... | collective-permute-start | bytes 786440 | tf_op jit(solution)/shard_map/ppermute | solution.py:23
  90.7 7.9 %collective-permute-start.7 = (f32[64,1024]{1,0:T(8,128)S(1)}, f32[64,1024]{1,0:T(8,128)S(1)}, u32[]{:S(2)}, u32[]{:S(2)}) collective-permute-start(f32[64,1024]{1,0:T(8,128)S(1)} %get-tuple-element.5), channel_id=1, source_target_pairs={{0,448},{64,0},{128,64},{192,128},{256,192},{320,256},{384,320},{4... | collective-permute-start | bytes 786440 | tf_op jit(solution)/shard_map/ppermute | solution.py:23
  115.2 9.8 %collective-permute-start.8 = (bf16[512,512]{1,0:T(8,128)(2,1)S(1)}, bf16[512,512]{1,0:T(8,128)(2,1)S(1)}, u32[]{:S(2)}, u32[]{:S(2)}) collective-permute-start(bf16[512,512]{1,0:T(8,128)(2,1)S(1)} %bitcast.66), channel_id=1, source_target_pairs={{0,32},{32,0},{1,33},{33,1},{2,34},{34,2},{3,35},{35,3},{4,36},{36... | collective-permute-start | bytes 1572872 | tf_op jit(solution)/shard_map/ppermute | solution.py:23
  125.8 1.0 copy-start.6

commit v12 on v11

--- a/solution.py
+++ b/solution.py
@@ -93,7 +93,7 @@
     both = gather_pair(half, "c")
     hidden = both.reshape(n_c, n_y, share, -1).transpose(1, 0, 2, 3).reshape(rows, -1)
     partial_out = jnp.dot(hidden, down_eff, preferred_element_type=jnp.float32)
-    partial_out = scatter_sum_a2a(scatter_sum_a2a(partial_out, "x", sent=jnp.bfloat16), "z")
+    partial_out = scatter_sum_a2a(partial_out, ("x", "z"), sent=jnp.bfloat16)
     return partial_out.astype(jnp.bfloat16)
 
 

time: 165 us -> 160 us (0.970)
  blocking collectives: 72.7 us -> 66.3 us
    all_to_all x2 -> x1, blocking collectives: 35.1 us -> 28.7 us  [scatter_sum_a2a(): got = lax.all_to_all(x.astype(sent), axis, 0, 0, tiled=True)]
where the time goes in v12:
time: 160 us; the launch traced here: 157 us
  blocking collectives  66.3 us (41%)
  starting transfers between devices  44 us (28%)
  waiting for transfers between devices  34.3 us (21%)
  local copies, waits for them, and re-layouts  5.86 us (4%)
  other arithmetic  4.1 us (3%)
  matrix products  1.97 us (1%)
    ppermute x9, starting transfers between devices, shift(): return lax.ppermute(x, axis, [(s, (s + step) % n) for s in range(n)])  40 us
    all_to_all x2, blocking collectives, gather_a2a(): return lax.all_to_all(copies, axis, 0, 0, tiled=True)  37.6 us
    all_to_all x1, blocking collectives, scatter_sum_a2a(): got = lax.all_to_all(x.astype(sent), axis, 0, 0, tiled=True)  28.7 us
    ppermute x9, waiting for transfers between devices, shift(): return lax.ppermute(x, axis, [(s, (s + step) % n) for s in range(n)])  22.6 us
    all_to_all x1, waiting for transfers between devices, gather_a2a(): return lax.all_to_all(copies, axis, 0, 0, tiled=True)  11.7 us
    all_to_all x1, starting transfers between devices, gather_a2a(): return lax.all_to_all(copies, axis, 0, 0, tiled=True)  4.01 us
  transfers between devices with their start and end apart: 10, of which 9 were waited for; matrix products, arithmetic and copies ran while one was open for 0% of the time, Pallas kernels for 0%

profile of v12, /device:TPU:1, one launch (start us, length us, event | category | flops | bytes accessed | tf_op | source)
XLA Modules:
  0.0 157.0 jit_solution(11162143453083063781)
XLA Ops:
  0.0 0.8 broadcast_in_dim.24
  0.8 21.1 %all_to_all.30 = bf16[8,32,512]{2,1,0:T(8,128)(2,1)S(1)} all-to-all(bf16[8,32,512]{2,1,0:T(8,128)(2,1)S(1)} %broadcast_in_dim.24), channel_id=1, replica_groups=mesh['y'=8,'c'=2,'z'=8,'x'=4] {'z'}, dimensions={0} | all-to-all | bytes 524288 | tf_op jit(solution)/shard_map/all_to_all | solution.py:69
  22.0 1.1 broadcast_in_dim.26
  23.0 4.0 %all-to-all-start.1 = ((bf16[4,256,512]{2,1,0:T(8,128)(2,1)}), bf16[4,256,512]{2,1,0:T(8,128)(2,1)S(1)}, u32[]{:S(2)}, u32[]{:S(2)}) async-start(bf16[4,256,512]{2,1,0:T(8,128)(2,1)} %broadcast_in_dim.26), calls=%async_computation.1 | async-start | bytes 2097152 | tf_op jit(solution)/shard_map/all_to_all | solution.py:69
  27.0 0.0 copy-done.3
  27.0 0.0 copy-done.4
  27.1 0.2 broadcast_in_dim.23
  27.3 0.2 broadcast_in_dim.22
  27.5 0.2 bitcast_multiply_fusion.2
  27.7 11.7 %all-to-all-done.1 = bf16[4,256,512]{2,1,0:T(8,128)(2,1)S(1)} async-done(((bf16[4,256,512]{2,1,0:T(8,128)(2,1)}), bf16[4,256,512]{2,1,0:T(8,128)(2,1)S(1)}, u32[]{:S(2)}, u32[]{:S(2)}) %all-to-all-start.1) | async-done | bytes 1048608 | tf_op jit(solution)/shard_map/all_to_all | solution.py:69
  39.3 0.1 copy.8
  39.4 1.2 fusion
  40.7 0.2 dynamic-slice_bitcast_fusion
  40.9 1.7 %copy-done = f32[1024,1024]{0,1:T(8,128)} copy-done((f32[1024,1024]{0,1:T(8,128)}, f32[1024,1024]{0,1:T(8,128)S(1)}, u32[]{:S(2)}) %copy-start) | copy-done | bytes 4194328
  42.6 5.7 %collective-permute-start = (f32[512,1024]{1,0:T(8,128)S(1)}, f32[512,1024]{1,0:T(8,128)}, u32[]{:S(2)}, u32[]{:S(2)}) collective-permute-start(f32[512,1024]{1,0:T(8,128)S(1)} %dynamic-slice_bitcast_fusion), channel_id=1, source_target_pairs={{0,32},{32,0},{1,33},{33,1},{2,34},{34,2},{3,35},{35,3},{4,36},{36... | collective-permute-start | bytes 6291464 | tf_op jit(solution)/shard_map/ppermute | solution.py:23
  48.3 3.9 %collective-permute-done = f32[512,1024]{1,0:T(8,128)} collective-permute-done((f32[512,1024]{1,0:T(8,128)S(1)}, f32[512,1024]{1,0:T(8,128)}, u32[]{:S(2)}, u32[]{:S(2)}) %collective-permute-start) | collective-permute-done | bytes 2097184 | tf_op jit(solution)/shard_map/ppermute | solution.py:23
  52.2 2.6 %bitcast_add_fusion = f32[512,1024]{1,0:T(8,128)S(1)} fusion(f32[512,1024]{1,0:T(8,128)} %collective-permute-done, f32[2,512,1024]{2,1,0:T(8,128)} %bitcast.55, s32[]{:T(128)S(6)} %select_n.107), kind=kLoop, calls=%fused_computation.1 | loop fusion | flops 524288 | bytes 6291460 | tf_op jit(solution)/shard_map/add | solution.py:48
  54.8 5.1 %collective-permute-start.4 = (f32[64,1024]{1,0:T(8,128)S(1)}, f32[64,1024]{1,0:T(8,128)S(1)}, u32[]{:S(2)}, u32[]{:S(2)}) collective-permute-start(f32[64,1024]{1,0:T(8,128)S(1)} %get-tuple-element.9), channel_id=1, source_target_pairs={{0,448},{64,0},{128,64},{192,128},{256,192},{320,256},{384,320},{4... | collective-permute-start | bytes 786440 | tf_op jit(solution)/shard_map/ppermute | solution.py:23
  60.0 1.9 %collective-permute-start.1 = (f32[64,1024]{1,0:T(8,128)S(1)}, f32[64,1024]{1,0:T(8,128)S(1)}, u32[]{:S(2)}, u32[]{:S(2)}) collective-permute-start(f32[64,1024]{1,0:T(8,128)S(1)} %get-tuple-element.10), channel_id=1, source_target_pairs={{0,64},{64,128},{128,192},{192,256},{256,320},{320,384},{384,448},... | collective-permute-start | bytes 786440 | tf_op jit(solution)/shard_map/ppermute | solution.py:23
  61.9 3.3 %collective-permute-done.4 = f32[64,1024]{1,0:T(8,128)S(1)} collective-permute-done((f32[64,1024]{1,0:T(8,128)S(1)}, f32[64,1024]{1,0:T(8,128)S(1)}, u32[]{:S(2)}, u32[]{:S(2)}) %collective-permute-start.4) | collective-permute-done | bytes 262176 | tf_op jit(solution)/shard_map/ppermute | solution.py:23
  65.2 5.3 %collective-permute-start.5 = (f32[64,1024]{1,0:T(8,128)S(1)}, f32[64,1024]{1,0:T(8,128)S(1)}, u32[]{:S(2)}, u32[]{:S(2)}) collective-permute-start(f32[64,1024]{1,0:T(8,128)S(1)} %bitcast_add_fusion.4), channel_id=1, source_target_pairs={{0,448},{64,0},{128,64},{192,128},{256,192},{320,256},{384,320},{4... | collective-permute-start | bytes 786440 | tf_op jit(solution)/shard_map/ppermute | solution.py:23
  70.6 0.0 collective-permute-done.1
  70.6 4.4 %collective-permute-done.5 = f32[64,1024]{1,0:T(8,128)S(1)} collective-permute-done((f32[64,1024]{1,0:T(8,128)S(1)}, f32[64,1024]{1,0:T(8,128)S(1)}, u32[]{:S(2)}, u32[]{:S(2)}) %collective-permute-start.5) | collective-permute-done | bytes 262176 | tf_op jit(solution)/shard_map/ppermute | solution.py:23
  75.0 0.1 bitcast_add_fusion.3
  75.1 5.3 %collective-permute-start.6 = (f32[64,1024]{1,0:T(8,128)S(1)}, f32[64,1024]{1,0:T(8,128)S(1)}, u32[]{:S(2)}, u32[]{:S(2)}) collective-permute-start(f32[64,1024]{1,0:T(8,128)S(1)} %get-tuple-element.7), channel_id=1, source_target_pairs={{0,448},{64,0},{128,64},{192,128},{256,192},{320,256},{384,320},{4... | collective-permute-start | bytes 786440 | tf_op jit(solution)/shard_map/ppermute | solution.py:23
  80.4 1.9 %collective-permute-start.2 = (f32[64,1024]{1,0:T(8,128)S(1)}, f32[64,1024]{1,0:T(8,128)S(1)}, u32[]{:S(2)}, u32[]{:S(2)}) collective-permute-start(f32[64,1024]{1,0:T(8,128)S(1)} %get-tuple-element.8), channel_id=1, source_target_pairs={{0,64},{64,128},{128,192},{192,256},{256,320},{320,384},{384,448},... | collective-permute-start | bytes 786440 | tf_op jit(solution)/shard_map/ppermute | solution.py:23
  82.4 0.0 copy-start.5
  82.4 1.6 %collective-permute-done.6 = f32[64,1024]{1,0:T(8,128)S(1)} collective-permute-done((f32[64,1024]{1,0:T(8,128)S(1)}, f32[64,1024]{1,0:T(8,128)S(1)}, u32[]{:S(2)}, u32[]{:S(2)}) %collective-permute-start.6) | collective-permute-done | bytes 262176 | tf_op jit(solution)/shard_map/ppermute | solution.py:23
  84.0 4.8 %collective-permute-done.2 = f32[64,1024]{1,0:T(8,128)S(1)} collective-permute-done((f32[64,1024]{1,0:T(8,128)S(1)}, f32[64,1024]{1,0:T(8,128)S(1)}, u32[]{:S(2)}, u32[]{:S(2)}) %collective-permute-start.2) | collective-permute-done | bytes 262176 | tf_op jit(solution)/shard_map/ppermute | solution.py:23
  88.7 0.1 bitcast_add_fusion.2
  88.8 1.9 %collective-permute-start.3 = (f32[64,1024]{1,0:T(8,128)S(1)}, f32[64,1024]{1,0:T(8,128)S(1)}, u32[]{:S(2)}, u32[]{:S(2)}) collective-permute-start(f32[64,1024]{1,0:T(8,128)S(1)} %get-tuple-element.6), channel_id=1, source_target_pairs={{0,64},{64,128},{128,192},{192,256},{256,320},{320,384},{384,448},... | collective-permute-start | bytes 786440 | tf_op jit(solution)/shard_map/ppermute | solution.py:23
  90.7 4.6 %collective-permute-start.7 = (f32[64,1024]{1,0:T(8,128)S(1)}, f32[64,1024]{1,0:T(8,128)S(1)}, u32[]{:S(2)}, u32[]{:S(2)}) collective-permute-start(f32[64,1024]{1,0:T(8,128)S(1)} %get-tuple-element.5), channel_id=1, source_target_pairs={{0,448},{64,0},{128,64},{192,128},{256,192},{320,256},{384,320},{4... | collective-permute-start | bytes 786440 | tf_op jit(solution)/shard_map/ppermute | solution.py:23
  95.3 1.8 %collective-permute-done.3 = f32[64,1024]{1,0:T(8,128)S(1)} collective-permute-done((f32[64,1024]{1,0:T(8,128)S(1)}, f32[64,1024]{1,0:T(8,128)S(1)}, u32[]{:S(2)}, u32[]{:S(2)}) %collective-permute-start.3) | collective-permute-done | bytes 262176 | tf_op jit(solution)/shard_map/ppermute | solution.py:23
  97.1 1.5 collective-permute-done.7
  98.7 16.5 %all_to_all.31 = bf16[8,64,512]{2,1,0:T(8,128)(2,1)S(1)} all-to-all(bf16[8,64,512]{2,1,0:T(8,128)(2,1)S(1)} %broadcast_in_dim.54), channel_id=1, replica_groups=mesh['y'=8,'c'=2,'z'=8,'x'=4] {'y'}, dimensions={0} | all-to-all | bytes 1048576 | tf_op jit(solution)/shard_map/all_to_all | solution.py:69
  115.2 8.3 %collective-permute-start.8 = (bf16[512,512]{1,0:T(8,128)(2,1)S(1)}, bf16[512,512]{1,0:T(8,128)(2,1)S(1)}, u32[]{:S(2)}, u32[]{:S(2)}) collective-permute-start(bf16[512,512]{1,0:T(8,128)(2,1)S(1)} %bitcast.64), channel_id=1, source_target_pairs={{0,32},{32,0},{1,33},{33,1},{2,34},{34,2},{3,35},{35,3},{4,36},{36... | collective-permute-start | bytes 1572872 | tf_op jit(solution)/shard_map/ppermute | solution.py:23
  123.5 0.0 copy-done.5
  123.6 1.4 collective-permute-done.8
  125.0 0.1 pad_maximum_fusion
  125.1 0.6 gather_fusion
  125.8 0.0 copy-start.6
  125.8 0.2 select_bitcast_fusion
  125.9 0.1 copy.9
  126.0 0.2 broadcast_in_dim.56
  126.3 0.6 copy-done.6
  126.8 0.7 convolution_convert_fusion
  127.5 28.7 %all_to_all.32 = bf16[32,32,512]{2,1,0:T(8,128)(2,1)S(1)} all-to-all(bf16[32,32,512]{2,1,0:T(8,128)(2,1)S(1)} %bitcast.70), channel_id=1, replica_groups=mesh['y'=8,'c'=2,'z'=8,'x'=4] {'x','z'}, dimensions={0} | all-to-all | bytes 2097152 | tf_op jit(solution)/shard_map/all_to_all | solution.py:74
  156.3 0.8 reduce_sum.12
  (18 shorter events, 0.3 us)
Async XLA Ops:
  0.0 27.0 %copy-start.3 = (s32[4,4]{1,0:T(4,128)S(1)}, s32[4,4]{1,0:T(4,128)}, u32[]{:S(2)}) copy-start(s32[4,4]{1,0:T(4,128)} %param.12) | copy-start | bytes 196
  0.0 27.0 %copy-start.4 = (s32[4,4]{1,0:T(4,128)S(1)}, s32[4,4]{1,0:T(4,128)}, u32[]{:S(2)}) copy-start(s32[4,4]{1,0:T(4,128)} %param.11) | copy-start | bytes 196
  22.0 5.5 %copy-start.1 = (bf16[512,512]{1,0:T(8,128)(2,1)S(1)}, bf16[512,512]{1,0:T(8,128)(2,1)}, u32[]{:S(2)}) copy-start(bf16[512,512]{1,0:T(8,128)(2,1)} %param.9) | copy-start | bytes 1572868
  22.0 5.5 %copy-start.2 = (bf16[512,512]{1,0:T(8,128)(2,1)S(1)}, bf16[512,512]{1,0:T(8,128)(2,1)}, u32[]{:S(2)}) copy-start(bf16[512,512]{1,0:T(8,128)(2,1)} %param.8) | copy-start | bytes 1572868
  23.0 16.3 %all-to-all-start.1 = ((bf16[4,256,512]{2,1,0:T(8,128)(2,1)}), bf16[4,256,512]{2,1,0:T(8,128)(2,1)S(1)}, u32[]{:S(2)}, u32[]{:S(2)}) async-start(bf16[4,256,512]{2,1,0:T(8,128)(2,1)} %broadcast_in_dim.26), calls=%async_computation.1 | async-start | bytes 2097152 | tf_op jit(solution)/shard_map/all_to_all | solution.py:69
  40.6 2.0 %copy-start = (f32[1024,1024]{0,1:T(8,128)}, f32[1024,1024]{0,1:T(8,128)S(1)}, u32[]{:S(2)}) copy-start(f32[1024,1024]{0,1:T(8,128)S(1)} %fusion) | copy-start | bytes 12582916
  42.6 9.6 %collective-permute-start = (f32[512,1024]{1,0:T(8,128)S(1)}, f32[512,1024]{1,0:T(8,128)}, u32[]{:S(2)}, u32[]{:S(2)}) collective-permute-start(f32[512,1024]{1,0:T(8,128)S(1)} %dynamic-slice_bitcast_fusion), channel_id=1, source_target_pairs={{0,32},{32,0},{1,33},{33,1},{2,34},{34,2},{3,35},{35,3},{4,36},{36... | collective-permute-start | bytes 6291464 | tf_op jit(solution)/shard_map/ppermute | solution.py:23
  54.8 10.4 %collective-permute-start.4 = (f32[64,1024]{1,0:T(8,128)S(1)}, f32[64,1024]{1,0:T(8,128)S(1)}, u32[]{:S(2)}, u32[]{:S(2)}) collective-permute-start(f32[64,1024]{1,0:T(8,128)S(1)} %get-tuple-element.9), channel_id=1, source_target_pairs={{0,448},{64,0},{128,64},{192,128},{256,192},{320,256},{384,320},{4... | collective-permute-start | bytes 786440 | tf_op jit(solution)/shard_map/ppermute | solution.py:23
  60.0 10.6 %collective-permute-start.1 = (f32[64,1024]{1,0:T(8,128)S(1)}, f32[64,1024]{1,0:T(8,128)S(1)}, u32[]{:S(2)}, u32[]{:S(2)}) collective-permute-start(f32[64,1024]{1,0:T(8,128)S(1)} %get-tuple-element.10), channel_id=1, source_target_pairs={{0,64},{64,128},{128,192},{192,256},{256,320},{320,384},{384,448},... | collective-permute-start | bytes 786440 | tf_op jit(solution)/shard_map/ppermute | solution.py:23
  65.2 9.7 %collective-permute-start.5 = (f32[64,1024]{1,0:T(8,128)S(1)}, f32[64,1024]{1,0:T(8,128)S(1)}, u32[]{:S(2)}, u32[]{:S(2)}) collective-permute-start(f32[64,1024]{1,0:T(8,128)S(1)} %bitcast_add_fusion.4), channel_id=1, source_target_pairs={{0,448},{64,0},{128,64},{192,128},{256,192},{320,256},{384,320},{4... | collective-permute-start | bytes 786440 | tf_op jit(solution)/shard_map/ppermute | solution.py:23
  75.1 8.9 %collective-permute-start.6 = (f32[64,1024]{1,0:T(8,128)S(1)}, f32[64,1024]{1,0:T(8,128)S(1)}, u32[]{:S(2)}, u32[]{:S(2)}) collective-permute-start(f32[64,1024]{1,0:T(8,128)S(1)} %get-tuple-element.7), channel_id=1, source_target_pairs={{0,448},{64,0},{128,64},{192,128},{256,192},{320,256},{384,320},{4... | collective-permute-start | bytes 786440 | tf_op jit(solution)/shard_map/ppermute | solution.py:23
  80.4 8.3 %collective-permute-start.2 = (f32[64,1024]{1,0:T(8,128)S(1)}, f32[64,1024]{1,0:T(8,128)S(1)}, u32[]{:S(2)}, u32[]{:S(2)}) collective-permute-start(f32[64,1024]{1,0:T(8,128)S(1)} %get-tuple-element.8), channel_id=1, source_target_pairs={{0,64},{64,128},{128,192},{192,256},{256,320},{320,384},{384,448},... | collective-permute-start | bytes 786440 | tf_op jit(solution)/shard_map/ppermute | solution.py:23
  82.4 41.2 %copy-start.5 = (s32[4,4]{1,0:T(4,128)S(1)}, s32[4,4]{1,0:T(4,128)}, u32[]{:S(2)}) copy-start(s32[4,4]{1,0:T(4,128)} %param.13) | copy-start | bytes 196
  88.8 8.3 %collective-permute-start.3 = (f32[64,1024]{1,0:T(8,128)S(1)}, f32[64,1024]{1,0:T(8,128)S(1)}, u32[]{:S(2)}, u32[]{:S(2)}) collective-permute-start(f32[64,1024]{1,0:T(8,128)S(1)} %get-tuple-element.6), channel_id=1, source_target_pairs={{0,64},{64,128},{128,192},{192,256},{256,320},{320,384},{384,448},... | collective-permute-start | bytes 786440 | tf_op jit(solution)/shard_map/ppermute | solution.py:23
  90.7 7.9 %collective-permute-start.7 = (f32[64,1024]{1,0:T(8,128)S(1)}, f32[64,1024]{1,0:T(8,128)S(1)}, u32[]{:S(2)}, u32[]{:S(2)}) collective-permute-start(f32[64,1024]{1,0:T(8,128)S(1)} %get-tuple-element.5), channel_id=1, source_target_pairs={{0,448},{64,0},{128,64},{192,128},{256,192},{320,256},{384,320},{4... | collective-permute-start | bytes 786440 | tf_op jit(solution)/shard_map/ppermute | solution.py:23
  115.2 9.8 %collective-permute-start.8 = (bf16[512,512]{1,0:T(8,128)(2,1)S(1)}, bf16[512,512]{1,0:T(8,128)(2,1)S(1)}, u32[]{:S(2)}, u32[]{:S(2)}) collective-permute-start(bf16[512,512]{1,0:T(8,128)(2,1)S(1)} %bitcast.64), channel_id=1, source_target_pairs={{0,32},{32,0},{1,33},{33,1},{2,34},{34,2},{3,35},{35,3},{4,36},{36... | collective-permute-start | bytes 1572872 | tf_op jit(solution)/shard_map/ppermute | solution.py:23
  125.8 1.0 copy-start.6

commit v13 on v12

--- a/solution.py
+++ b/solution.py
@@ -28,16 +28,24 @@
     i = lax.axis_index(axis)
     blocks = x.reshape((n, x.shape[0] // n) + x.shape[1:])
     own = lambda k: lax.dynamic_index_in_dim(blocks, k % n, axis=0, keepdims=False)
-    up_steps, down_steps = (n - 1) // 2, n // 2
-    acc_up = own(i + up_steps)
-    for s in range(1, up_steps + 1):
+    steps = (n - 1) // 2
+    acc_up = own(i + steps)
+    for s in range(1, steps + 1):
         got = shift(acc_up, axis, 1)
-        acc_up = got + own(i + up_steps - s) if s < up_steps else got
-    acc_down = own(i - down_steps)
-    for s in range(1, down_steps + 1):
+        acc_up = got + own(i + steps - s) if s < steps else got
+    acc_down = own(i - steps)
+    for s in range(1, steps + 1):
         got = shift(acc_down, axis, -1)
-        acc_down = got + own(i - down_steps + s) if s < down_steps else got
-    return acc_up + acc_down + own(i)
+        acc_down = got + own(i - steps + s) if s < steps else got
+    total = acc_up + acc_down + own(i)
+    if n % 2 == 0:
+        far = own(i + n // 2)
+        cut = far.shape[-1] // 2
+        near = jnp.concatenate(
+            [shift(far[..., :cut], axis, n // 2), shift(far[..., cut:], axis, -(n // 2))], axis=-1
+        )
+        total = total + near
+    return total
 
 
 def scatter_sum_pair(x, axis):

time: 160 us -> 170 us (1.062)
  waiting for transfers between devices: 34.3 us -> 41.2 us
  blocking collectives: 66.3 us -> 69.4 us
    ppermute x9 -> x10, waiting for transfers between devices: 22.6 us -> 29.6 us  [shift(): return lax.ppermute(x, axis, [(s, (s + step) % n) for s in range(n)])]
    all_to_all x2, blocking collectives: 37.6 us -> 40.7 us  [gather_a2a(): return lax.all_to_all(copies, axis, 0, 0, tiled=True)]
    ppermute x9 -> x10, starting transfers between devices: 40 us -> 38.5 us  [shift(): return lax.ppermute(x, axis, [(s, (s + step) % n) for s in range(n)])]
  transfers between devices with their start and end apart: 10 -> 11, of which waited for: 9 -> 9; matrix products, arithmetic and copies ran while one was open for 0% -> 0% of each run, Pallas kernels for 0% -> 0%
where the time goes in v13:
time: 170 us; the launch traced here: 167 us
  blocking collectives  69.4 us (41%)
  starting transfers between devices  42.5 us (25%)
  waiting for transfers between devices  41.2 us (24%)
  local copies, waits for them, and re-layouts  5.9 us (3%)
  other arithmetic  5.73 us (3%)
  matrix products  1.97 us (1%)
    all_to_all x2, blocking collectives, gather_a2a(): return lax.all_to_all(copies, axis, 0, 0, tiled=True)  40.7 us
    ppermute x10, starting transfers between devices, shift(): return lax.ppermute(x, axis, [(s, (s + step) % n) for s in range(n)])  38.5 us
    ppermute x10, waiting for transfers between devices, shift(): return lax.ppermute(x, axis, [(s, (s + step) % n) for s in range(n)])  29.6 us
    all_to_all x1, blocking collectives, scatter_sum_a2a(): got = lax.all_to_all(x.astype(sent), axis, 0, 0, tiled=True)  28.7 us
    all_to_all x1, waiting for transfers between devices, gather_a2a(): return lax.all_to_all(copies, axis, 0, 0, tiled=True)  11.7 us
    all_to_all x1, starting transfers between devices, gather_a2a(): return lax.all_to_all(copies, axis, 0, 0, tiled=True)  4.01 us
  transfers between devices with their start and end apart: 11, of which 9 were waited for; matrix products, arithmetic and copies ran while one was open for 0% of the time, Pallas kernels for 0%

profile of v13, /device:TPU:1, one launch (start us, length us, event | category | flops | bytes accessed | tf_op | source)
XLA Modules:
  0.0 167.2 jit_solution(5108036677795618734)
XLA Ops:
  0.0 0.8 broadcast_in_dim.24
  0.8 21.1 %all_to_all.30 = bf16[8,32,512]{2,1,0:T(8,128)(2,1)S(1)} all-to-all(bf16[8,32,512]{2,1,0:T(8,128)(2,1)S(1)} %broadcast_in_dim.24), channel_id=1, replica_groups=mesh['y'=8,'c'=2,'z'=8,'x'=4] {'z'}, dimensions={0} | all-to-all | bytes 524288 | tf_op jit(solution)/shard_map/all_to_all | solution.py:77
  22.0 1.1 broadcast_in_dim.26
  23.0 4.0 %all-to-all-start.1 = ((bf16[4,256,512]{2,1,0:T(8,128)(2,1)}), bf16[4,256,512]{2,1,0:T(8,128)(2,1)S(1)}, u32[]{:S(2)}, u32[]{:S(2)}) async-start(bf16[4,256,512]{2,1,0:T(8,128)(2,1)} %broadcast_in_dim.26), calls=%async_computation.1 | async-start | bytes 2097152 | tf_op jit(solution)/shard_map/all_to_all | solution.py:77
  27.1 0.2 broadcast_in_dim.23
  27.3 0.2 broadcast_in_dim.22
  27.5 0.2 bitcast_multiply_fusion.2
  27.7 11.7 %all-to-all-done.1 = bf16[4,256,512]{2,1,0:T(8,128)(2,1)S(1)} async-done(((bf16[4,256,512]{2,1,0:T(8,128)(2,1)}), bf16[4,256,512]{2,1,0:T(8,128)(2,1)S(1)}, u32[]{:S(2)}, u32[]{:S(2)}) %all-to-all-start.1) | async-done | bytes 1048608 | tf_op jit(solution)/shard_map/all_to_all | solution.py:77
  39.3 0.1 copy.8
  39.4 1.2 fusion
  40.7 0.2 dynamic-slice_bitcast_fusion
  40.9 1.7 %copy-done = f32[1024,1024]{0,1:T(8,128)} copy-done((f32[1024,1024]{0,1:T(8,128)}, f32[1024,1024]{0,1:T(8,128)S(1)}, u32[]{:S(2)}) %copy-start) | copy-done | bytes 4194328
  42.6 5.7 %collective-permute-start = (f32[512,1024]{1,0:T(8,128)S(1)}, f32[512,1024]{1,0:T(8,128)}, u32[]{:S(2)}, u32[]{:S(2)}) collective-permute-start(f32[512,1024]{1,0:T(8,128)S(1)} %dynamic-slice_bitcast_fusion), channel_id=1, source_target_pairs={{0,32},{32,0},{1,33},{33,1},{2,34},{34,2},{3,35},{35,3},{4,36},{36... | collective-permute-start | bytes 6291464 | tf_op jit(solution)/shard_map/ppermute | solution.py:23
  48.3 3.8 %collective-permute-done = f32[512,1024]{1,0:T(8,128)} collective-permute-done((f32[512,1024]{1,0:T(8,128)S(1)}, f32[512,1024]{1,0:T(8,128)}, u32[]{:S(2)}, u32[]{:S(2)}) %collective-permute-start) | collective-permute-done | bytes 2097184 | tf_op jit(solution)/shard_map/ppermute | solution.py:23
  52.2 2.6 %bitcast_add_fusion = f32[512,1024]{1,0:T(8,128)S(1)} fusion(f32[512,1024]{1,0:T(8,128)} %collective-permute-done, f32[2,512,1024]{2,1,0:T(8,128)} %bitcast.57, s32[]{:T(128)S(6)} %select_n.107), kind=kLoop, calls=%fused_computation.1 | loop fusion | flops 524288 | bytes 6291460 | tf_op jit(solution)/shard_map/add | solution.py:56
  54.8 0.1 dynamic-slice_bitcast_fusion.2
  54.9 5.1 %collective-permute-start.4 = (f32[64,1024]{1,0:T(8,128)S(1)}, f32[64,1024]{1,0:T(8,128)S(1)}, u32[]{:S(2)}, u32[]{:S(2)}) collective-permute-start(f32[64,1024]{1,0:T(8,128)S(1)} %get-tuple-element.9), channel_id=1, source_target_pairs={{0,448},{64,0},{128,64},{192,128},{256,192},{320,256},{384,320},{4... | collective-permute-start | bytes 786440 | tf_op jit(solution)/shard_map/ppermute | solution.py:23
  60.0 1.9 %collective-permute-start.1 = (f32[64,1024]{1,0:T(8,128)S(1)}, f32[64,1024]{1,0:T(8,128)}, u32[]{:S(2)}, u32[]{:S(2)}) collective-permute-start(f32[64,1024]{1,0:T(8,128)S(1)} %get-tuple-element.11), channel_id=1, source_target_pairs={{0,64},{64,128},{128,192},{192,256},{256,320},{320,384},{384,448},... | collective-permute-start | bytes 786440 | tf_op jit(solution)/shard_map/ppermute | solution.py:23
  61.9 3.3 %collective-permute-done.4 = f32[64,1024]{1,0:T(8,128)S(1)} collective-permute-done((f32[64,1024]{1,0:T(8,128)S(1)}, f32[64,1024]{1,0:T(8,128)S(1)}, u32[]{:S(2)}, u32[]{:S(2)}) %collective-permute-start.4) | collective-permute-done | bytes 262176 | tf_op jit(solution)/shard_map/ppermute | solution.py:23
  65.2 5.1 %collective-permute-done.1 = f32[64,1024]{1,0:T(8,128)} collective-permute-done((f32[64,1024]{1,0:T(8,128)S(1)}, f32[64,1024]{1,0:T(8,128)}, u32[]{:S(2)}, u32[]{:S(2)}) %collective-permute-start.1) | collective-permute-done | bytes 262176 | tf_op jit(solution)/shard_map/ppermute | solution.py:23
  70.4 1.0 bitcast_add_fusion.3
  71.4 1.9 %collective-permute-start.5 = (f32[64,1024]{1,0:T(8,128)S(1)}, f32[64,1024]{1,0:T(8,128)S(1)}, u32[]{:S(2)}, u32[]{:S(2)}) collective-permute-start(f32[64,1024]{1,0:T(8,128)S(1)} %get-tuple-element.7), channel_id=1, source_target_pairs={{0,448},{64,0},{128,64},{192,128},{256,192},{320,256},{384,320},{4... | collective-permute-start | bytes 786440 | tf_op jit(solution)/shard_map/ppermute | solution.py:23
  73.3 3.4 %collective-permute-start.2 = (f32[64,1024]{1,0:T(8,128)S(1)}, f32[64,1024]{1,0:T(8,128)S(1)}, u32[]{:S(2)}, u32[]{:S(2)}) collective-permute-start(f32[64,1024]{1,0:T(8,128)S(1)} %get-tuple-element.8), channel_id=1, source_target_pairs={{0,64},{64,128},{128,192},{192,256},{256,320},{320,384},{384,448},... | collective-permute-start | bytes 786440 | tf_op jit(solution)/shard_map/ppermute | solution.py:23
  76.7 2.9 %collective-permute-done.5 = f32[64,1024]{1,0:T(8,128)S(1)} collective-permute-done((f32[64,1024]{1,0:T(8,128)S(1)}, f32[64,1024]{1,0:T(8,128)S(1)}, u32[]{:S(2)}, u32[]{:S(2)}) %collective-permute-start.5) | collective-permute-done | bytes 262176 | tf_op jit(solution)/shard_map/ppermute | solution.py:23
  79.7 3.0 %collective-permute-done.2 = f32[64,1024]{1,0:T(8,128)S(1)} collective-permute-done((f32[64,1024]{1,0:T(8,128)S(1)}, f32[64,1024]{1,0:T(8,128)S(1)}, u32[]{:S(2)}, u32[]{:S(2)}) %collective-permute-start.2) | collective-permute-done | bytes 262176 | tf_op jit(solution)/shard_map/ppermute | solution.py:23
  82.7 0.8 bitcast_add_fusion.2
  83.4 2.1 %collective-permute-start.3 = (f32[64,1024]{1,0:T(8,128)}, f32[64,1024]{1,0:T(8,128)S(1)}, u32[]{:S(2)}, u32[]{:S(2)}) collective-permute-start(f32[64,1024]{1,0:T(8,128)} %get-tuple-element.6), channel_id=1, source_target_pairs={{0,64},{64,128},{128,192},{192,256},{256,320},{320,384},{384,448},... | collective-permute-start | bytes 786440 | tf_op jit(solution)/shard_map/ppermute | solution.py:23
  85.6 4.5 %collective-permute-start.6 = (f32[64,1024]{1,0:T(8,128)S(1)}, f32[64,1024]{1,0:T(8,128)S(1)}, u32[]{:S(2)}, u32[]{:S(2)}) collective-permute-start(f32[64,1024]{1,0:T(8,128)S(1)} %get-tuple-element.5), channel_id=1, source_target_pairs={{0,448},{64,0},{128,64},{192,128},{256,192},{320,256},{384,320},{4... | collective-permute-start | bytes 786440 | tf_op jit(solution)/shard_map/ppermute | solution.py:23
  90.1 4.6 %collective-permute-start.8 = (f32[64,512]{1,0:T(8,128)S(1)}, f32[64,512]{1,0:T(8,128)S(1)}, u32[]{:S(2)}, u32[]{:S(2)}) collective-permute-start(f32[64,512]{1,0:T(8,128)S(1)} %get-tuple-element.13), channel_id=1, source_target_pairs={{0,256},{64,320},{128,384},{192,448},{256,0},{320,64},{384,128},{4... | collective-permute-start | bytes 393224 | tf_op jit(solution)/shard_map/ppermute | solution.py:23
  94.7 4.6 %collective-permute-start.7 = (f32[64,512]{1,0:T(8,128)S(1)}, f32[64,512]{1,0:T(8,128)S(1)}, u32[]{:S(2)}, u32[]{:S(2)}) collective-permute-start(f32[64,512]{1,0:T(8,128)S(1)} %get-tuple-element.12), channel_id=1, source_target_pairs={{0,256},{64,320},{128,384},{192,448},{256,0},{320,64},{384,128},{4... | collective-permute-start | bytes 393224 | tf_op jit(solution)/shard_map/ppermute | solution.py:23
  99.3 0.9 collective-permute-done.8
  100.2 9.1 %collective-permute-done.7 = f32[64,512]{1,0:T(8,128)S(1)} collective-permute-done((f32[64,512]{1,0:T(8,128)S(1)}, f32[64,512]{1,0:T(8,128)S(1)}, u32[]{:S(2)}, u32[]{:S(2)}) %collective-permute-start.7) | collective-permute-done | bytes 131104 | tf_op jit(solution)/shard_map/ppermute | solution.py:23
  109.2 0.0 collective-permute-done.3
  109.2 0.0 collective-permute-done.6
  109.2 0.1 maximum_add_fusion
  109.4 19.6 %all_to_all.31 = bf16[8,64,512]{2,1,0:T(8,128)(2,1)S(1)} all-to-all(bf16[8,64,512]{2,1,0:T(8,128)(2,1)S(1)} %broadcast_in_dim.54), channel_id=1, replica_groups=mesh['y'=8,'c'=2,'z'=8,'x'=4] {'y'}, dimensions={0} | all-to-all | bytes 1048576 | tf_op jit(solution)/shard_map/all_to_all | solution.py:77
  128.9 4.8 %collective-permute-start.9 = (bf16[512,512]{1,0:T(8,128)(2,1)S(1)}, bf16[512,512]{1,0:T(8,128)(2,1)S(1)}, u32[]{:S(2)}, u32[]{:S(2)}) collective-permute-start(bf16[512,512]{1,0:T(8,128)(2,1)S(1)} %bitcast.65), channel_id=1, source_target_pairs={{0,32},{32,0},{1,33},{33,1},{2,34},{34,2},{3,35},{35,3},{4,36},{36... | collective-permute-start | bytes 1572872 | tf_op jit(solution)/shard_map/ppermute | solution.py:23
  133.8 1.4 collective-permute-done.9
  135.2 0.1 pad_maximum_fusion
  135.3 0.6 gather_fusion
  135.9 0.0 copy-start.6
  136.0 0.2 select_bitcast_fusion
  136.1 0.1 copy.9
  136.2 0.2 broadcast_in_dim.56
  136.4 0.6 copy-done.6
  137.0 0.7 convolution_convert_fusion
  137.7 28.7 %all_to_all.32 = bf16[32,32,512]{2,1,0:T(8,128)(2,1)S(1)} all-to-all(bf16[32,32,512]{2,1,0:T(8,128)(2,1)S(1)} %bitcast.71), channel_id=1, replica_groups=mesh['y'=8,'c'=2,'z'=8,'x'=4] {'x','z'}, dimensions={0} | all-to-all | bytes 2097152 | tf_op jit(solution)/shard_map/all_to_all | solution.py:82
  166.4 0.8 reduce_sum.12
  (20 shorter events, 0.2 us)
Async XLA Ops:
  0.0 27.0 %copy-start.3 = (s32[4,4]{1,0:T(4,128)S(1)}, s32[4,4]{1,0:T(4,128)}, u32[]{:S(2)}) copy-start(s32[4,4]{1,0:T(4,128)} %param.12) | copy-start | bytes 196
  0.0 27.1 %copy-start.4 = (s32[4,4]{1,0:T(4,128)S(1)}, s32[4,4]{1,0:T(4,128)}, u32[]{:S(2)}) copy-start(s32[4,4]{1,0:T(4,128)} %param.11) | copy-start | bytes 196
  22.0 5.5 %copy-start.1 = (bf16[512,512]{1,0:T(8,128)(2,1)S(1)}, bf16[512,512]{1,0:T(8,128)(2,1)}, u32[]{:S(2)}) copy-start(bf16[512,512]{1,0:T(8,128)(2,1)} %param.9) | copy-start | bytes 1572868
  22.0 5.6 %copy-start.2 = (bf16[512,512]{1,0:T(8,128)(2,1)S(1)}, bf16[512,512]{1,0:T(8,128)(2,1)}, u32[]{:S(2)}) copy-start(bf16[512,512]{1,0:T(8,128)(2,1)} %param.8) | copy-start | bytes 1572868
  23.0 16.3 %all-to-all-start.1 = ((bf16[4,256,512]{2,1,0:T(8,128)(2,1)}), bf16[4,256,512]{2,1,0:T(8,128)(2,1)S(1)}, u32[]{:S(2)}, u32[]{:S(2)}) async-start(bf16[4,256,512]{2,1,0:T(8,128)(2,1)} %broadcast_in_dim.26), calls=%async_computation.1 | async-start | bytes 2097152 | tf_op jit(solution)/shard_map/all_to_all | solution.py:77
  40.7 1.9 %copy-start = (f32[1024,1024]{0,1:T(8,128)}, f32[1024,1024]{0,1:T(8,128)S(1)}, u32[]{:S(2)}) copy-start(f32[1024,1024]{0,1:T(8,128)S(1)} %fusion) | copy-start | bytes 12582916
  42.6 9.6 %collective-permute-start = (f32[512,1024]{1,0:T(8,128)S(1)}, f32[512,1024]{1,0:T(8,128)}, u32[]{:S(2)}, u32[]{:S(2)}) collective-permute-start(f32[512,1024]{1,0:T(8,128)S(1)} %dynamic-slice_bitcast_fusion), channel_id=1, source_target_pairs={{0,32},{32,0},{1,33},{33,1},{2,34},{34,2},{3,35},{35,3},{4,36},{36... | collective-permute-start | bytes 6291464 | tf_op jit(solution)/shard_map/ppermute | solution.py:23
  54.9 10.4 %collective-permute-start.4 = (f32[64,1024]{1,0:T(8,128)S(1)}, f32[64,1024]{1,0:T(8,128)S(1)}, u32[]{:S(2)}, u32[]{:S(2)}) collective-permute-start(f32[64,1024]{1,0:T(8,128)S(1)} %get-tuple-element.9), channel_id=1, source_target_pairs={{0,448},{64,0},{128,64},{192,128},{256,192},{320,256},{384,320},{4... | collective-permute-start | bytes 786440 | tf_op jit(solution)/shard_map/ppermute | solution.py:23
  60.0 10.4 %collective-permute-start.1 = (f32[64,1024]{1,0:T(8,128)S(1)}, f32[64,1024]{1,0:T(8,128)}, u32[]{:S(2)}, u32[]{:S(2)}) collective-permute-start(f32[64,1024]{1,0:T(8,128)S(1)} %get-tuple-element.11), channel_id=1, source_target_pairs={{0,64},{64,128},{128,192},{192,256},{256,320},{320,384},{384,448},... | collective-permute-start | bytes 786440 | tf_op jit(solution)/shard_map/ppermute | solution.py:23
  71.4 8.2 %collective-permute-start.5 = (f32[64,1024]{1,0:T(8,128)S(1)}, f32[64,1024]{1,0:T(8,128)S(1)}, u32[]{:S(2)}, u32[]{:S(2)}) collective-permute-start(f32[64,1024]{1,0:T(8,128)S(1)} %get-tuple-element.7), channel_id=1, source_target_pairs={{0,448},{64,0},{128,64},{192,128},{256,192},{320,256},{384,320},{4... | collective-permute-start | bytes 786440 | tf_op jit(solution)/shard_map/ppermute | solution.py:23
  73.3 9.3 %collective-permute-start.2 = (f32[64,1024]{1,0:T(8,128)S(1)}, f32[64,1024]{1,0:T(8,128)S(1)}, u32[]{:S(2)}, u32[]{:S(2)}) collective-permute-start(f32[64,1024]{1,0:T(8,128)S(1)} %get-tuple-element.8), channel_id=1, source_target_pairs={{0,64},{64,128},{128,192},{192,256},{256,320},{320,384},{384,448},... | collective-permute-start | bytes 786440 | tf_op jit(solution)/shard_map/ppermute | solution.py:23
  83.4 50.3 %copy-start.5 = (s32[4,4]{1,0:T(4,128)S(1)}, s32[4,4]{1,0:T(4,128)}, u32[]{:S(2)}) copy-start(s32[4,4]{1,0:T(4,128)} %param.13) | copy-start | bytes 196
  83.4 25.8 %collective-permute-start.3 = (f32[64,1024]{1,0:T(8,128)}, f32[64,1024]{1,0:T(8,128)S(1)}, u32[]{:S(2)}, u32[]{:S(2)}) collective-permute-start(f32[64,1024]{1,0:T(8,128)} %get-tuple-element.6), channel_id=1, source_target_pairs={{0,64},{64,128},{128,192},{192,256},{256,320},{320,384},{384,448},... | collective-permute-start | bytes 786440 | tf_op jit(solution)/shard_map/ppermute | solution.py:23
  85.6 23.7 %collective-permute-start.6 = (f32[64,1024]{1,0:T(8,128)S(1)}, f32[64,1024]{1,0:T(8,128)S(1)}, u32[]{:S(2)}, u32[]{:S(2)}) collective-permute-start(f32[64,1024]{1,0:T(8,128)S(1)} %get-tuple-element.5), channel_id=1, source_target_pairs={{0,448},{64,0},{128,64},{192,128},{256,192},{320,256},{384,320},{4... | collective-permute-start | bytes 786440 | tf_op jit(solution)/shard_map/ppermute | solution.py:23
  90.1 10.1 %collective-permute-start.8 = (f32[64,512]{1,0:T(8,128)S(1)}, f32[64,512]{1,0:T(8,128)S(1)}, u32[]{:S(2)}, u32[]{:S(2)}) collective-permute-start(f32[64,512]{1,0:T(8,128)S(1)} %get-tuple-element.13), channel_id=1, source_target_pairs={{0,256},{64,320},{128,384},{192,448},{256,0},{320,64},{384,128},{4... | collective-permute-start | bytes 393224 | tf_op jit(solution)/shard_map/ppermute | solution.py:23
  94.7 14.6 %collective-permute-start.7 = (f32[64,512]{1,0:T(8,128)S(1)}, f32[64,512]{1,0:T(8,128)S(1)}, u32[]{:S(2)}, u32[]{:S(2)}) collective-permute-start(f32[64,512]{1,0:T(8,128)S(1)} %get-tuple-element.12), channel_id=1, source_target_pairs={{0,256},{64,320},{128,384},{192,448},{256,0},{320,64},{384,128},{4... | collective-permute-start | bytes 393224 | tf_op jit(solution)/shard_map/ppermute | solution.py:23
  128.9 6.3 %collective-permute-start.9 = (bf16[512,512]{1,0:T(8,128)(2,1)S(1)}, bf16[512,512]{1,0:T(8,128)(2,1)S(1)}, u32[]{:S(2)}, u32[]{:S(2)}) collective-permute-start(bf16[512,512]{1,0:T(8,128)(2,1)S(1)} %bitcast.65), channel_id=1, source_target_pairs={{0,32},{32,0},{1,33},{33,1},{2,34},{34,2},{3,35},{35,3},{4,36},{36... | collective-permute-start | bytes 1572872 | tf_op jit(solution)/shard_map/ppermute | solution.py:23
  135.9 1.0 copy-start.6
